TPU v7x, 256 devices: a whole 4x4x8 slice. The times are simulated.
256 devices in a mesh: ctx: 64 (over y, z_lo, x), tp: 4 (over z_hi, core).
Axes of the slice: x: 4, y: 4, z: 8 (z_hi: 2, z_lo: 4; z = z_hi * 4 + z_lo), core: 2. Of those that a mesh axis runs over, the one named last changes fastest.
Arguments:
- activations: bfloat16 [40960, 4096], P('ctx', 'tp'), may hold values from -6 to 6
- group_counts: int32 [64], replicated, may hold values from 1 to 5, as said below
- genome_starts: int32 [32], replicated, may hold values from 0 to 24448, as said below
- in_weight: bfloat16 [4096, 3, 2048], P('ctx', None, 'tp'), may hold values from -0.09375 to 0.09375
- short_taps: float32 [7, 3, 2048], P(None, None, 'tp'), may hold values from -2 to 2
- long_taps: float32 [128, 2048], P(None, 'tp'), may hold values from -0.5 to 0.5
- out_weight: bfloat16 [2048, 4096], P('tp', 'ctx'), may hold values from -0.125 to 0.125
Outputs:
- block_out: bfloat16 [40960, 4096], P('ctx', 'tp')
Inputs may be any that keep to these rules, and one draw needn't show every extreme that they name: Every device holds 1 or more blocks; group_counts[2k] + group_counts[2k+1] = 6 for every k. `genome_starts`: strictly increasing; the first entry is 0 and the last is exactly 24448.
All inputs are finite; a program needn't handle non-finite values.
Results may differ from a plain program's by a relative error of at most 0.012.
Values may be sent and summed in bfloat16 or wider, within the bound.
No kernel may reach another device: no remote copies, remote signals or barrier semaphores. Data moves between devices by JAX's collectives and lax.ppermute only.
A program may use at most 128 MiB of HBM per device.

v0:
```python
import jax
import jax.numpy as jnp
from jax import lax
from jax.sharding import PartitionSpec as P

GROUP = 128


def passed_along(shard, axis, by):
    peers = lax.axis_size(axis)
    pairs = [(i, i + by) for i in range(peers) if 0 <= i + by < peers]
    return lax.ppermute(shard, axis, pairs)


def genome_start(positions, genome_starts):
    above = genome_starts[None, :] <= positions[:, None]
    return jnp.max(jnp.where(above, genome_starts[None, :], 0), axis=1)


def causal_taps(padded, taps, positions, gstart, width):
    count = positions.shape[0]
    shape = (count,) + (1,) * (padded.ndim - 1)
    summed = jnp.zeros((count,) + padded.shape[1:], jnp.float32)
    for j in range(width):
        in_genome = (positions - j >= gstart).reshape(shape)
        window = padded[width - 1 - j : width - 1 - j + count]
        summed = summed + jnp.where(in_genome, window * taps[j], jnp.float32(0.0))
    return summed


def body(activations, group_counts, genome_starts, in_weight, short_taps, long_taps, out_weight):
    ctx_size = lax.axis_size("ctx")
    my_index = lax.axis_index("ctx")
    own_rows = activations.shape[0]
    device_ids = jnp.arange(ctx_size, dtype=jnp.int32)
    own_count = jnp.sum(jnp.where(device_ids == my_index, group_counts, 0))
    offset = jnp.sum(jnp.where(device_ids < my_index, group_counts, 0))
    row_ids = jnp.arange(own_rows, dtype=jnp.int32)
    positions = offset * GROUP + row_ids
    tail_end = own_count * GROUP

    def last_rows(source, count):
        return lax.dynamic_slice_in_dim(source, tail_end - count, count, 0)

    gstart = genome_start(positions, genome_starts)
    all_feats = lax.all_gather(activations, "tp", axis=1, tiled=True)
    widened = all_feats.astype(jnp.float32)
    normed = (
        widened * lax.rsqrt(jnp.mean(widened * widened, axis=1, keepdims=True) + 1e-06)
    ).astype(jnp.bfloat16)
    row_count = normed.shape[0]
    branches = in_weight.shape[1]
    chans = in_weight.shape[2]
    shard_rows = lax.all_gather(in_weight, "ctx", axis=0, tiled=True)
    flat = shard_rows.reshape(shard_rows.shape[0], branches * chans)
    summed = jnp.dot(normed, flat, preferred_element_type=jnp.float32)
    projected = summed.astype(jnp.bfloat16).reshape(row_count, branches, chans)
    rim_short = passed_along(last_rows(projected, 6), "ctx", 1)
    feat = causal_taps(
        jnp.concatenate([rim_short, projected], axis=0).astype(jnp.float32),
        short_taps,
        positions,
        gstart,
        7,
    )
    mixed = (feat[:, 1] * feat[:, 2]).astype(jnp.bfloat16)
    rim_long = passed_along(last_rows(mixed, 127), "ctx", 1)
    filtered = causal_taps(
        jnp.concatenate([rim_long, mixed], axis=0).astype(jnp.float32),
        long_taps,
        positions,
        gstart,
        128,
    )
    gated = (feat[:, 0] * filtered).astype(jnp.bfloat16)
    partial_out = jnp.dot(
        gated,
        lax.all_gather(out_weight, "ctx", axis=1, tiled=True),
        preferred_element_type=jnp.float32,
    )
    branch_out = lax.psum_scatter(
        partial_out.astype(jnp.bfloat16), "tp", scatter_dimension=1, tiled=True
    ).astype(jnp.float32)
    result = (activations.astype(jnp.float32) + branch_out).astype(jnp.bfloat16)
    slot_ids = jnp.arange(own_rows, dtype=jnp.int32)
    live_rows = (slot_ids < own_count * GROUP)[:, None]
    return jnp.where(live_rows, result, jnp.zeros_like(result))


def solution(mesh):
    placed = (
        P("ctx", "tp"),
        P(),
        P(),
        P("ctx", None, "tp"),
        P(None, None, "tp"),
        P(None, "tp"),
        P("tp", "ctx"),
    )
    return jax.shard_map(
        body, mesh=mesh, in_specs=placed, out_specs=P("ctx", "tp"), check_vma=False
    )
```

profile of v0, /device:TPU:9, one launch (start us, length us, event | category | flops | bytes accessed | tf_op | source)
XLA Modules:
  0.0 920.5 jit_solution(7368510152280378375)
XLA Ops:
  6.6 0.7 all-gather.4.cloned.1.call-update
  7.3 0.7 all-gather.6.cloned.1.call-update
  8.1 0.7 all-gather.8.cloned.1.call-update
  9.1 0.6 fusion.283
  11.2 1.3 add_compare_fusion.95
  12.5 78.2 %all-gather.4.cloned.1.call-done = bf16[640,4096]{1,0:T(8,128)(2,1)} async-done(((bf16[640,1024]{1,0:T(8,128)(2,1)}), bf16[640,4096]{1,0:T(8,128)(2,1)}) %all-gather.4.cloned.1.call-update) | async-done | bytes 5242896 | tf_op jit(solution)/shard_map/all_gather | solution.py:46
  90.7 3.6 fusion
  94.3 289.1 %all-gather.6.cloned.1.call-done = bf16[4096,3,512]{2,0,1:T(8,128)(2,1)} async-done(((bf16[64,3,512]{2,0,1:T(8,128)(2,1)}), bf16[4096,3,512]{2,0,1:T(8,128)(2,1)}) %all-gather.6.cloned.1.call-update) | async-done | bytes 12582928 | tf_op jit(solution)/shard_map/all_gather | solution.py:54
  383.4 17.0 %copy.21 = bf16[4096,3,512]{0,2,1:T(8,128)(2,1)} copy(bf16[4096,3,512]{2,0,1:T(8,128)(2,1)} %all-gather.6.cloned.1.call-done) | data formatting | bytes 25165824 | tf_op jit(solution)/shard_map/all_gather | solution.py:54
  400.3 13.9 %fusion.18 = bf16[640,1536]{1,0:T(8,128)(2,1)} fusion(bf16[4096,1536]{0,1:T(8,128)(2,1)} %bitcast.161, bf16[640,4096]{1,0:T(8,128)(2,1)} %all-gather.4.cloned.1.call-done, f32[640]{0:T(1024)S(1)} %add_rsqrt_fusion), kind=kOutput, calls=%fused_computation.27 | convolution fusion | flops 8061911040 | bytes 19794432 | tf_op jit(solution)/shard_map/dot_general | solution.py:56
  414.2 2.8 copy.22
  417.2 1.9 collective-permute-start
  419.2 11.4 %collective-permute-done = bf16[6,3,512]{0,2,1:T(8,128)(2,1)S(1)} collective-permute-done((bf16[6,3,512]{0,2,1:T(8,128)(2,1)S(1)}, bf16[6,3,512]{0,2,1:T(8,128)(2,1)S(1)}, u32[]{:S(2)}, u32[]{:S(2)}) %collective-permute-start) | collective-permute-done | bytes 18464 | tf_op jit(solution)/shard_map/ppermute | solution.py:12
  430.5 1.0 maximum_convert_fusion
  431.6 8.1 fusion.6
  439.9 2.1 collective-permute-start.1
  442.1 8.3 collective-permute-done.1
  450.4 0.4 maximum_convert_fusion.1
  451.2 15.7 %fusion.217 = f32[640,512]{0,1:T(8,128)S(1)} fusion(f32[767,512]{0,1:T(8,128)S(1)} %maximum_convert_fusion.1, f32[512]{0:T(512)S(1)} %bitcast.178, f32[512]{0:T(512)S(1)} %bitcast.179, f32[512]{0:T(512)S(1)} %bitcast.180, f32[512]{0:T(512)S(1)} %bitcast.181, f32[512]{0:T(512)S(1)} %bitcast.182, f32[512]{0:T(512)S(1)} %bitcast.183, f32[512]{0:T(512)S(1)} %bitcast.184, ...), kind=kLoop, calls=%fused_computation.323 | loop fusion | flops 31129600 | bytes 43339776 | tf_op jit(solution)/shard_map/add | solution.py:27
  467.3 47.7 %fusion.299 = bf16[640,512]{0,1:T(8,128)(2,1)S(1)} fusion(f32[767,512]{0,1:T(8,128)S(1)} %maximum_convert_fusion.1, f32[640,512]{0,1:T(8,128)S(1)} %fusion.217, f32[512]{0:T(512)S(1)} %bitcast.197, f32[512]{0:T(512)S(1)} %bitcast.292, f32[512]{0:T(512)S(1)} %bitcast.237, f32[512]{0:T(512)S(1)} %bitcast.238, f32[512]{0:T(512)S(1)} %bitcast.239, ...), kind=kLoop, calls=%fused_computation.35.clone.clone.1 | loop fusion | flops 95027200 | bytes 129363968 | tf_op jit(solution)/shard_map/dot_general | solution.py:76
  515.1 216.1 %all-gather.8.cloned.1.call-done = bf16[512,4096]{0,1:T(8,128)(2,1)} async-done(((bf16[512,64]{0,1:T(8,128)(2,1)}), bf16[512,4096]{0,1:T(8,128)(2,1)}) %all-gather.8.cloned.1.call-update) | async-done | bytes 4194320 | tf_op jit(solution)/shard_map/all_gather | solution.py:78
  731.1 7.5 convolution_convert_fusion
  738.6 172.5 %reduce-scatter.2.cloned.1.call-done = bf16[640,1024]{1,0:T(8,128)(2,1)} async-done(((bf16[640,4096]{1,0:T(8,128)(2,1)}), bf16[640,1024]{1,0:T(8,128)(2,1)}) %reduce-scatter.2.cloned.1.call-update) | async-done | bytes 1310736 | tf_op jit(solution)/shard_map/reduce_scatter | solution.py:81
  911.2 2.8 fusion.21
  (115 shorter events, 1.3 us)
Async XLA Ops:
  6.5 84.2 %all-gather.4.cloned.1.call-start = ((), (), s32[]{:S(2)}) async-start(), calls=%async_computation.1 | async-start | bytes 6553600 | tf_op jit(solution)/shard_map/all_gather | solution.py:46
  7.3 376.1 %all-gather.6.cloned.1.call-start = ((), (), s32[]{:S(2)}) async-start(), calls=%async_computation.2 | async-start | bytes 12779520 | tf_op jit(solution)/shard_map/all_gather | solution.py:54
  8.0 723.1 %all-gather.8.cloned.1.call-start = ((), (), s32[]{:S(2)}) async-start(), calls=%async_computation.3 | async-start | bytes 4259840 | tf_op jit(solution)/shard_map/all_gather | solution.py:78
  8.8 902.4 %reduce-scatter.2.cloned.1.call-start = ((), (), s32[]{:S(2)}) async-start(), calls=%async_computation.4 | async-start | bytes 6553600 | tf_op jit(solution)/shard_map/reduce_scatter | solution.py:81
  417.2 13.3 %collective-permute-start = (bf16[6,3,512]{0,2,1:T(8,128)(2,1)S(1)}, bf16[6,3,512]{0,2,1:T(8,128)(2,1)S(1)}, u32[]{:S(2)}, u32[]{:S(2)}) collective-permute-start(bf16[6,3,512]{0,2,1:T(8,128)(2,1)S(1)} %constant_dynamic-slice_fusion), channel_id=1, source_target_pairs={{0,4},{4,8},{8,12},{12,16},{16,20},{20,24},{24,28},{28,32},{32,36}... | collective-permute-start | bytes 55304 | tf_op jit(solution)/shard_map/ppermute | solution.py:12
  439.9 10.5 %collective-permute-start.1 = (bf16[127,512]{0,1:T(8,128)(2,1)S(1)}, bf16[127,512]{0,1:T(8,128)(2,1)S(1)}, u32[]{:S(2)}, u32[]{:S(2)}) collective-permute-start(bf16[127,512]{0,1:T(8,128)(2,1)S(1)} %dynamic-slice_bitcast_fusion), channel_id=1, source_target_pairs={{0,4},{4,8},{8,12},{12,16},{16,20},{20,24},{24,28},{28,32},{32,36}... | collective-permute-start | bytes 390152 | tf_op jit(solution)/shard_map/ppermute | solution.py:12
  450.8 16.1 %copy-start.3 = (pred[640]{0:T(1024)(128)(4,1)S(1)}, pred[640]{0:T(1024)(128)(4,1)}, u32[]{:S(2)}) copy-start(pred[640]{0:T(1024)(128)(4,1)} %get-tuple-element.160) | copy-start | bytes 1924
  450.8 16.1 %copy-start.4 = (pred[640]{0:T(1024)(128)(4,1)S(1)}, pred[640]{0:T(1024)(128)(4,1)}, u32[]{:S(2)}) copy-start(pred[640]{0:T(1024)(128)(4,1)} %get-tuple-element.161) | copy-start | bytes 1924
  450.8 16.1 %copy-start.5 = (pred[640]{0:T(1024)(128)(4,1)S(1)}, pred[640]{0:T(1024)(128)(4,1)}, u32[]{:S(2)}) copy-start(pred[640]{0:T(1024)(128)(4,1)} %get-tuple-element.162) | copy-start | bytes 1924
  450.8 16.1 %copy-start.6 = (pred[640]{0:T(1024)(128)(4,1)S(1)}, pred[640]{0:T(1024)(128)(4,1)}, u32[]{:S(2)}) copy-start(pred[640]{0:T(1024)(128)(4,1)} %get-tuple-element.163) | copy-start | bytes 1924
  450.8 16.1 %copy-start.7 = (pred[640]{0:T(1024)(128)(4,1)S(1)}, pred[640]{0:T(1024)(128)(4,1)}, u32[]{:S(2)}) copy-start(pred[640]{0:T(1024)(128)(4,1)} %get-tuple-element.164) | copy-start | bytes 1924
  450.8 16.1 %copy-start.8 = (pred[640]{0:T(1024)(128)(4,1)S(1)}, pred[640]{0:T(1024)(128)(4,1)}, u32[]{:S(2)}) copy-start(pred[640]{0:T(1024)(128)(4,1)} %get-tuple-element.165) | copy-start | bytes 1924
  450.8 16.1 %copy-start.9 = (pred[640]{0:T(1024)(128)(4,1)S(1)}, pred[640]{0:T(1024)(128)(4,1)}, u32[]{:S(2)}) copy-start(pred[640]{0:T(1024)(128)(4,1)} %get-tuple-element.166) | copy-start | bytes 1924
  450.9 16.1 %copy-start.10 = (pred[640]{0:T(1024)(128)(4,1)S(1)}, pred[640]{0:T(1024)(128)(4,1)}, u32[]{:S(2)}) copy-start(pred[640]{0:T(1024)(128)(4,1)} %get-tuple-element.167) | copy-start | bytes 1924
  450.9 16.1 %copy-start.11 = (pred[640]{0:T(1024)(128)(4,1)S(1)}, pred[640]{0:T(1024)(128)(4,1)}, u32[]{:S(2)}) copy-start(pred[640]{0:T(1024)(128)(4,1)} %get-tuple-element.168) | copy-start | bytes 1924
  450.9 16.1 %copy-start.12 = (pred[640]{0:T(1024)(128)(4,1)S(1)}, pred[640]{0:T(1024)(128)(4,1)}, u32[]{:S(2)}) copy-start(pred[640]{0:T(1024)(128)(4,1)} %get-tuple-element.169) | copy-start | bytes 1924
  450.9 16.1 %copy-start.13 = (pred[640]{0:T(1024)(128)(4,1)S(1)}, pred[640]{0:T(1024)(128)(4,1)}, u32[]{:S(2)}) copy-start(pred[640]{0:T(1024)(128)(4,1)} %get-tuple-element.170) | copy-start | bytes 1924
  450.9 16.1 %copy-start.14 = (pred[640]{0:T(1024)(128)(4,1)S(1)}, pred[640]{0:T(1024)(128)(4,1)}, u32[]{:S(2)}) copy-start(pred[640]{0:T(1024)(128)(4,1)} %get-tuple-element.171) | copy-start | bytes 1924
  450.9 16.1 %copy-start.15 = (pred[640]{0:T(1024)(128)(4,1)S(1)}, pred[640]{0:T(1024)(128)(4,1)}, u32[]{:S(2)}) copy-start(pred[640]{0:T(1024)(128)(4,1)} %get-tuple-element.172) | copy-start | bytes 1924
  450.9 16.1 %copy-start.16 = (pred[640]{0:T(1024)(128)(4,1)S(1)}, pred[640]{0:T(1024)(128)(4,1)}, u32[]{:S(2)}) copy-start(pred[640]{0:T(1024)(128)(4,1)} %get-tuple-element.173) | copy-start | bytes 1924
  450.9 16.1 %copy-start.17 = (pred[640]{0:T(1024)(128)(4,1)S(1)}, pred[640]{0:T(1024)(128)(4,1)}, u32[]{:S(2)}) copy-start(pred[640]{0:T(1024)(128)(4,1)} %get-tuple-element.174) | copy-start | bytes 1924
  450.9 16.1 %copy-start.18 = (pred[640]{0:T(1024)(128)(4,1)S(1)}, pred[640]{0:T(1024)(128)(4,1)}, u32[]{:S(2)}) copy-start(pred[640]{0:T(1024)(128)(4,1)} %get-tuple-element.175) | copy-start | bytes 1924
  450.9 16.1 %copy-start.19 = (pred[640]{0:T(1024)(128)(4,1)S(1)}, pred[640]{0:T(1024)(128)(4,1)}, u32[]{:S(2)}) copy-start(pred[640]{0:T(1024)(128)(4,1)} %get-tuple-element.176) | copy-start | bytes 1924
  738.6 172.6 %copy-start = (bf16[640,1024]{1,0:T(8,128)(2,1)S(1)}, bf16[640,1024]{1,0:T(8,128)(2,1)}, u32[]{:S(2)}) copy-start(bf16[640,1024]{1,0:T(8,128)(2,1)} %param.7) | copy-start | bytes 3932164
  (27 other events, 385.2 us)
Sparse Core Ops, SparseCore 0:
  9.2 81.4 all-gather.3
  92.5 290.8 all-gather.5
  385.2 345.9 all-gather.7
  738.7 172.3 reduce-scatter.1
where the time goes:
time: 922 us; the launch traced here: 920 us
  waiting for transfers between devices  778 us (84%)
  other arithmetic  81.6 us (9%)
  matrix products  21.4 us (2%)
  local copies, waits for them, and re-layouts  20.5 us (2%)
  between operations  15.3 us (2%)
    all_gather x1, waiting for transfers between devices, body(): shard_rows = lax.all_gather(in_weight, 'ctx', axis=0, tiled=True)  289 us
    all_gather x1, waiting for transfers between devices, body(): lax.all_gather(out_weight, 'ctx', axis=1, tiled=True)  216 us
    reduce_scatter x1, waiting for transfers between devices, body(): lax.psum_scatter(partial_out.astype(jnp.bfloat16), 'tp', scatter_dimensio...  173 us
    all_gather x1, waiting for transfers between devices, body(): all_feats = lax.all_gather(activations, 'tp', axis=1, tiled=True)  78.2 us
    dot_general x1, other arithmetic, body(): jnp.dot(gated, lax.all_gather(out_weight, 'ctx', axis=1, tiled=True), pre...  47.7 us
    add x2, other arithmetic, causal_taps(): summed = summed + jnp.where(in_genome, window * taps[j], jnp.float32(0.0))  23.8 us
    ppermute x2, waiting for transfers between devices, passed_along(): return lax.ppermute(shard, axis, pairs)  19.6 us
  transfers between devices with their start and end apart: 6, of which 6 were waited for; matrix products, arithmetic and copies ran while one was open for 12% of the time, Pallas kernels for 0%

commit v1 on v0

--- a/solution.py
+++ b/solution.py
@@ -51,8 +51,11 @@
     row_count = normed.shape[0]
     branches = in_weight.shape[1]
     chans = in_weight.shape[2]
-    shard_rows = lax.all_gather(in_weight, "ctx", axis=0, tiled=True)
-    flat = shard_rows.reshape(shard_rows.shape[0], branches * chans)
+    local_in = in_weight.reshape(in_weight.shape[0], branches * chans)
+    both = jnp.concatenate([local_in, out_weight.T], axis=1)
+    both_rows = lax.all_gather(both, "ctx", axis=0, tiled=True)
+    flat = both_rows[:, : branches * chans]
+    out_rows = both_rows[:, branches * chans :]
     summed = jnp.dot(normed, flat, preferred_element_type=jnp.float32)
     projected = summed.astype(jnp.bfloat16).reshape(row_count, branches, chans)
     rim_short = passed_along(last_rows(projected, 6), "ctx", 1)
@@ -73,9 +76,10 @@
         128,
     )
     gated = (feat[:, 0] * filtered).astype(jnp.bfloat16)
-    partial_out = jnp.dot(
+    partial_out = lax.dot_general(
         gated,
-        lax.all_gather(out_weight, "ctx", axis=1, tiled=True),
+        out_rows,
+        (((1,), (1,)), ((), ())),
         preferred_element_type=jnp.float32,
     )
     branch_out = lax.psum_scatter(

time: 922 us -> 682 us (0.74)
  waiting for transfers between devices: 778 us -> 554 us
  local copies, waits for them, and re-layouts: 20.5 us -> 3.66 us
    all_gather x2 -> x1, waiting for transfers between devices: 505 us -> 297 us  [body(): both_rows = lax.all_gather(both, 'ctx', axis=0, tiled=True)]
    all_gather x1 -> x0, local copies, waits for them, and re-layouts: 17 us -> none  [body(): shard_rows = lax.all_gather(in_weight, 'ctx', axis=0, tiled=True)]
    reduce_scatter x1, waiting for transfers between devices: 173 us -> 157 us  [body(): lax.psum_scatter(partial_out.astype(jnp.bfloat16), 'tp', scatter_dimensio...]
  transfers between devices with their start and end apart: 6 -> 5, of which waited for: 6 -> 5; matrix products, arithmetic and copies ran while one was open for 12% -> 1% of each run, Pallas kernels for 0% -> 0%
where the time goes in v1:
time: 682 us; the launch traced here: 680 us
  waiting for transfers between devices  554 us (81%)
  other arithmetic  82.4 us (12%)
  matrix products  21.3 us (3%)
  between operations  15.4 us (2%)
    all_gather x1, waiting for transfers between devices, body(): both_rows = lax.all_gather(both, 'ctx', axis=0, tiled=True)  297 us
    reduce_scatter x1, waiting for transfers between devices, body(): lax.psum_scatter(partial_out.astype(jnp.bfloat16), 'tp', scatter_dimensio...  157 us
    all_gather x1, waiting for transfers between devices, body(): all_feats = lax.all_gather(activations, 'tp', axis=1, tiled=True)  78.5 us
    dot_general x1, other arithmetic, body(): lax.dot_general(gated, out_rows, (((1,), (1,)), ((), ())), preferred_elem...  47.7 us
    add x2, other arithmetic, causal_taps(): summed = summed + jnp.where(in_genome, window * taps[j], jnp.float32(0.0))  23.8 us
    ppermute x2, waiting for transfers between devices, passed_along(): return lax.ppermute(shard, axis, pairs)  20.1 us
    dot_general x1, matrix products, body(): summed = jnp.dot(normed, flat, preferred_element_type=jnp.float32)  13.9 us
  transfers between devices with their start and end apart: 5, of which 5 were waited for; matrix products, arithmetic and copies ran while one was open for 1% of the time, Pallas kernels for 0%

profile of v1, /device:TPU:9, one launch (start us, length us, event | category | flops | bytes accessed | tf_op | source)
XLA Modules:
  0.0 680.5 jit_solution(17413484477117585637)
XLA Ops:
  6.6 0.7 all-gather.3.cloned.1.call-update
  7.3 0.1 copy-done.2
  7.5 0.7 pad_maximum_fusion
  8.3 0.7 fusion.287
  10.9 1.3 add_compare_fusion.95
  12.2 78.5 %all-gather.3.cloned.1.call-done = bf16[640,4096]{1,0:T(8,128)(2,1)} async-done(((bf16[640,1024]{1,0:T(8,128)(2,1)}), bf16[640,4096]{1,0:T(8,128)(2,1)}) %all-gather.3.cloned.1.call-update) | async-done | bytes 5242896 | tf_op jit(solution)/shard_map/all_gather | solution.py:46
  90.7 3.6 fusion.2
  94.3 297.3 %all-gather.5.cloned.1.call-done = bf16[4096,2048]{1,0:T(8,128)(2,1)} async-done(((bf16[64,2048]{1,0:T(8,128)(2,1)}), bf16[4096,2048]{1,0:T(8,128)(2,1)}) %all-gather.5.cloned.1.call-update) | async-done | bytes 16777232 | tf_op jit(solution)/shard_map/all_gather | solution.py:56
  391.6 13.9 %fusion.20 = bf16[640,1536]{1,0:T(8,128)(2,1)} fusion(bf16[4096,2048]{1,0:T(8,128)(2,1)} %all-gather.5.cloned.1.call-done, bf16[640,4096]{1,0:T(8,128)(2,1)} %all-gather.3.cloned.1.call-done, f32[640]{0:T(1024)S(1)} %add_rsqrt_fusion), kind=kOutput, calls=%fused_computation.29 | convolution fusion | flops 8061911040 | bytes 19794432 | tf_op jit(solution)/shard_map/dot_general | solution.py:59
  405.5 2.8 copy.16
  408.2 0.2 constant_dynamic-slice_fusion
  408.4 1.9 collective-permute-start
  410.4 11.8 %collective-permute-done = bf16[6,3,512]{0,2,1:T(8,128)(2,1)S(1)} collective-permute-done((bf16[6,3,512]{0,2,1:T(8,128)(2,1)S(1)}, bf16[6,3,512]{0,2,1:T(8,128)(2,1)S(1)}, u32[]{:S(2)}, u32[]{:S(2)}) %collective-permute-start) | collective-permute-done | bytes 18464 | tf_op jit(solution)/shard_map/ppermute | solution.py:12
  422.2 1.0 maximum_convert_fusion
  423.3 8.1 %fusion.8 = f32[640,3,512]{0,2,1:T(8,128)S(1)} fusion(f32[646,3,512]{0,2,1:T(8,128)S(1)} %maximum_convert_fusion, f32[3,512]{1,0:T(4,128)S(1)} %get-tuple-element.270, f32[3,512]{1,0:T(4,128)S(1)} %get-tuple-element.271, f32[3,512]{1,0:T(4,128)S(1)} %get-tuple-element.272, f32[3,512]{1,0:T(4,128)S(1)} %get-tuple-element.273, ...), kind=kLoop, calls=%fused_computation.11 | loop fusion | flops 19660800 | bytes 31504768 | tf_op jit(solution)/shard_map/add | solution.py:27
  431.3 0.1 fusion.283
  431.6 2.1 collective-permute-start.1
  433.8 8.3 %collective-permute-done.1 = bf16[127,512]{0,1:T(8,128)(2,1)S(1)} collective-permute-done((bf16[127,512]{0,1:T(8,128)(2,1)S(1)}, bf16[127,512]{0,1:T(8,128)(2,1)S(1)}, u32[]{:S(2)}, u32[]{:S(2)}) %collective-permute-start.1) | collective-permute-done | bytes 130080 | tf_op jit(solution)/shard_map/ppermute | solution.py:12
  442.1 0.4 maximum_convert_fusion.1
  442.9 15.7 %fusion.221 = f32[640,512]{0,1:T(8,128)S(1)} fusion(f32[767,512]{0,1:T(8,128)S(1)} %maximum_convert_fusion.1, f32[512]{0:T(512)S(1)} %bitcast.198, f32[512]{0:T(512)S(1)} %bitcast.180, f32[512]{0:T(512)S(1)} %bitcast.181, f32[512]{0:T(512)S(1)} %bitcast.182, f32[512]{0:T(512)S(1)} %bitcast.183, f32[512]{0:T(512)S(1)} %bitcast.184, f32[512]{0:T(512)S(1)} %bitcast.185, ...), kind=kLoop, calls=%fused_computation.325 | loop fusion | flops 31129600 | bytes 43339776 | tf_op jit(solution)/shard_map/add | solution.py:27
  459.0 47.7 %fusion.304 = bf16[640,512]{0,1:T(8,128)(2,1)S(1)} fusion(f32[767,512]{0,1:T(8,128)S(1)} %maximum_convert_fusion.1, f32[640,512]{0,1:T(8,128)S(1)} %fusion.221, f32[512]{0:T(512)S(1)} %bitcast.199, f32[512]{0:T(512)S(1)} %bitcast.200, f32[512]{0:T(512)S(1)} %bitcast.239, f32[512]{0:T(512)S(1)} %bitcast.240, f32[512]{0:T(512)S(1)} %bitcast.241, ...), kind=kLoop, calls=%fused_computation.37.clone.clone.2 | loop fusion | flops 95027200 | bytes 129363968 | tf_op jit(solution)/shard_map/dot_general | solution.py:79
  506.7 7.5 %convolution_convert_fusion = bf16[640,4096]{1,0:T(8,128)(2,1)} fusion(bf16[4096,2048]{1,0:T(8,128)(2,1)} %all-gather.5.cloned.1.call-done, bf16[640,512]{0,1:T(8,128)(2,1)S(1)} %fusion.304), kind=kOutput, calls=%fused_computation.6 | convolution fusion | flops 2686976000 | bytes 10092544 | tf_op jit(solution)/shard_map/dot_general | solution.py:79
  514.3 156.9 %reduce-scatter.2.cloned.1.call-done = bf16[640,1024]{1,0:T(8,128)(2,1)} async-done(((bf16[640,4096]{1,0:T(8,128)(2,1)}), bf16[640,1024]{1,0:T(8,128)(2,1)}) %reduce-scatter.2.cloned.1.call-update) | async-done | bytes 1310736 | tf_op jit(solution)/shard_map/reduce_scatter | solution.py:85
  671.2 2.8 fusion.25
  (117 shorter events, 1.0 us)
Async XLA Ops:
  6.6 84.2 %all-gather.3.cloned.1.call-start = ((), (), s32[]{:S(2)}) async-start(), calls=%async_computation.1 | async-start | bytes 6553600 | tf_op jit(solution)/shard_map/all_gather | solution.py:46
  7.3 384.3 %all-gather.5.cloned.1.call-start = ((), (), s32[]{:S(2)}) async-start(), calls=%async_computation.2 | async-start | bytes 17039360 | tf_op jit(solution)/shard_map/all_gather | solution.py:56
  8.2 662.9 %reduce-scatter.2.cloned.1.call-start = ((), (), s32[]{:S(2)}) async-start(), calls=%async_computation.3 | async-start | bytes 6553600 | tf_op jit(solution)/shard_map/reduce_scatter | solution.py:85
  408.4 13.8 %collective-permute-start = (bf16[6,3,512]{0,2,1:T(8,128)(2,1)S(1)}, bf16[6,3,512]{0,2,1:T(8,128)(2,1)S(1)}, u32[]{:S(2)}, u32[]{:S(2)}) collective-permute-start(bf16[6,3,512]{0,2,1:T(8,128)(2,1)S(1)} %constant_dynamic-slice_fusion), channel_id=1, source_target_pairs={{0,4},{4,8},{8,12},{12,16},{16,20},{20,24},{24,28},{28,32},{32,36}... | collective-permute-start | bytes 55304 | tf_op jit(solution)/shard_map/ppermute | solution.py:12
  431.6 10.5 %collective-permute-start.1 = (bf16[127,512]{0,1:T(8,128)(2,1)S(1)}, bf16[127,512]{0,1:T(8,128)(2,1)S(1)}, u32[]{:S(2)}, u32[]{:S(2)}) collective-permute-start(bf16[127,512]{0,1:T(8,128)(2,1)S(1)} %dynamic-slice_bitcast_fusion), channel_id=1, source_target_pairs={{0,4},{4,8},{8,12},{12,16},{16,20},{20,24},{24,28},{28,32},{32,36}... | collective-permute-start | bytes 390152 | tf_op jit(solution)/shard_map/ppermute | solution.py:12
  442.5 16.1 %copy-start.5 = (pred[640]{0:T(1024)(128)(4,1)S(1)}, pred[640]{0:T(1024)(128)(4,1)}, u32[]{:S(2)}) copy-start(pred[640]{0:T(1024)(128)(4,1)} %get-tuple-element.160) | copy-start | bytes 1924
  442.5 16.1 %copy-start.6 = (pred[640]{0:T(1024)(128)(4,1)S(1)}, pred[640]{0:T(1024)(128)(4,1)}, u32[]{:S(2)}) copy-start(pred[640]{0:T(1024)(128)(4,1)} %get-tuple-element.161) | copy-start | bytes 1924
  442.5 16.1 %copy-start.7 = (pred[640]{0:T(1024)(128)(4,1)S(1)}, pred[640]{0:T(1024)(128)(4,1)}, u32[]{:S(2)}) copy-start(pred[640]{0:T(1024)(128)(4,1)} %get-tuple-element.162) | copy-start | bytes 1924
  442.5 16.1 %copy-start.8 = (pred[640]{0:T(1024)(128)(4,1)S(1)}, pred[640]{0:T(1024)(128)(4,1)}, u32[]{:S(2)}) copy-start(pred[640]{0:T(1024)(128)(4,1)} %get-tuple-element.163) | copy-start | bytes 1924
  442.5 16.1 %copy-start.9 = (pred[640]{0:T(1024)(128)(4,1)S(1)}, pred[640]{0:T(1024)(128)(4,1)}, u32[]{:S(2)}) copy-start(pred[640]{0:T(1024)(128)(4,1)} %get-tuple-element.164) | copy-start | bytes 1924
  442.5 16.1 %copy-start.10 = (pred[640]{0:T(1024)(128)(4,1)S(1)}, pred[640]{0:T(1024)(128)(4,1)}, u32[]{:S(2)}) copy-start(pred[640]{0:T(1024)(128)(4,1)} %get-tuple-element.165) | copy-start | bytes 1924
  442.5 16.1 %copy-start.11 = (pred[640]{0:T(1024)(128)(4,1)S(1)}, pred[640]{0:T(1024)(128)(4,1)}, u32[]{:S(2)}) copy-start(pred[640]{0:T(1024)(128)(4,1)} %get-tuple-element.166) | copy-start | bytes 1924
  442.5 16.1 %copy-start.12 = (pred[640]{0:T(1024)(128)(4,1)S(1)}, pred[640]{0:T(1024)(128)(4,1)}, u32[]{:S(2)}) copy-start(pred[640]{0:T(1024)(128)(4,1)} %get-tuple-element.167) | copy-start | bytes 1924
  442.6 16.1 %copy-start.13 = (pred[640]{0:T(1024)(128)(4,1)S(1)}, pred[640]{0:T(1024)(128)(4,1)}, u32[]{:S(2)}) copy-start(pred[640]{0:T(1024)(128)(4,1)} %get-tuple-element.168) | copy-start | bytes 1924
  442.6 16.1 %copy-start.14 = (pred[640]{0:T(1024)(128)(4,1)S(1)}, pred[640]{0:T(1024)(128)(4,1)}, u32[]{:S(2)}) copy-start(pred[640]{0:T(1024)(128)(4,1)} %get-tuple-element.169) | copy-start | bytes 1924
  442.6 16.1 %copy-start.15 = (pred[640]{0:T(1024)(128)(4,1)S(1)}, pred[640]{0:T(1024)(128)(4,1)}, u32[]{:S(2)}) copy-start(pred[640]{0:T(1024)(128)(4,1)} %get-tuple-element.170) | copy-start | bytes 1924
  442.6 16.1 %copy-start.16 = (pred[640]{0:T(1024)(128)(4,1)S(1)}, pred[640]{0:T(1024)(128)(4,1)}, u32[]{:S(2)}) copy-start(pred[640]{0:T(1024)(128)(4,1)} %get-tuple-element.171) | copy-start | bytes 1924
  442.6 16.1 %copy-start.17 = (pred[640]{0:T(1024)(128)(4,1)S(1)}, pred[640]{0:T(1024)(128)(4,1)}, u32[]{:S(2)}) copy-start(pred[640]{0:T(1024)(128)(4,1)} %get-tuple-element.172) | copy-start | bytes 1924
  442.6 16.1 %copy-start.18 = (pred[640]{0:T(1024)(128)(4,1)S(1)}, pred[640]{0:T(1024)(128)(4,1)}, u32[]{:S(2)}) copy-start(pred[640]{0:T(1024)(128)(4,1)} %get-tuple-element.173) | copy-start | bytes 1924
  442.6 16.1 %copy-start.19 = (pred[640]{0:T(1024)(128)(4,1)S(1)}, pred[640]{0:T(1024)(128)(4,1)}, u32[]{:S(2)}) copy-start(pred[640]{0:T(1024)(128)(4,1)} %get-tuple-element.174) | copy-start | bytes 1924
  442.6 16.1 %copy-start.20 = (pred[640]{0:T(1024)(128)(4,1)S(1)}, pred[640]{0:T(1024)(128)(4,1)}, u32[]{:S(2)}) copy-start(pred[640]{0:T(1024)(128)(4,1)} %get-tuple-element.175) | copy-start | bytes 1924
  442.6 16.1 %copy-start.21 = (pred[640]{0:T(1024)(128)(4,1)S(1)}, pred[640]{0:T(1024)(128)(4,1)}, u32[]{:S(2)}) copy-start(pred[640]{0:T(1024)(128)(4,1)} %get-tuple-element.176) | copy-start | bytes 1924
  442.6 16.1 %copy-start.22 = (pred[640]{0:T(1024)(128)(4,1)S(1)}, pred[640]{0:T(1024)(128)(4,1)}, u32[]{:S(2)}) copy-start(pred[640]{0:T(1024)(128)(4,1)} %get-tuple-element.177) | copy-start | bytes 1924
  514.2 157.0 %copy-start = (bf16[640,1024]{1,0:T(8,128)(2,1)S(1)}, bf16[640,1024]{1,0:T(8,128)(2,1)}, u32[]{:S(2)}) copy-start(bf16[640,1024]{1,0:T(8,128)(2,1)} %param.7) | copy-start | bytes 3932164
  (28 other events, 370.7 us)
Sparse Core Ops, SparseCore 0:
  9.2 81.4 all-gather.2
  92.5 299.0 all-gather.4
  514.4 156.7 reduce-scatter.1

commit v2 on v1

--- a/solution.py
+++ b/solution.py
@@ -4,6 +4,8 @@
 from jax.sharding import PartitionSpec as P
 
 GROUP = 128
+CTX = ("y", "zl", "x")
+TP = ("zh", "core")
 
 
 def passed_along(shard, axis, by):
@@ -29,8 +31,8 @@
 
 
 def body(activations, group_counts, genome_starts, in_weight, short_taps, long_taps, out_weight):
-    ctx_size = lax.axis_size("ctx")
-    my_index = lax.axis_index("ctx")
+    ctx_size = lax.axis_size(CTX)
+    my_index = lax.axis_index(CTX)
     own_rows = activations.shape[0]
     device_ids = jnp.arange(ctx_size, dtype=jnp.int32)
     own_count = jnp.sum(jnp.where(device_ids == my_index, group_counts, 0))
@@ -43,7 +45,7 @@
         return lax.dynamic_slice_in_dim(source, tail_end - count, count, 0)
 
     gstart = genome_start(positions, genome_starts)
-    all_feats = lax.all_gather(activations, "tp", axis=1, tiled=True)
+    all_feats = lax.all_gather(activations, TP, axis=1, tiled=True)
     widened = all_feats.astype(jnp.float32)
     normed = (
         widened * lax.rsqrt(jnp.mean(widened * widened, axis=1, keepdims=True) + 1e-06)
@@ -53,12 +55,14 @@
     chans = in_weight.shape[2]
     local_in = in_weight.reshape(in_weight.shape[0], branches * chans)
     both = jnp.concatenate([local_in, out_weight.T], axis=1)
-    both_rows = lax.all_gather(both, "ctx", axis=0, tiled=True)
+    both_rows = both
+    for part in reversed(CTX):
+        both_rows = lax.all_gather(both_rows, part, axis=0, tiled=True)
     flat = both_rows[:, : branches * chans]
     out_rows = both_rows[:, branches * chans :]
     summed = jnp.dot(normed, flat, preferred_element_type=jnp.float32)
     projected = summed.astype(jnp.bfloat16).reshape(row_count, branches, chans)
-    rim_short = passed_along(last_rows(projected, 6), "ctx", 1)
+    rim_short = passed_along(last_rows(projected, 6), CTX, 1)
     feat = causal_taps(
         jnp.concatenate([rim_short, projected], axis=0).astype(jnp.float32),
         short_taps,
@@ -67,7 +71,7 @@
         7,
     )
     mixed = (feat[:, 1] * feat[:, 2]).astype(jnp.bfloat16)
-    rim_long = passed_along(last_rows(mixed, 127), "ctx", 1)
+    rim_long = passed_along(last_rows(mixed, 127), CTX, 1)
     filtered = causal_taps(
         jnp.concatenate([rim_long, mixed], axis=0).astype(jnp.float32),
         long_taps,
@@ -83,7 +87,7 @@
         preferred_element_type=jnp.float32,
     )
     branch_out = lax.psum_scatter(
-        partial_out.astype(jnp.bfloat16), "tp", scatter_dimension=1, tiled=True
+        partial_out.astype(jnp.bfloat16), TP, scatter_dimension=1, tiled=True
     ).astype(jnp.float32)
     result = (activations.astype(jnp.float32) + branch_out).astype(jnp.bfloat16)
     slot_ids = jnp.arange(own_rows, dtype=jnp.int32)
@@ -92,15 +96,16 @@
 
 
 def solution(mesh):
+    fine = jax.sharding.Mesh(mesh.devices.reshape(4, 4, 4, 2, 2), CTX + TP)
     placed = (
-        P("ctx", "tp"),
+        P(CTX, TP),
         P(),
         P(),
-        P("ctx", None, "tp"),
-        P(None, None, "tp"),
-        P(None, "tp"),
-        P("tp", "ctx"),
+        P(CTX, None, TP),
+        P(None, None, TP),
+        P(None, TP),
+        P(TP, CTX),
     )
     return jax.shard_map(
-        body, mesh=mesh, in_specs=placed, out_specs=P("ctx", "tp"), check_vma=False
+        body, mesh=fine, in_specs=placed, out_specs=P(CTX, TP), check_vma=False
     )

time: 682 us -> 591 us (0.87)
  waiting for transfers between devices: 554 us -> 459 us
    reduce_scatter x1, waiting for transfers between devices: 157 us -> 95.2 us  [body(): lax.psum_scatter(partial_out.astype(jnp.bfloat16), TP, scatter_dimension=...]
    all_gather x2 -> x4, waiting for transfers between devices: 376 us -> 342 us  [the longest x3 265 us: body(): both_rows = lax.all_gather(both_rows, part, axis=0, tiled=True)]
  transfers between devices with their start and end apart: 5 -> 7, of which waited for: 5 -> 7; matrix products, arithmetic and copies ran while one was open for 1% -> 1% of each run, Pallas kernels for 0% -> 0%
where the time goes in v2:
time: 591 us; the launch traced here: 589 us
  waiting for transfers between devices  459 us (78%)
  other arithmetic  83.1 us (14%)
  matrix products  21.3 us (4%)
  between operations  15.2 us (3%)
    all_gather x3, waiting for transfers between devices, body(): both_rows = lax.all_gather(both_rows, part, axis=0, tiled=True)  265 us
    reduce_scatter x1, waiting for transfers between devices, body(): lax.psum_scatter(partial_out.astype(jnp.bfloat16), TP, scatter_dimension=...  95.2 us
    all_gather x1, waiting for transfers between devices, body(): all_feats = lax.all_gather(activations, TP, axis=1, tiled=True)  76.6 us
    dot_general x1, other arithmetic, body(): lax.dot_general(gated, out_rows, (((1,), (1,)), ((), ())), preferred_elem...  47.7 us
    add x2, other arithmetic, causal_taps(): summed = summed + jnp.where(in_genome, window * taps[j], jnp.float32(0.0))  23.8 us
    ppermute x2, waiting for transfers between devices, passed_along(): return lax.ppermute(shard, axis, pairs)  21.7 us
    dot_general x1, matrix products, body(): summed = jnp.dot(normed, flat, preferred_element_type=jnp.float32)  13.8 us
  transfers between devices with their start and end apart: 7, of which 7 were waited for; matrix products, arithmetic and copies ran while one was open for 1% of the time, Pallas kernels for 0%

profile of v2, /device:TPU:9, one launch (start us, length us, event | category | flops | bytes accessed | tf_op | source)
XLA Modules:
  0.0 589.3 jit_solution(5868965116954056828)
XLA Ops:
  6.5 0.9 copy.30
  7.5 1.6 pad_maximum_fusion
  9.1 27.5 %all-gather.7.cloned.1.call-done = bf16[256,2048]{1,0:T(8,128)(2,1)} async-done(((bf16[64,2048]{1,0:T(8,128)(2,1)}), bf16[256,2048]{1,0:T(8,128)(2,1)}) %all-gather.7.cloned.1.call-update) | async-done | bytes 1048592 | tf_op jit(solution)/shard_map/all_gather | solution.py:60
  36.7 0.7 all-gather.5.cloned.1.call-update
  37.5 87.2 %all-gather.9.cloned.1.call-done = bf16[1024,2048]{1,0:T(8,128)(2,1)} async-done(((bf16[256,2048]{1,0:T(8,128)(2,1)}), bf16[1024,2048]{1,0:T(8,128)(2,1)}) %all-gather.9.cloned.1.call-update) | async-done | bytes 4194320 | tf_op jit(solution)/shard_map/all_gather | solution.py:60
  124.8 0.6 copy-done.44
  125.3 0.6 fusion.287
  127.7 1.3 add_compare_fusion.95
  129.0 76.6 %all-gather.5.cloned.1.call-done = bf16[640,4096]{1,0:T(8,128)(2,1)} async-done(((bf16[640,1024]{1,0:T(8,128)(2,1)}), bf16[640,4096]{1,0:T(8,128)(2,1)}) %all-gather.5.cloned.1.call-update) | async-done | bytes 5242896 | tf_op jit(solution)/shard_map/all_gather | solution.py:48
  205.6 3.6 fusion.2
  209.1 150.2 %all-gather.11.cloned.1.call-done = bf16[4096,2048]{1,0:T(8,128)(2,1)} async-done(((bf16[1024,2048]{1,0:T(8,128)(2,1)}), bf16[4096,2048]{1,0:T(8,128)(2,1)}) %all-gather.11.cloned.1.call-update) | async-done | bytes 16777232 | tf_op jit(solution)/shard_map/all_gather | solution.py:60
  359.4 13.8 %fusion.20 = bf16[640,1536]{1,0:T(8,128)(2,1)} fusion(bf16[4096,2048]{1,0:T(8,128)(2,1)} %all-gather.11.cloned.1.call-done, bf16[640,4096]{1,0:T(8,128)(2,1)} %all-gather.5.cloned.1.call-done, f32[640]{0:T(1024)S(1)} %add_rsqrt_fusion), kind=kOutput, calls=%fused_computation.29 | convolution fusion | flops 8061911040 | bytes 19794432 | tf_op jit(solution)/shard_map/dot_general | solution.py:63
  373.2 2.8 copy.16
  376.2 3.1 collective-permute-start
  379.3 13.4 %collective-permute-done = bf16[6,3,512]{0,2,1:T(8,128)(2,1)S(1)} collective-permute-done((bf16[6,3,512]{0,2,1:T(8,128)(2,1)S(1)}, bf16[6,3,512]{0,2,1:T(8,128)(2,1)S(1)}, u32[]{:S(2)}, u32[]{:S(2)}) %collective-permute-start) | collective-permute-done | bytes 18464 | tf_op jit(solution)/shard_map/ppermute | solution.py:14
  392.7 1.0 maximum_convert_fusion
  393.8 8.1 %fusion.8 = f32[640,3,512]{0,2,1:T(8,128)S(1)} fusion(f32[646,3,512]{0,2,1:T(8,128)S(1)} %maximum_convert_fusion, f32[3,512]{1,0:T(4,128)S(1)} %get-tuple-element.270, f32[3,512]{1,0:T(4,128)S(1)} %get-tuple-element.271, f32[3,512]{1,0:T(4,128)S(1)} %get-tuple-element.272, f32[3,512]{1,0:T(4,128)S(1)} %get-tuple-element.273, ...), kind=kLoop, calls=%fused_computation.11 | loop fusion | flops 19660800 | bytes 31504768 | tf_op jit(solution)/shard_map/add | solution.py:29
  402.1 2.1 collective-permute-start.1
  404.3 8.3 %collective-permute-done.1 = bf16[127,512]{0,1:T(8,128)(2,1)S(1)} collective-permute-done((bf16[127,512]{0,1:T(8,128)(2,1)S(1)}, bf16[127,512]{0,1:T(8,128)(2,1)S(1)}, u32[]{:S(2)}, u32[]{:S(2)}) %collective-permute-start.1) | collective-permute-done | bytes 130080 | tf_op jit(solution)/shard_map/ppermute | solution.py:14
  413.4 15.7 %fusion.221 = f32[640,512]{0,1:T(8,128)S(1)} fusion(f32[767,512]{0,1:T(8,128)S(1)} %maximum_convert_fusion.1, f32[512]{0:T(512)S(1)} %bitcast.198, f32[512]{0:T(512)S(1)} %bitcast.180, f32[512]{0:T(512)S(1)} %bitcast.181, f32[512]{0:T(512)S(1)} %bitcast.182, f32[512]{0:T(512)S(1)} %bitcast.183, f32[512]{0:T(512)S(1)} %bitcast.184, f32[512]{0:T(512)S(1)} %bitcast.185, ...), kind=kLoop, calls=%fused_computation.325 | loop fusion | flops 31129600 | bytes 43339776 | tf_op jit(solution)/shard_map/add | solution.py:29
  429.5 47.7 %fusion.304 = bf16[640,512]{0,1:T(8,128)(2,1)S(1)} fusion(f32[767,512]{0,1:T(8,128)S(1)} %maximum_convert_fusion.1, f32[640,512]{0,1:T(8,128)S(1)} %fusion.221, f32[512]{0:T(512)S(1)} %bitcast.199, f32[512]{0:T(512)S(1)} %bitcast.200, f32[512]{0:T(512)S(1)} %bitcast.239, f32[512]{0:T(512)S(1)} %bitcast.240, f32[512]{0:T(512)S(1)} %bitcast.241, ...), kind=kLoop, calls=%fused_computation.37.clone.clone.2 | loop fusion | flops 95027200 | bytes 129363968 | tf_op jit(solution)/shard_map/dot_general | solution.py:83
  477.2 7.5 %convolution_convert_fusion = bf16[640,4096]{1,0:T(8,128)(2,1)} fusion(bf16[4096,2048]{1,0:T(8,128)(2,1)} %all-gather.11.cloned.1.call-done, bf16[640,512]{0,1:T(8,128)(2,1)S(1)} %fusion.304), kind=kOutput, calls=%fused_computation.6 | convolution fusion | flops 2686976000 | bytes 10092544 | tf_op jit(solution)/shard_map/dot_general | solution.py:83
  484.8 95.2 %reduce-scatter.2.cloned.1.call-done = bf16[640,1024]{1,0:T(8,128)(2,1)} async-done(((bf16[640,4096]{1,0:T(8,128)(2,1)}), bf16[640,1024]{1,0:T(8,128)(2,1)}) %reduce-scatter.2.cloned.1.call-update) | async-done | bytes 1310736 | tf_op jit(solution)/shard_map/reduce_scatter | solution.py:89
  579.9 2.8 fusion.25
  (119 shorter events, 1.7 us)
Async XLA Ops:
  6.5 30.1 %all-gather.7.cloned.1.call-start = ((), (), s32[]{:S(2)}) async-start(), calls=%async_computation.2 | async-start | bytes 1310720 | tf_op jit(solution)/shard_map/all_gather | solution.py:60
  9.1 115.6 %all-gather.9.cloned.1.call-start = ((), (), s32[]{:S(2)}) async-start(), calls=%async_computation.3 | async-start | bytes 5242880 | tf_op jit(solution)/shard_map/all_gather | solution.py:60
  36.7 168.9 %all-gather.5.cloned.1.call-start = ((), (), s32[]{:S(2)}) async-start(), calls=%async_computation.1 | async-start | bytes 6553600 | tf_op jit(solution)/shard_map/all_gather | solution.py:48
  37.4 322.0 %all-gather.11.cloned.1.call-start = ((), (), s32[]{:S(2)}) async-start(), calls=%async_computation.4 | async-start | bytes 20971520 | tf_op jit(solution)/shard_map/all_gather | solution.py:60
  124.7 455.2 %reduce-scatter.2.cloned.1.call-start = ((), (), s32[]{:S(2)}) async-start(), calls=%async_computation.5 | async-start | bytes 6553600 | tf_op jit(solution)/shard_map/reduce_scatter | solution.py:89
  376.2 16.5 %collective-permute-start = (bf16[6,3,512]{0,2,1:T(8,128)(2,1)S(1)}, bf16[6,3,512]{0,2,1:T(8,128)(2,1)S(1)}, u32[]{:S(2)}, u32[]{:S(2)}) collective-permute-start(bf16[6,3,512]{0,2,1:T(8,128)(2,1)S(1)} %constant_dynamic-slice_fusion), channel_id=1, source_target_pairs={{0,4},{4,8},{8,12},{12,16},{16,20},{20,24},{24,28},{28,32},{32,36}... | collective-permute-start | bytes 55304 | tf_op jit(solution)/shard_map/ppermute | solution.py:14
  402.1 10.5 %collective-permute-start.1 = (bf16[127,512]{0,1:T(8,128)(2,1)S(1)}, bf16[127,512]{0,1:T(8,128)(2,1)S(1)}, u32[]{:S(2)}, u32[]{:S(2)}) collective-permute-start(bf16[127,512]{0,1:T(8,128)(2,1)S(1)} %dynamic-slice_bitcast_fusion), channel_id=1, source_target_pairs={{0,4},{4,8},{8,12},{12,16},{16,20},{20,24},{24,28},{28,32},{32,36}... | collective-permute-start | bytes 390152 | tf_op jit(solution)/shard_map/ppermute | solution.py:14
  413.0 16.1 %copy-start.3 = (pred[640]{0:T(1024)(128)(4,1)S(1)}, pred[640]{0:T(1024)(128)(4,1)}, u32[]{:S(2)}) copy-start(pred[640]{0:T(1024)(128)(4,1)} %get-tuple-element.160) | copy-start | bytes 1924
  413.0 16.1 %copy-start.4 = (pred[640]{0:T(1024)(128)(4,1)S(1)}, pred[640]{0:T(1024)(128)(4,1)}, u32[]{:S(2)}) copy-start(pred[640]{0:T(1024)(128)(4,1)} %get-tuple-element.161) | copy-start | bytes 1924
  413.0 16.1 %copy-start.5 = (pred[640]{0:T(1024)(128)(4,1)S(1)}, pred[640]{0:T(1024)(128)(4,1)}, u32[]{:S(2)}) copy-start(pred[640]{0:T(1024)(128)(4,1)} %get-tuple-element.162) | copy-start | bytes 1924
  413.0 16.1 %copy-start.6 = (pred[640]{0:T(1024)(128)(4,1)S(1)}, pred[640]{0:T(1024)(128)(4,1)}, u32[]{:S(2)}) copy-start(pred[640]{0:T(1024)(128)(4,1)} %get-tuple-element.163) | copy-start | bytes 1924
  413.0 16.1 %copy-start.7 = (pred[640]{0:T(1024)(128)(4,1)S(1)}, pred[640]{0:T(1024)(128)(4,1)}, u32[]{:S(2)}) copy-start(pred[640]{0:T(1024)(128)(4,1)} %get-tuple-element.164) | copy-start | bytes 1924
  413.0 16.1 %copy-start.8 = (pred[640]{0:T(1024)(128)(4,1)S(1)}, pred[640]{0:T(1024)(128)(4,1)}, u32[]{:S(2)}) copy-start(pred[640]{0:T(1024)(128)(4,1)} %get-tuple-element.165) | copy-start | bytes 1924
  413.0 16.1 %copy-start.9 = (pred[640]{0:T(1024)(128)(4,1)S(1)}, pred[640]{0:T(1024)(128)(4,1)}, u32[]{:S(2)}) copy-start(pred[640]{0:T(1024)(128)(4,1)} %get-tuple-element.166) | copy-start | bytes 1924
  413.1 16.1 %copy-start.10 = (pred[640]{0:T(1024)(128)(4,1)S(1)}, pred[640]{0:T(1024)(128)(4,1)}, u32[]{:S(2)}) copy-start(pred[640]{0:T(1024)(128)(4,1)} %get-tuple-element.167) | copy-start | bytes 1924
  413.1 16.1 %copy-start.11 = (pred[640]{0:T(1024)(128)(4,1)S(1)}, pred[640]{0:T(1024)(128)(4,1)}, u32[]{:S(2)}) copy-start(pred[640]{0:T(1024)(128)(4,1)} %get-tuple-element.168) | copy-start | bytes 1924
  413.1 16.1 %copy-start.12 = (pred[640]{0:T(1024)(128)(4,1)S(1)}, pred[640]{0:T(1024)(128)(4,1)}, u32[]{:S(2)}) copy-start(pred[640]{0:T(1024)(128)(4,1)} %get-tuple-element.169) | copy-start | bytes 1924
  413.1 16.1 %copy-start.13 = (pred[640]{0:T(1024)(128)(4,1)S(1)}, pred[640]{0:T(1024)(128)(4,1)}, u32[]{:S(2)}) copy-start(pred[640]{0:T(1024)(128)(4,1)} %get-tuple-element.170) | copy-start | bytes 1924
  413.1 16.1 %copy-start.14 = (pred[640]{0:T(1024)(128)(4,1)S(1)}, pred[640]{0:T(1024)(128)(4,1)}, u32[]{:S(2)}) copy-start(pred[640]{0:T(1024)(128)(4,1)} %get-tuple-element.171) | copy-start | bytes 1924
  413.1 16.1 %copy-start.15 = (pred[640]{0:T(1024)(128)(4,1)S(1)}, pred[640]{0:T(1024)(128)(4,1)}, u32[]{:S(2)}) copy-start(pred[640]{0:T(1024)(128)(4,1)} %get-tuple-element.172) | copy-start | bytes 1924
  413.1 16.1 %copy-start.16 = (pred[640]{0:T(1024)(128)(4,1)S(1)}, pred[640]{0:T(1024)(128)(4,1)}, u32[]{:S(2)}) copy-start(pred[640]{0:T(1024)(128)(4,1)} %get-tuple-element.173) | copy-start | bytes 1924
  413.1 16.1 %copy-start.17 = (pred[640]{0:T(1024)(128)(4,1)S(1)}, pred[640]{0:T(1024)(128)(4,1)}, u32[]{:S(2)}) copy-start(pred[640]{0:T(1024)(128)(4,1)} %get-tuple-element.174) | copy-start | bytes 1924
  413.1 16.1 %copy-start.18 = (pred[640]{0:T(1024)(128)(4,1)S(1)}, pred[640]{0:T(1024)(128)(4,1)}, u32[]{:S(2)}) copy-start(pred[640]{0:T(1024)(128)(4,1)} %get-tuple-element.175) | copy-start | bytes 1924
  484.8 95.2 %copy-start = (bf16[640,1024]{1,0:T(8,128)(2,1)S(1)}, bf16[640,1024]{1,0:T(8,128)(2,1)}, u32[]{:S(2)}) copy-start(bf16[640,1024]{1,0:T(8,128)(2,1)} %param.7) | copy-start | bytes 3932164
  (28 other events, 395.9 us)
Sparse Core Ops, SparseCore 0:
  9.2 27.4 all-gather.6
  38.5 86.1 all-gather.8
  126.5 78.9 all-gather.4
  207.2 152.1 all-gather.10
  484.9 95.0 reduce-scatter.1

commit v3 on v2

--- a/solution.py
+++ b/solution.py
@@ -4,6 +4,7 @@
 from jax.sharding import PartitionSpec as P
 
 GROUP = 128
+PAIR_BLOCKS = 6
 CTX = ("y", "zl", "x")
 TP = ("zh", "core")
 
@@ -12,6 +13,30 @@
     peers = lax.axis_size(axis)
     pairs = [(i, i + by) for i in range(peers) if 0 <= i + by < peers]
     return lax.ppermute(shard, axis, pairs)
+
+
+def swapped(shard, axis):
+    peers = lax.axis_size(axis)
+    pairs = [(i, i ^ 1) for i in range(peers)]
+    return lax.ppermute(shard, axis, pairs)
+
+
+def shifted(source, offset, count):
+    width = source.shape[1:]
+    pad = 2 * count
+    zeros = jnp.zeros((pad,) + width, source.dtype)
+    padded = jnp.concatenate([zeros, source, zeros], axis=0)
+    start = jnp.clip(pad + offset, 0, padded.shape[0] - count)
+    return lax.dynamic_slice_in_dim(padded, start, count, 0)
+
+
+def spliced(first, first_off, first_len, second, second_off, count):
+    rows = jnp.arange(count, dtype=jnp.int32).reshape((count,) + (1,) * (first.ndim - 1))
+    return jnp.where(
+        rows < first_len,
+        shifted(first, first_off, count),
+        shifted(second, second_off, count),
+    )
 
 
 def genome_start(positions, genome_starts):
@@ -31,21 +56,30 @@
 
 
 def body(activations, group_counts, genome_starts, in_weight, short_taps, long_taps, out_weight):
-    ctx_size = lax.axis_size(CTX)
     my_index = lax.axis_index(CTX)
     own_rows = activations.shape[0]
-    device_ids = jnp.arange(ctx_size, dtype=jnp.int32)
-    own_count = jnp.sum(jnp.where(device_ids == my_index, group_counts, 0))
-    offset = jnp.sum(jnp.where(device_ids < my_index, group_counts, 0))
-    row_ids = jnp.arange(own_rows, dtype=jnp.int32)
-    positions = offset * GROUP + row_ids
-    tail_end = own_count * GROUP
+    share = PAIR_BLOCKS * GROUP // 2
+    window = own_rows - share
+    parity = my_index % 2
+    even_count = jnp.sum(
+        jnp.where(jnp.arange(group_counts.shape[0]) == my_index - parity, group_counts, 0)
+    )
+    even_rows = even_count * GROUP
+    own_count = jnp.where(parity == 0, even_count, PAIR_BLOCKS - even_count)
+
+    sent = lax.dynamic_slice_in_dim(activations, (1 - parity) * share, window, 0)
+    got = swapped(sent, CTX)
+    x_even = spliced(activations, 0, even_rows, got, -even_rows, share)
+    x_odd = spliced(got, 0, even_rows - share, activations, share - even_rows, share)
+    x_own = jnp.where(parity == 0, x_even, x_odd)
+
+    positions = my_index * share + jnp.arange(share, dtype=jnp.int32)
 
     def last_rows(source, count):
-        return lax.dynamic_slice_in_dim(source, tail_end - count, count, 0)
+        return source[share - count :]
 
     gstart = genome_start(positions, genome_starts)
-    all_feats = lax.all_gather(activations, TP, axis=1, tiled=True)
+    all_feats = lax.all_gather(x_own, TP, axis=1, tiled=True)
     widened = all_feats.astype(jnp.float32)
     normed = (
         widened * lax.rsqrt(jnp.mean(widened * widened, axis=1, keepdims=True) + 1e-06)
@@ -89,10 +123,23 @@
     branch_out = lax.psum_scatter(
         partial_out.astype(jnp.bfloat16), TP, scatter_dimension=1, tiled=True
     ).astype(jnp.float32)
-    result = (activations.astype(jnp.float32) + branch_out).astype(jnp.bfloat16)
+    result = (x_own.astype(jnp.float32) + branch_out).astype(jnp.bfloat16)
+
+    back = lax.dynamic_slice_in_dim(result, (1 - parity) * (share - window), window, 0)
+    got_back = swapped(back, CTX)
+    out_even = spliced(result, 0, share, got_back, -share, own_rows)
+    out_odd = spliced(
+        got_back,
+        even_rows - (share - window),
+        share - even_rows,
+        result,
+        even_rows - share,
+        own_rows,
+    )
+    placed_rows = jnp.where(parity == 0, out_even, out_odd)
     slot_ids = jnp.arange(own_rows, dtype=jnp.int32)
     live_rows = (slot_ids < own_count * GROUP)[:, None]
-    return jnp.where(live_rows, result, jnp.zeros_like(result))
+    return jnp.where(live_rows, placed_rows, jnp.zeros_like(placed_rows))
 
 
 def solution(mesh):

time: 591 us -> 532 us (0.900)
  waiting for transfers between devices: 459 us -> 412 us
  other arithmetic: 83.1 us -> 73.5 us
  matrix products: 21.3 us -> 13.8 us
    reduce_scatter x1, waiting for transfers between devices: 95.2 us -> 70.2 us  [body(): lax.psum_scatter(partial_out.astype(jnp.bfloat16), TP, scatter_dimension=...]
    all_gather x1, waiting for transfers between devices: 76.6 us -> 53 us  [body(): all_feats = lax.all_gather(x_own, TP, axis=1, tiled=True)]
    ppermute x0 -> x2, waiting for transfers between devices: none -> 19.3 us  [swapped(): return lax.ppermute(shard, axis, pairs)]
    all_gather x3, waiting for transfers between devices: 265 us -> 250 us  [body(): both_rows = lax.all_gather(both_rows, part, axis=0, tiled=True)]
    dot_general x1, other arithmetic: 47.7 us -> 32.6 us  [body(): lax.dot_general(gated, out_rows, (((1,), (1,)), ((), ())), preferred_elem...]
    select_n x1 -> x2, other arithmetic: 2.78 us -> 14.5 us  [the longest x1 9.31 us: body(): return jnp.where(live_rows, placed_rows, jnp.zeros_like(placed_rows))]
    add x2, other arithmetic: 23.8 us -> 16.7 us  [causal_taps(): summed = summed + jnp.where(in_genome, window * taps[j], jnp.float32(0.0))]
  transfers between devices with their start and end apart: 7 -> 9, of which waited for: 7 -> 9; matrix products, arithmetic and copies ran while one was open for 1% -> 3% of each run, Pallas kernels for 0% -> 0%
where the time goes in v3:
time: 532 us; the launch traced here: 531 us
  waiting for transfers between devices  412 us (77%)
  other arithmetic  73.5 us (14%)
  between operations  15.9 us (3%)
  matrix products  13.8 us (3%)
  local copies, waits for them, and re-layouts  7.65 us (1%)
  starting transfers between devices  7.45 us (1%)
    all_gather x3, waiting for transfers between devices, body(): both_rows = lax.all_gather(both_rows, part, axis=0, tiled=True)  250 us
    reduce_scatter x1, waiting for transfers between devices, body(): lax.psum_scatter(partial_out.astype(jnp.bfloat16), TP, scatter_dimension=...  70.2 us
    all_gather x1, waiting for transfers between devices, body(): all_feats = lax.all_gather(x_own, TP, axis=1, tiled=True)  53 us
    dot_general x1, other arithmetic, body(): lax.dot_general(gated, out_rows, (((1,), (1,)), ((), ())), preferred_elem...  32.6 us
    ppermute x2, waiting for transfers between devices, passed_along(): return lax.ppermute(shard, axis, pairs)  20 us
    ppermute x2, waiting for transfers between devices, swapped(): return lax.ppermute(shard, axis, pairs)  19.3 us
    add x2, other arithmetic, causal_taps(): summed = summed + jnp.where(in_genome, window * taps[j], jnp.float32(0.0))  16.7 us
  transfers between devices with their start and end apart: 9, of which 9 were waited for; matrix products, arithmetic and copies ran while one was open for 3% of the time, Pallas kernels for 0%

profile of v3, /device:TPU:9, one launch (start us, length us, event | category | flops | bytes accessed | tf_op | source)
XLA Modules:
  0.0 530.5 jit_solution(8355105288129810825)
XLA Ops:
  7.6 1.6 pad_maximum_fusion
  9.2 27.5 %all-gather.7.cloned.1.call-done = bf16[256,2048]{1,0:T(8,128)(2,1)} async-done(((bf16[64,2048]{1,0:T(8,128)(2,1)}), bf16[256,2048]{1,0:T(8,128)(2,1)}) %all-gather.7.cloned.1.call-update) | async-done | bytes 1048592 | tf_op jit(solution)/shard_map/all_gather | solution.py:94
  38.7 9.0 %collective-permute-done = bf16[256,1024]{1,0:T(8,128)(2,1)S(1)} collective-permute-done((bf16[256,1024]{1,0:T(8,128)(2,1)S(1)}, bf16[256,1024]{1,0:T(8,128)(2,1)S(1)}, u32[]{:S(2)}, u32[]{:S(2)}) %collective-permute-start) | collective-permute-done | bytes 524320 | tf_op jit(solution)/shard_map/ppermute | solution.py:21
  47.9 5.2 fusion.38
  53.2 71.6 %all-gather.9.cloned.1.call-done = bf16[1024,2048]{1,0:T(8,128)(2,1)} async-done(((bf16[256,2048]{1,0:T(8,128)(2,1)}), bf16[1024,2048]{1,0:T(8,128)(2,1)}) %all-gather.9.cloned.1.call-update) | async-done | bytes 4194320 | tf_op jit(solution)/shard_map/all_gather | solution.py:94
  127.7 1.5 add_compare_fusion.95
  129.3 53.0 %all-gather.5.cloned.1.call-done = bf16[384,4096]{1,0:T(8,128)(2,1)} async-done(((bf16[384,1024]{1,0:T(8,128)(2,1)}), bf16[384,4096]{1,0:T(8,128)(2,1)}) %all-gather.5.cloned.1.call-update) | async-done | bytes 3145744 | tf_op jit(solution)/shard_map/all_gather | solution.py:82
  182.2 2.7 fusion.2
  185.6 150.5 %all-gather.11.cloned.1.call-done = bf16[4096,2048]{1,0:T(8,128)(2,1)} async-done(((bf16[1024,2048]{1,0:T(8,128)(2,1)}), bf16[4096,2048]{1,0:T(8,128)(2,1)}) %all-gather.11.cloned.1.call-update) | async-done | bytes 16777232 | tf_op jit(solution)/shard_map/all_gather | solution.py:94
  336.1 8.1 %fusion.7 = bf16[384,1536]{1,0:T(8,128)(2,1)S(1)} fusion(bf16[4096,2048]{1,0:T(8,128)(2,1)} %all-gather.11.cloned.1.call-done, bf16[384,4096]{1,0:T(8,128)(2,1)S(1)} %copy-done.2, f32[384]{0:T(512)} %add_rsqrt_fusion), kind=kOutput, calls=%fused_computation.23 | convolution fusion | flops 4837146624 | bytes 16910336 | tf_op jit(solution)/shard_map/dot_general | solution.py:97
  345.5 3.1 collective-permute-start.1
  348.6 1.7 copy.17
  350.3 11.7 %collective-permute-done.1 = bf16[6,3,512]{0,2,1:T(8,128)(2,1)S(1)} collective-permute-done((bf16[6,3,512]{0,2,1:T(8,128)(2,1)S(1)}, bf16[6,3,512]{0,2,1:T(8,128)(2,1)S(1)}, u32[]{:S(2)}, u32[]{:S(2)}) %collective-permute-start.1) | collective-permute-done | bytes 18464 | tf_op jit(solution)/shard_map/ppermute | solution.py:15
  362.9 5.7 %fusion.13 = f32[384,3,512]{0,2,1:T(8,128)S(1)} fusion(f32[390,3,512]{0,2,1:T(8,128)S(1)} %maximum_convert_fusion, f32[3,512]{1,0:T(4,128)S(1)} %get-tuple-element.270, f32[3,512]{1,0:T(4,128)S(1)} %get-tuple-element.271, f32[3,512]{1,0:T(4,128)S(1)} %get-tuple-element.272, f32[3,512]{1,0:T(4,128)S(1)} %get-tuple-element.273, ...), kind=kLoop, calls=%fused_computation.26 | loop fusion | flops 11796480 | bytes 18920064 | tf_op jit(solution)/shard_map/add | solution.py:54
  369.1 2.1 collective-permute-start.2
  371.3 8.3 %collective-permute-done.2 = bf16[127,512]{0,1:T(8,128)(2,1)S(1)} collective-permute-done((bf16[127,512]{0,1:T(8,128)(2,1)S(1)}, bf16[127,512]{0,1:T(8,128)(2,1)S(1)}, u32[]{:S(2)}, u32[]{:S(2)}) %collective-permute-start.2) | collective-permute-done | bytes 130080 | tf_op jit(solution)/shard_map/ppermute | solution.py:15
  380.3 10.9 %fusion.235 = f32[384,512]{0,1:T(8,128)S(1)} fusion(f32[511,512]{0,1:T(8,128)S(1)} %maximum_convert_fusion.1, f32[512]{0:T(512)S(1)} %bitcast.277, f32[512]{0:T(512)S(1)} %bitcast.278, f32[512]{0:T(512)S(1)} %bitcast.279, f32[512]{0:T(512)S(1)} %bitcast.280, f32[512]{0:T(512)S(1)} %bitcast.281, f32[512]{0:T(512)S(1)} %bitcast.282, f32[512]{0:T(512)S(1)} %bitcast.283, ...), kind=kLoop, calls=%fused_computation.354 | loop fusion | flops 18677760 | bytes 26030080 | tf_op jit(solution)/shard_map/add | solution.py:54
  391.4 32.6 %fusion.317 = bf16[384,512]{0,1:T(8,128)(2,1)S(1)} fusion(f32[511,512]{0,1:T(8,128)S(1)} %maximum_convert_fusion.1, f32[384,512]{0,1:T(8,128)S(1)} %fusion.235, f32[512]{0:T(512)S(1)} %bitcast.168, f32[512]{0:T(512)S(1)} %bitcast.263, f32[512]{0:T(512)S(1)} %bitcast.208, f32[512]{0:T(512)S(1)} %bitcast.209, f32[512]{0:T(512)S(1)} %bitcast.210, ...), kind=kLoop, calls=%fused_computation.66.clone.clone.2 | loop fusion | flops 57016320 | bytes 77697024 | tf_op jit(solution)/shard_map/dot_general | solution.py:117
  424.0 5.7 %convolution_convert_fusion = bf16[384,4096]{1,0:T(8,128)(2,1)} fusion(bf16[4096,2048]{1,0:T(8,128)(2,1)} %all-gather.11.cloned.1.call-done, bf16[384,512]{0,1:T(8,128)(2,1)S(1)} %fusion.317), kind=kOutput, calls=%fused_computation.12 | convolution fusion | flops 1612185600 | bytes 7733248 | tf_op jit(solution)/shard_map/dot_general | solution.py:117
  429.7 70.2 %reduce-scatter.2.cloned.1.call-done = bf16[384,1024]{1,0:T(8,128)(2,1)} async-done(((bf16[384,4096]{1,0:T(8,128)(2,1)}), bf16[384,1024]{1,0:T(8,128)(2,1)}) %reduce-scatter.2.cloned.1.call-update) | async-done | bytes 786448 | tf_op jit(solution)/shard_map/reduce_scatter | solution.py:123
  499.9 1.4 add_convert_fusion
  501.4 1.5 collective-permute-start.3
  504.1 10.3 %collective-permute-done.3 = bf16[256,1024]{1,0:T(8,128)(2,1)S(1)} collective-permute-done((bf16[256,1024]{1,0:T(8,128)(2,1)S(1)}, bf16[256,1024]{1,0:T(8,128)(2,1)S(1)}, u32[]{:S(2)}, u32[]{:S(2)}) %collective-permute-start.3) | collective-permute-done | bytes 524320 | tf_op jit(solution)/shard_map/ppermute | solution.py:21
  514.7 9.3 %fusion.31 = bf16[640,1024]{1,0:T(8,128)(2,1)} fusion(s32[]{:T(128)S(6)} %min.20, bf16[1280,1024]{1,0:T(8,128)(2,1)S(1)} %broadcast.1506, s32[]{:T(128)S(6)} %min.21, bf16[256,1024]{1,0:T(8,128)(2,1)S(1)} %collective-permute-done.3, bf16[384,1024]{1,0:T(8,128)(2,1)S(1)} %add_convert_fusion, pred[640]{0:T(1024)(128)(4,1)S(1)} %get-tuple-element.276, ...), kind=kLoop, calls=%fused_computation.53 | loop fusion | flops 10485760 | bytes 5244809 | tf_op jit(solution)/shard_map/jit(_where)/select_n | solution.py:142
  (152 shorter events, 9.3 us)
Async XLA Ops:
  6.5 30.3 %copy-start.1 = (bf16[640,1024]{1,0:T(8,128)(2,1)S(1)}, bf16[640,1024]{1,0:T(8,128)(2,1)}, u32[]{:S(2)}) copy-start(bf16[640,1024]{1,0:T(8,128)(2,1)} %param.7) | copy-start | bytes 3932164
  6.5 31.0 %copy-start.54 = (s32[64]{0:T(128)S(1)}, s32[64]{0:T(128)}, u32[]{:S(2)}) copy-start(s32[64]{0:T(128)} %param.8) | copy-start | bytes 772
  6.5 30.2 %all-gather.7.cloned.1.call-start = ((), (), s32[]{:S(2)}) async-start(), calls=%async_computation.2 | async-start | bytes 1310720 | tf_op jit(solution)/shard_map/all_gather | solution.py:94
  9.2 115.6 %all-gather.9.cloned.1.call-start = ((), (), s32[]{:S(2)}) async-start(), calls=%async_computation.3 | async-start | bytes 5242880 | tf_op jit(solution)/shard_map/all_gather | solution.py:94
  36.8 145.5 %all-gather.5.cloned.1.call-start = ((), (), s32[]{:S(2)}) async-start(), calls=%async_computation.1 | async-start | bytes 3932160 | tf_op jit(solution)/shard_map/all_gather | solution.py:82
  36.9 10.8 %collective-permute-start = (bf16[256,1024]{1,0:T(8,128)(2,1)S(1)}, bf16[256,1024]{1,0:T(8,128)(2,1)S(1)}, u32[]{:S(2)}, u32[]{:S(2)}) collective-permute-start(bf16[256,1024]{1,0:T(8,128)(2,1)S(1)} %constant_dynamic-slice_fusion.1), channel_id=1, source_target_pairs={{0,4},{4,0},{8,12},{12,8},{16,20},{20,16},{24,28},{28,24},{32,36},... | collective-permute-start | bytes 1572872 | tf_op jit(solution)/shard_map/ppermute | solution.py:21
  53.1 71.8 %copy-start.53 = (s32[32]{0:T(128)S(1)}, s32[32]{0:T(128)}, u32[]{:S(2)}) copy-start(s32[32]{0:T(128)} %param.9) | copy-start | bytes 388
  53.1 71.9 %copy-start.5 = (f32[7,3,512]{2,0,1:T(8,128)S(1)}, f32[7,3,512]{2,0,1:T(8,128)}, u32[]{:S(2)}) copy-start(f32[7,3,512]{2,0,1:T(8,128)} %param.11) | copy-start | bytes 129028
  53.1 71.9 %copy-start.4 = (f32[128,512]{1,0:T(8,128)S(1)}, f32[128,512]{1,0:T(8,128)}, u32[]{:S(2)}) copy-start(f32[128,512]{1,0:T(8,128)} %param.12) | copy-start | bytes 786436
  53.1 282.9 %all-gather.11.cloned.1.call-start = ((), (), s32[]{:S(2)}) async-start(), calls=%async_computation.4 | async-start | bytes 20971520 | tf_op jit(solution)/shard_map/all_gather | solution.py:94
  124.8 375.1 %reduce-scatter.2.cloned.1.call-start = ((), (), s32[]{:S(2)}) async-start(), calls=%async_computation.5 | async-start | bytes 3932160 | tf_op jit(solution)/shard_map/reduce_scatter | solution.py:123
  182.2 153.8 %copy-start.2 = (bf16[384,4096]{1,0:T(8,128)(2,1)S(1)}, bf16[384,4096]{1,0:T(8,128)(2,1)}, u32[]{:S(2)}) copy-start(bf16[384,4096]{1,0:T(8,128)(2,1)} %all-gather.5.cloned.1.call-done) | copy-start | bytes 9437188
  345.5 16.5 %collective-permute-start.1 = (bf16[6,3,512]{0,2,1:T(8,128)(2,1)S(1)}, bf16[6,3,512]{0,2,1:T(8,128)(2,1)S(1)}, u32[]{:S(2)}, u32[]{:S(2)}) collective-permute-start(bf16[6,3,512]{0,2,1:T(8,128)(2,1)S(1)} %bitcast.164), channel_id=1, source_target_pairs={{0,4},{4,8},{8,12},{12,16},{16,20},{20,24},{24,28},{28,32},{32,36}... | collective-permute-start | bytes 55304 | tf_op jit(solution)/shard_map/ppermute | solution.py:15
  368.7 11.2 %copy-start.16 = (f32[1,512]{1,0:T(1,128)S(1)}, f32[1,512]{1,0:T(1,128)}, u32[]{:S(2)}) copy-start(f32[1,512]{1,0:T(1,128)} %get-tuple-element.120) | copy-start | bytes 6148
  368.7 11.2 %copy-start.17 = (f32[1,512]{1,0:T(1,128)S(1)}, f32[1,512]{1,0:T(1,128)}, u32[]{:S(2)}) copy-start(f32[1,512]{1,0:T(1,128)} %get-tuple-element.121) | copy-start | bytes 6148
  368.7 11.2 %copy-start.18 = (f32[1,512]{1,0:T(1,128)S(1)}, f32[1,512]{1,0:T(1,128)}, u32[]{:S(2)}) copy-start(f32[1,512]{1,0:T(1,128)} %get-tuple-element.122) | copy-start | bytes 6148
  368.7 11.2 %copy-start.19 = (f32[1,512]{1,0:T(1,128)S(1)}, f32[1,512]{1,0:T(1,128)}, u32[]{:S(2)}) copy-start(f32[1,512]{1,0:T(1,128)} %get-tuple-element.123) | copy-start | bytes 6148
  368.8 11.2 %copy-start.20 = (f32[1,512]{1,0:T(1,128)S(1)}, f32[1,512]{1,0:T(1,128)}, u32[]{:S(2)}) copy-start(f32[1,512]{1,0:T(1,128)} %get-tuple-element.124) | copy-start | bytes 6148
  368.8 11.2 %copy-start.21 = (f32[1,512]{1,0:T(1,128)S(1)}, f32[1,512]{1,0:T(1,128)}, u32[]{:S(2)}) copy-start(f32[1,512]{1,0:T(1,128)} %get-tuple-element.125) | copy-start | bytes 6148
  368.8 11.2 %copy-start.22 = (f32[1,512]{1,0:T(1,128)S(1)}, f32[1,512]{1,0:T(1,128)}, u32[]{:S(2)}) copy-start(f32[1,512]{1,0:T(1,128)} %get-tuple-element.126) | copy-start | bytes 6148
  368.8 11.2 %copy-start.23 = (f32[1,512]{1,0:T(1,128)S(1)}, f32[1,512]{1,0:T(1,128)}, u32[]{:S(2)}) copy-start(f32[1,512]{1,0:T(1,128)} %get-tuple-element.127) | copy-start | bytes 6148
  369.1 10.5 %collective-permute-start.2 = (bf16[127,512]{0,1:T(8,128)(2,1)S(1)}, bf16[127,512]{0,1:T(8,128)(2,1)S(1)}, u32[]{:S(2)}, u32[]{:S(2)}) collective-permute-start(bf16[127,512]{0,1:T(8,128)(2,1)S(1)} %slice_bitcast_fusion.1), channel_id=1, source_target_pairs={{0,4},{4,8},{8,12},{12,16},{16,20},{20,24},{24,28},{28,32},{32,36}... | collective-permute-start | bytes 390152 | tf_op jit(solution)/shard_map/ppermute | solution.py:15
  429.7 70.3 %copy-start = (bf16[384,1024]{1,0:T(8,128)(2,1)S(1)}, bf16[384,1024]{1,0:T(8,128)(2,1)}, u32[]{:S(2)}) copy-start(bf16[384,1024]{1,0:T(8,128)(2,1)} %fusion.38) | copy-start | bytes 2359300
  501.4 12.9 %collective-permute-start.3 = (bf16[256,1024]{1,0:T(8,128)(2,1)S(1)}, bf16[256,1024]{1,0:T(8,128)(2,1)S(1)}, u32[]{:S(2)}, u32[]{:S(2)}) collective-permute-start(bf16[256,1024]{1,0:T(8,128)(2,1)S(1)} %constant_dynamic-slice_fusion), channel_id=1, source_target_pairs={{0,4},{4,0},{8,12},{12,8},{16,20},{20,16},{24,28},{28,24},{32,36},... | collective-permute-start | bytes 1572872 | tf_op jit(solution)/shard_map/ppermute | solution.py:21
  (40 other events, 364.0 us)
Sparse Core Ops, SparseCore 0:
  9.3 27.4 all-gather.6
  38.6 86.1 all-gather.8
  126.6 55.5 all-gather.4
  183.9 152.1 all-gather.10
  429.8 70.0 reduce-scatter.1

commit v4 on v3

--- a/solution.py
+++ b/solution.py
@@ -37,6 +37,31 @@
         shifted(first, first_off, count),
         shifted(second, second_off, count),
     )
+
+
+def tp_blocks_gather(block, axis):
+    peers = lax.axis_size(axis)
+    me = lax.axis_index(axis)
+    got = [block]
+    for by in range(1, peers):
+        got.append(lax.ppermute(block, axis, [(i, (i + by) % peers) for i in range(peers)]))
+    stacked = jnp.stack(got)
+    order = (me - jnp.arange(peers, dtype=jnp.int32)) % peers
+    ordered = jnp.take(stacked, order, axis=0)
+    return jnp.moveaxis(ordered, 0, 1).reshape(block.shape[0], peers * block.shape[1])
+
+
+def tp_blocks_sum(full, axis):
+    peers = lax.axis_size(axis)
+    me = lax.axis_index(axis)
+    width = full.shape[1] // peers
+    blocks = full.reshape(full.shape[0], peers, width)
+    total = lax.dynamic_index_in_dim(blocks, me, 1, keepdims=False).astype(jnp.float32)
+    for by in range(1, peers):
+        sent = lax.dynamic_index_in_dim(blocks, (me + by) % peers, 1, keepdims=False)
+        got = lax.ppermute(sent, axis, [(i, (i + by) % peers) for i in range(peers)])
+        total = total + got.astype(jnp.float32)
+    return total
 
 
 def genome_start(positions, genome_starts):
@@ -79,7 +104,7 @@
         return source[share - count :]
 
     gstart = genome_start(positions, genome_starts)
-    all_feats = lax.all_gather(x_own, TP, axis=1, tiled=True)
+    all_feats = tp_blocks_gather(x_own, TP)
     widened = all_feats.astype(jnp.float32)
     normed = (
         widened * lax.rsqrt(jnp.mean(widened * widened, axis=1, keepdims=True) + 1e-06)
@@ -120,9 +145,7 @@
         (((1,), (1,)), ((), ())),
         preferred_element_type=jnp.float32,
     )
-    branch_out = lax.psum_scatter(
-        partial_out.astype(jnp.bfloat16), TP, scatter_dimension=1, tiled=True
-    ).astype(jnp.float32)
+    branch_out = tp_blocks_sum(partial_out.astype(jnp.bfloat16), TP)
     result = (x_own.astype(jnp.float32) + branch_out).astype(jnp.bfloat16)
 
     back = lax.dynamic_slice_in_dim(result, (1 - parity) * (share - window), window, 0)

time: 532 us -> 495 us (0.930)
  waiting for transfers between devices: 412 us -> 327 us
  local copies, waits for them, and re-layouts: 7.65 us -> 31.7 us
  starting transfers between devices: 7.45 us -> 22.6 us
  other arithmetic: 73.5 us -> 83 us
    ppermute x0 -> x6, waiting for transfers between devices: none -> 119 us  [the longest x3 63.8 us: tp_blocks_sum(): lax.ppermute(sent, axis, [(i, (i + by) % peers) for i in range(peers)])]
    all_gather x3, waiting for transfers between devices: 250 us -> 172 us  [body(): both_rows = lax.all_gather(both_rows, part, axis=0, tiled=True)]
    reduce_scatter x1 -> x0, waiting for transfers between devices: 70.2 us -> none  [body(): lax.psum_scatter(partial_out.astype(jnp.bfloat16), TP, scatter_dimension=...]
    all_gather x1 -> x0, waiting for transfers between devices: 53 us -> none  [body(): all_feats = lax.all_gather(x_own, TP, axis=1, tiled=True)]
    ppermute x0 -> x6, starting transfers between devices: none -> 15.9 us  [the longest x3 8.91 us: tp_blocks_sum(): lax.ppermute(sent, axis, [(i, (i + by) % peers) for i in range(peers)])]
    dynamic_slice x0 -> x1, local copies, waits for them, and re-layouts: none -> 7.36 us  [tp_blocks_sum(): lax.dynamic_index_in_dim(blocks, me, 1, keepdims=False).astype(jnp.float32)]
    convert_element_type x0 -> x2, other arithmetic: none -> 7.16 us  [the longest x1 3.82 us: body(): widened = all_feats.astype(jnp.float32)]
    convert_element_type x0 -> x1, local copies, waits for them, and re-layouts: none -> 6.62 us  [body(): widened = all_feats.astype(jnp.float32)]
  transfers between devices with their start and end apart: 9 -> 13, of which waited for: 9 -> 13; matrix products, arithmetic and copies ran while one was open for 3% -> 7% of each run, Pallas kernels for 0% -> 0%
where the time goes in v4:
time: 495 us; the launch traced here: 494 us
  waiting for transfers between devices  327 us (66%)
  other arithmetic  83 us (17%)
  local copies, waits for them, and re-layouts  31.7 us (6%)
  starting transfers between devices  22.6 us (5%)
  between operations  16.1 us (3%)
  matrix products  13.9 us (3%)
    all_gather x3, waiting for transfers between devices, body(): both_rows = lax.all_gather(both_rows, part, axis=0, tiled=True)  172 us
    ppermute x3, waiting for transfers between devices, tp_blocks_sum(): lax.ppermute(sent, axis, [(i, (i + by) % peers) for i in range(peers)])  63.8 us
    ppermute x3, waiting for transfers between devices, tp_blocks_gather(): lax.ppermute(block, axis, [(i, (i + by) % peers) for i in range(peers)])  55 us
    dot_general x1, other arithmetic, body(): lax.dot_general(gated, out_rows, (((1,), (1,)), ((), ())), preferred_elem...  32.6 us
    ppermute x2, waiting for transfers between devices, passed_along(): return lax.ppermute(shard, axis, pairs)  20 us
    add x2, other arithmetic, causal_taps(): summed = summed + jnp.where(in_genome, window * taps[j], jnp.float32(0.0))  17.4 us
    ppermute x2, waiting for transfers between devices, swapped(): return lax.ppermute(shard, axis, pairs)  16.4 us
  transfers between devices with their start and end apart: 13, of which 13 were waited for; matrix products, arithmetic and copies ran while one was open for 7% of the time, Pallas kernels for 0%

profile of v4, /device:TPU:9, one launch (start us, length us, event | category | flops | bytes accessed | tf_op | source)
XLA Modules:
  0.0 494.4 jit_solution(17752059787916481870)
XLA Ops:
  9.1 27.5 %all-gather.4.cloned.1.call-done = bf16[256,2048]{1,0:T(8,128)(2,1)} async-done(((bf16[64,2048]{1,0:T(8,128)(2,1)}), bf16[256,2048]{1,0:T(8,128)(2,1)}) %all-gather.4.cloned.1.call-update) | async-done | bytes 1048592 | tf_op jit(solution)/shard_map/all_gather | solution.py:119
  36.7 88.0 %all-gather.6.cloned.1.call-done = bf16[1024,2048]{1,0:T(8,128)(2,1)} async-done(((bf16[256,2048]{1,0:T(8,128)(2,1)}), bf16[1024,2048]{1,0:T(8,128)(2,1)}) %all-gather.6.cloned.1.call-update) | async-done | bytes 4194320 | tf_op jit(solution)/shard_map/all_gather | solution.py:119
  130.2 7.3 %collective-permute-done = bf16[256,1024]{1,0:T(8,128)(2,1)S(1)} collective-permute-done((bf16[256,1024]{1,0:T(8,128)(2,1)S(1)}, bf16[256,1024]{1,0:T(8,128)(2,1)S(1)}, u32[]{:S(2)}, u32[]{:S(2)}) %collective-permute-start) | collective-permute-done | bytes 524320 | tf_op jit(solution)/shard_map/ppermute | solution.py:21
  137.7 4.4 fusion.38
  142.1 6.1 %collective-permute-start.1 = (bf16[384,1024]{1,0:T(8,128)(2,1)S(1)}, bf16[384,1024]{1,0:T(8,128)(2,1)S(1)}, u32[]{:S(2)}, u32[]{:S(2)}) collective-permute-start(bf16[384,1024]{1,0:T(8,128)(2,1)S(1)} %fusion.38), channel_id=1, source_target_pairs={{0,1},{1,2},{2,3},{3,0},{4,5},{5,6},{6,7},{7,4},{8,9},{9,10},{10,1... | collective-permute-start | bytes 2359304 | tf_op jit(solution)/shard_map/ppermute | solution.py:47
  151.9 20.7 %collective-permute-done.1 = bf16[384,1024]{1,0:T(8,128)(2,1)S(1)} collective-permute-done((bf16[384,1024]{1,0:T(8,128)(2,1)S(1)}, bf16[384,1024]{1,0:T(8,128)(2,1)S(1)}, u32[]{:S(2)}, u32[]{:S(2)}) %collective-permute-start.1) | collective-permute-done | bytes 786464 | tf_op jit(solution)/shard_map/ppermute | solution.py:47
  172.6 31.2 %collective-permute-done.2 = bf16[384,1024]{1,0:T(8,128)(2,1)S(1)} collective-permute-done((bf16[384,1024]{1,0:T(8,128)(2,1)S(1)}, bf16[384,1024]{1,0:T(8,128)(2,1)S(1)}, u32[]{:S(2)}, u32[]{:S(2)}) %collective-permute-start.2) | collective-permute-done | bytes 786464 | tf_op jit(solution)/shard_map/ppermute | solution.py:47
  211.5 3.8 convert_bitcast_fusion
  215.3 6.6 %copy.30 = f32[384,4,1024]{0,2,1:T(8,128)} copy(f32[384,4,1024]{2,0,1:T(8,128)} %convert_bitcast_fusion) | data formatting | bytes 12582912 | tf_op jit(solution)/shard_map/convert_element_type | solution.py:108
  226.9 56.4 %all-gather.8.cloned.1.call-done = bf16[4096,2048]{1,0:T(8,128)(2,1)} async-done(((bf16[1024,2048]{1,0:T(8,128)(2,1)}), bf16[4096,2048]{1,0:T(8,128)(2,1)}) %all-gather.8.cloned.1.call-update) | async-done | bytes 16777232 | tf_op jit(solution)/shard_map/all_gather | solution.py:119
  283.3 8.2 %fusion.5 = bf16[384,1536]{1,0:T(8,128)(2,1)S(1)} fusion(bf16[384,4096]{0,1:T(8,128)(2,1)S(1)} %fusion.3, bf16[4096,2048]{1,0:T(8,128)(2,1)} %all-gather.8.cloned.1.call-done), kind=kOutput, calls=%fused_computation.26 | convolution fusion | flops 4832428032 | bytes 16908288 | tf_op jit(solution)/shard_map/dot_general | solution.py:122
  297.7 11.6 %collective-permute-done.4 = bf16[6,3,512]{0,2,1:T(8,128)(2,1)S(1)} collective-permute-done((bf16[6,3,512]{0,2,1:T(8,128)(2,1)S(1)}, bf16[6,3,512]{0,2,1:T(8,128)(2,1)S(1)}, u32[]{:S(2)}, u32[]{:S(2)}) %collective-permute-start.4) | collective-permute-done | bytes 18464 | tf_op jit(solution)/shard_map/ppermute | solution.py:15
  310.2 5.7 %fusion.9 = f32[384,3,512]{0,2,1:T(8,128)S(1)} fusion(f32[390,3,512]{0,2,1:T(8,128)S(1)} %maximum_convert_fusion, f32[3,512]{1,0:T(4,128)S(1)} %get-tuple-element.274, f32[3,512]{1,0:T(4,128)S(1)} %get-tuple-element.275, f32[3,512]{1,0:T(4,128)S(1)} %get-tuple-element.276, f32[3,512]{1,0:T(4,128)S(1)} %get-tuple-element.277, ...), kind=kLoop, calls=%fused_computation.29 | loop fusion | flops 11796480 | bytes 18920064 | tf_op jit(solution)/shard_map/add | solution.py:79
  318.6 8.3 %collective-permute-done.5 = bf16[127,512]{0,1:T(8,128)(2,1)S(1)} collective-permute-done((bf16[127,512]{0,1:T(8,128)(2,1)S(1)}, bf16[127,512]{0,1:T(8,128)(2,1)S(1)}, u32[]{:S(2)}, u32[]{:S(2)}) %collective-permute-start.5) | collective-permute-done | bytes 130080 | tf_op jit(solution)/shard_map/ppermute | solution.py:15
  327.6 11.7 %fusion.235 = f32[384,512]{0,1:T(8,128)S(1)} fusion(f32[511,512]{0,1:T(8,128)S(1)} %maximum_convert_fusion.1, f32[512]{0:T(512)} %bitcast.327, f32[512]{0:T(512)S(1)} %bitcast.309, f32[512]{0:T(512)S(1)} %bitcast.310, f32[512]{0:T(512)S(1)} %bitcast.311, f32[512]{0:T(512)S(1)} %bitcast.312, f32[512]{0:T(512)S(1)} %bitcast.313, f32[512]{0:T(512)S(1)} %bitcast.314, ...), kind=kLoop, calls=%fused_computation.361 | loop fusion | flops 18677760 | bytes 26030080 | tf_op jit(solution)/shard_map/add | solution.py:79
  339.4 32.6 %fusion.321 = bf16[384,512]{0,1:T(8,128)(2,1)S(1)} fusion(f32[511,512]{0,1:T(8,128)S(1)} %maximum_convert_fusion.1, f32[384,512]{0,1:T(8,128)S(1)} %fusion.235, f32[512]{0:T(512)S(1)} %bitcast.200, f32[512]{0:T(512)S(1)} %bitcast.201, f32[512]{0:T(512)S(1)} %bitcast.259, f32[512]{0:T(512)S(1)} %bitcast.260, f32[512]{0:T(512)S(1)} %bitcast.261, ...), kind=kLoop, calls=%fused_computation.73.clone.clone.2 | loop fusion | flops 57016320 | bytes 77697024 | tf_op jit(solution)/shard_map/dot_general | solution.py:142
  372.0 5.7 %convolution_convert_fusion = bf16[384,4096]{1,0:T(8,128)(2,1)} fusion(bf16[4096,2048]{1,0:T(8,128)(2,1)} %all-gather.8.cloned.1.call-done, bf16[384,512]{0,1:T(8,128)(2,1)S(1)} %fusion.321), kind=kOutput, calls=%fused_computation.14 | convolution fusion | flops 1612185600 | bytes 7733248 | tf_op jit(solution)/shard_map/dot_general | solution.py:142
  377.7 4.8 reshape.1060
  382.5 7.4 %constant_dynamic-slice_fusion.4 = (bf16[384,1,1024]{2,1,0:T(2,128)(2,1)}, bf16[384,1,1024]{2,1,0:T(2,128)(2,1)S(1)}, bf16[384,1,1024]{2,1,0:T(2,128)(2,1)S(1)}, bf16[384,1,1024]{2,1,0:T(2,128)(2,1)S(1)}) fusion(bf16[384,4,1024]{2,1,0:T(4,128)(2,1)S(1)} %reshape.1060, s32[]{:T(128)S(6)} %select_n.686, s32[]{:T(128)S(6)} %select_n.690, s32[]{:T(128)S(6)} %select_n.688, ...), kind=kLoop, calls=%fused_computation.476 | loop fusion | bytes 6291472 | tf_op jit(solution)/shard_map/jit(dynamic_index_in_dim)/dynamic_slice | solution.py:59
  390.1 8.5 %collective-permute-start.6 = (bf16[384,1024]{1,0:T(8,128)(2,1)S(1)}, bf16[384,1024]{1,0:T(8,128)(2,1)}, u32[]{:S(2)}, u32[]{:S(2)}) collective-permute-start(bf16[384,1024]{1,0:T(8,128)(2,1)S(1)} %bitcast.195), channel_id=1, source_target_pairs={{0,1},{1,2},{2,3},{3,0},{4,5},{5,6},{6,7},{7,4},{8,9},{9,10},{10,1... | collective-permute-start | bytes 2359304 | tf_op jit(solution)/shard_map/ppermute | solution.py:62
  401.4 42.6 %collective-permute-done.6 = bf16[384,1024]{1,0:T(8,128)(2,1)} collective-permute-done((bf16[384,1024]{1,0:T(8,128)(2,1)S(1)}, bf16[384,1024]{1,0:T(8,128)(2,1)}, u32[]{:S(2)}, u32[]{:S(2)}) %collective-permute-start.6) | collective-permute-done | bytes 786464 | tf_op jit(solution)/shard_map/ppermute | solution.py:62
  444.0 21.0 %collective-permute-done.7 = bf16[384,1024]{1,0:T(8,128)(2,1)} collective-permute-done((bf16[384,1024]{1,0:T(8,128)(2,1)}, bf16[384,1024]{1,0:T(8,128)(2,1)}, u32[]{:S(2)}, u32[]{:S(2)}) %collective-permute-start.7) | collective-permute-done | bytes 786464 | tf_op jit(solution)/shard_map/ppermute | solution.py:62
  469.1 9.1 %collective-permute-done.9 = bf16[256,1024]{1,0:T(8,128)(2,1)S(1)} collective-permute-done((bf16[256,1024]{1,0:T(8,128)(2,1)S(1)}, bf16[256,1024]{1,0:T(8,128)(2,1)S(1)}, u32[]{:S(2)}, u32[]{:S(2)}) %collective-permute-start.9) | collective-permute-done | bytes 524320 | tf_op jit(solution)/shard_map/ppermute | solution.py:21
  478.6 9.3 %fusion.31 = bf16[640,1024]{1,0:T(8,128)(2,1)} fusion(s32[]{:T(128)S(6)} %min.20, bf16[1280,1024]{1,0:T(8,128)(2,1)S(1)} %broadcast.1609, s32[]{:T(128)S(6)} %min.21, bf16[256,1024]{1,0:T(8,128)(2,1)S(1)} %collective-permute-done.9, bf16[384,1024]{1,0:T(8,128)(2,1)S(1)} %fusion.24, pred[640]{0:T(1024)(128)(4,1)S(1)} %get-tuple-element.280, ...), kind=kLoop, calls=%fused_computation.60 | loop fusion | flops 10485760 | bytes 5244809 | tf_op jit(solution)/shard_map/jit(_where)/select_n | solution.py:165
  (173 shorter events, 39.7 us)
Async XLA Ops:
  6.5 30.1 %all-gather.4.cloned.1.call-start = ((), (), s32[]{:S(2)}) async-start(), calls=%async_computation | async-start | bytes 1310720 | tf_op jit(solution)/shard_map/all_gather | solution.py:119
  9.1 115.6 %all-gather.6.cloned.1.call-start = ((), (), s32[]{:S(2)}) async-start(), calls=%async_computation.1 | async-start | bytes 5242880 | tf_op jit(solution)/shard_map/all_gather | solution.py:119
  36.7 88.1 %copy-start.3 = (bf16[640,1024]{1,0:T(8,128)(2,1)S(1)}, bf16[640,1024]{1,0:T(8,128)(2,1)}, u32[]{:S(2)}) copy-start(bf16[640,1024]{1,0:T(8,128)(2,1)} %param.7) | copy-start | bytes 3932164
  36.7 246.6 %all-gather.8.cloned.1.call-start = ((), (), s32[]{:S(2)}) async-start(), calls=%async_computation.2 | async-start | bytes 20971520 | tf_op jit(solution)/shard_map/all_gather | solution.py:119
  124.8 12.7 %collective-permute-start = (bf16[256,1024]{1,0:T(8,128)(2,1)S(1)}, bf16[256,1024]{1,0:T(8,128)(2,1)S(1)}, u32[]{:S(2)}, u32[]{:S(2)}) collective-permute-start(bf16[256,1024]{1,0:T(8,128)(2,1)S(1)} %constant_dynamic-slice_fusion.5), channel_id=1, source_target_pairs={{0,4},{4,0},{8,12},{12,8},{16,20},{20,16},{24,28},{28,24},{32,36},... | collective-permute-start | bytes 1572872 | tf_op jit(solution)/shard_map/ppermute | solution.py:21
  142.1 64.8 %copy-start = (bf16[384,1024]{1,0:T(8,128)(2,1)}, bf16[384,1024]{1,0:T(8,128)(2,1)S(1)}, u32[]{:S(2)}) copy-start(bf16[384,1024]{1,0:T(8,128)(2,1)S(1)} %fusion.38) | copy-start | bytes 2359300
  142.1 30.5 %collective-permute-start.1 = (bf16[384,1024]{1,0:T(8,128)(2,1)S(1)}, bf16[384,1024]{1,0:T(8,128)(2,1)S(1)}, u32[]{:S(2)}, u32[]{:S(2)}) collective-permute-start(bf16[384,1024]{1,0:T(8,128)(2,1)S(1)} %fusion.38), channel_id=1, source_target_pairs={{0,1},{1,2},{2,3},{3,0},{4,5},{5,6},{6,7},{7,4},{8,9},{9,10},{10,1... | collective-permute-start | bytes 2359304 | tf_op jit(solution)/shard_map/ppermute | solution.py:47
  148.2 55.5 %collective-permute-start.2 = (bf16[384,1024]{1,0:T(8,128)(2,1)S(1)}, bf16[384,1024]{1,0:T(8,128)(2,1)S(1)}, u32[]{:S(2)}, u32[]{:S(2)}) collective-permute-start(bf16[384,1024]{1,0:T(8,128)(2,1)S(1)} %fusion.38), channel_id=1, source_target_pairs={{0,2},{1,3},{2,0},{3,1},{4,6},{5,7},{6,4},{7,5},{8,10},{9,11},{10,... | collective-permute-start | bytes 2359304 | tf_op jit(solution)/shard_map/ppermute | solution.py:47
  149.2 57.7 %collective-permute-start.3 = (bf16[384,1024]{1,0:T(8,128)(2,1)S(1)}, bf16[384,1024]{1,0:T(8,128)(2,1)S(1)}, u32[]{:S(2)}, u32[]{:S(2)}) collective-permute-start(bf16[384,1024]{1,0:T(8,128)(2,1)S(1)} %fusion.38), channel_id=1, source_target_pairs={{0,3},{1,0},{2,1},{3,2},{4,7},{5,4},{6,5},{7,6},{8,11},{9,8},{10,9... | collective-permute-start | bytes 2359304 | tf_op jit(solution)/shard_map/ppermute | solution.py:47
  292.8 16.5 %collective-permute-start.4 = (bf16[6,3,512]{0,2,1:T(8,128)(2,1)S(1)}, bf16[6,3,512]{0,2,1:T(8,128)(2,1)S(1)}, u32[]{:S(2)}, u32[]{:S(2)}) collective-permute-start(bf16[6,3,512]{0,2,1:T(8,128)(2,1)S(1)} %bitcast.196), channel_id=1, source_target_pairs={{0,4},{4,8},{8,12},{12,16},{16,20},{20,24},{24,28},{28,32},{32,36}... | collective-permute-start | bytes 55304 | tf_op jit(solution)/shard_map/ppermute | solution.py:15
  316.4 10.5 %collective-permute-start.5 = (bf16[127,512]{0,1:T(8,128)(2,1)S(1)}, bf16[127,512]{0,1:T(8,128)(2,1)S(1)}, u32[]{:S(2)}, u32[]{:S(2)}) collective-permute-start(bf16[127,512]{0,1:T(8,128)(2,1)S(1)} %slice_bitcast_fusion.1), channel_id=1, source_target_pairs={{0,4},{4,8},{8,12},{12,16},{16,20},{20,24},{24,28},{28,32},{32,36}... | collective-permute-start | bytes 390152 | tf_op jit(solution)/shard_map/ppermute | solution.py:15
  327.5 11.8 %copy-start.7 = (f32[1,512]{1,0:T(1,128)S(1)}, f32[1,512]{1,0:T(1,128)}, u32[]{:S(2)}) copy-start(f32[1,512]{1,0:T(1,128)} %get-tuple-element.75) | copy-start | bytes 6148
  327.5 11.8 %copy-start.8 = (f32[1,512]{1,0:T(1,128)S(1)}, f32[1,512]{1,0:T(1,128)}, u32[]{:S(2)}) copy-start(f32[1,512]{1,0:T(1,128)} %get-tuple-element.76) | copy-start | bytes 6148
  327.5 11.8 %copy-start.9 = (f32[1,512]{1,0:T(1,128)S(1)}, f32[1,512]{1,0:T(1,128)}, u32[]{:S(2)}) copy-start(f32[1,512]{1,0:T(1,128)} %get-tuple-element.77) | copy-start | bytes 6148
  327.5 11.8 %copy-start.10 = (f32[1,512]{1,0:T(1,128)S(1)}, f32[1,512]{1,0:T(1,128)}, u32[]{:S(2)}) copy-start(f32[1,512]{1,0:T(1,128)} %get-tuple-element.78) | copy-start | bytes 6148
  327.6 11.8 %copy-start.11 = (f32[1,512]{1,0:T(1,128)S(1)}, f32[1,512]{1,0:T(1,128)}, u32[]{:S(2)}) copy-start(f32[1,512]{1,0:T(1,128)} %get-tuple-element.79) | copy-start | bytes 6148
  327.6 11.8 %copy-start.12 = (f32[1,512]{1,0:T(1,128)S(1)}, f32[1,512]{1,0:T(1,128)}, u32[]{:S(2)}) copy-start(f32[1,512]{1,0:T(1,128)} %get-tuple-element.80) | copy-start | bytes 6148
  327.6 11.8 %copy-start.13 = (f32[1,512]{1,0:T(1,128)S(1)}, f32[1,512]{1,0:T(1,128)}, u32[]{:S(2)}) copy-start(f32[1,512]{1,0:T(1,128)} %get-tuple-element.81) | copy-start | bytes 6148
  390.1 53.9 %collective-permute-start.6 = (bf16[384,1024]{1,0:T(8,128)(2,1)S(1)}, bf16[384,1024]{1,0:T(8,128)(2,1)}, u32[]{:S(2)}, u32[]{:S(2)}) collective-permute-start(bf16[384,1024]{1,0:T(8,128)(2,1)S(1)} %bitcast.195), channel_id=1, source_target_pairs={{0,1},{1,2},{2,3},{3,0},{4,5},{5,6},{6,7},{7,4},{8,9},{9,10},{10,1... | collective-permute-start | bytes 2359304 | tf_op jit(solution)/shard_map/ppermute | solution.py:62
  398.6 66.6 %copy-start.1 = (bf16[384,1024]{1,0:T(8,128)(2,1)S(1)}, bf16[384,1024]{1,0:T(8,128)(2,1)}, u32[]{:S(2)}) copy-start(bf16[384,1024]{1,0:T(8,128)(2,1)} %copy-done) | copy-start | bytes 2359300
  398.6 66.6 %copy-start.2 = (bf16[384,1,1024]{2,1,0:T(2,128)(2,1)S(1)}, bf16[384,1,1024]{2,1,0:T(2,128)(2,1)}, u32[]{:S(2)}) copy-start(bf16[384,1,1024]{2,1,0:T(2,128)(2,1)} %get-tuple-element.5) | copy-start | bytes 2359300
  399.8 65.3 %collective-permute-start.7 = (bf16[384,1024]{1,0:T(8,128)(2,1)}, bf16[384,1024]{1,0:T(8,128)(2,1)}, u32[]{:S(2)}, u32[]{:S(2)}) collective-permute-start(bf16[384,1024]{1,0:T(8,128)(2,1)} %bitcast.186), channel_id=1, source_target_pairs={{0,2},{1,3},{2,0},{3,1},{4,6},{5,7},{6,4},{7,5},{8,10},{9,11},{10,... | collective-permute-start | bytes 2359304 | tf_op jit(solution)/shard_map/ppermute | solution.py:62
  400.9 64.2 %collective-permute-start.8 = (bf16[384,1024]{1,0:T(8,128)(2,1)}, bf16[384,1024]{1,0:T(8,128)(2,1)}, u32[]{:S(2)}, u32[]{:S(2)}) collective-permute-start(bf16[384,1024]{1,0:T(8,128)(2,1)} %bitcast.185), channel_id=1, source_target_pairs={{0,3},{1,0},{2,1},{3,2},{4,7},{5,4},{6,5},{7,6},{8,11},{9,8},{10,9... | collective-permute-start | bytes 2359304 | tf_op jit(solution)/shard_map/ppermute | solution.py:62
  467.7 10.5 %collective-permute-start.9 = (bf16[256,1024]{1,0:T(8,128)(2,1)S(1)}, bf16[256,1024]{1,0:T(8,128)(2,1)S(1)}, u32[]{:S(2)}, u32[]{:S(2)}) collective-permute-start(bf16[256,1024]{1,0:T(8,128)(2,1)S(1)} %constant_dynamic-slice_fusion), channel_id=1, source_target_pairs={{0,4},{4,0},{8,12},{12,8},{16,20},{20,16},{24,28},{28,24},{32,36},... | collective-permute-start | bytes 1572872 | tf_op jit(solution)/shard_map/ppermute | solution.py:21
  (45 other events, 390.2 us)
Sparse Core Ops, SparseCore 0:
  9.2 27.4 all-gather.3
  38.5 86.1 all-gather.5
  126.5 156.7 all-gather.7

commit v5 on v4

--- a/solution.py
+++ b/solution.py
@@ -7,6 +7,7 @@
 PAIR_BLOCKS = 6
 CTX = ("y", "zl", "x")
 TP = ("zh", "core")
+GATHER_ORDER = ("zl", "x", "y")
 
 
 def passed_along(shard, axis, by):
@@ -115,10 +116,22 @@
     local_in = in_weight.reshape(in_weight.shape[0], branches * chans)
     both = jnp.concatenate([local_in, out_weight.T], axis=1)
     both_rows = both
-    for part in reversed(CTX):
+    for part in GATHER_ORDER:
         both_rows = lax.all_gather(both_rows, part, axis=0, tiled=True)
+    ny, nz, nx = (lax.axis_size(a) for a in CTX)
+    block = in_weight.shape[0]
     flat = both_rows[:, : branches * chans]
-    out_rows = both_rows[:, branches * chans :]
+    normed = (
+        normed.reshape(row_count, ny, nz, nx, block)
+        .transpose(0, 1, 3, 2, 4)
+        .reshape(row_count, ny * nz * nx * block)
+    )
+    out_rows = (
+        both_rows[:, branches * chans :]
+        .reshape(ny, nx, nz, block, -1)
+        .transpose(0, 2, 1, 3, 4)
+        .reshape(ny * nz * nx * block, -1)
+    )
     summed = jnp.dot(normed, flat, preferred_element_type=jnp.float32)
     projected = summed.astype(jnp.bfloat16).reshape(row_count, branches, chans)
     rim_short = passed_along(last_rows(projected, 6), CTX, 1)

time: 495 us -> 465 us (0.939)
  waiting for transfers between devices: 327 us -> 296 us
    all_gather x3, waiting for transfers between devices: 172 us -> 144 us  [body(): both_rows = lax.all_gather(both_rows, part, axis=0, tiled=True)]
  transfers between devices with their start and end apart: 13 -> 13, of which waited for: 13 -> 13; matrix products, arithmetic and copies ran while one was open for 7% -> 8% of each run, Pallas kernels for 0% -> 0%
where the time goes in v5:
time: 465 us
  waiting for transfers between devices  296 us (64%)
  other arithmetic  83.5 us (18%)
  local copies, waits for them, and re-layouts  34.8 us (7%)
  starting transfers between devices  22.5 us (5%)
  between operations  16.2 us (3%)
  matrix products  11.7 us (3%)
    all_gather x3, waiting for transfers between devices, body(): both_rows = lax.all_gather(both_rows, part, axis=0, tiled=True)  144 us
    ppermute x3, waiting for transfers between devices, tp_blocks_sum(): lax.ppermute(sent, axis, [(i, (i + by) % peers) for i in range(peers)])  63.8 us
    ppermute x3, waiting for transfers between devices, tp_blocks_gather(): lax.ppermute(block, axis, [(i, (i + by) % peers) for i in range(peers)])  53.6 us
    dot_general x1, other arithmetic, body(): lax.dot_general(gated, out_rows, (((1,), (1,)), ((), ())), preferred_elem...  32.6 us
    add x2, other arithmetic, causal_taps(): summed = summed + jnp.where(in_genome, window * taps[j], jnp.float32(0.0))  17.4 us
    ppermute x2, waiting for transfers between devices, passed_along(): return lax.ppermute(shard, axis, pairs)  17.3 us
    ppermute x2, waiting for transfers between devices, swapped(): return lax.ppermute(shard, axis, pairs)  17.1 us
    select_n x1, other arithmetic, body(): return jnp.where(live_rows, placed_rows, jnp.zeros_like(placed_rows))  9.32 us
  transfers between devices with their start and end apart: 13, of which 13 were waited for; matrix products, arithmetic and copies ran while one was open for 8% of the time, Pallas kernels for 0%

profile of v5, /device:TPU:9, one launch (start us, length us, event | category | flops | bytes accessed | tf_op | source)
XLA Modules:
  0.0 464.7 jit_solution(6883621436718358072)
XLA Ops:
  9.1 35.8 %all-gather.4.cloned.1.call-done = bf16[256,2048]{1,0:T(8,128)(2,1)} async-done(((bf16[64,2048]{1,0:T(8,128)(2,1)}), bf16[256,2048]{1,0:T(8,128)(2,1)}) %all-gather.4.cloned.1.call-update) | async-done | bytes 1048592 | tf_op jit(solution)/shard_map/all_gather | solution.py:120
  45.0 52.0 %all-gather.6.cloned.1.call-done = bf16[1024,2048]{1,0:T(8,128)(2,1)} async-done(((bf16[256,2048]{1,0:T(8,128)(2,1)}), bf16[1024,2048]{1,0:T(8,128)(2,1)}) %all-gather.6.cloned.1.call-update) | async-done | bytes 4194320 | tf_op jit(solution)/shard_map/all_gather | solution.py:120
  101.9 7.9 %collective-permute-done = bf16[256,1024]{1,0:T(8,128)(2,1)S(1)} collective-permute-done((bf16[256,1024]{1,0:T(8,128)(2,1)S(1)}, bf16[256,1024]{1,0:T(8,128)(2,1)S(1)}, u32[]{:S(2)}, u32[]{:S(2)}) %collective-permute-start) | collective-permute-done | bytes 524320 | tf_op jit(solution)/shard_map/ppermute | solution.py:22
  110.0 4.4 fusion.37
  114.4 7.1 %collective-permute-start.1 = (bf16[384,1024]{1,0:T(8,128)(2,1)S(1)}, bf16[384,1024]{1,0:T(8,128)(2,1)S(1)}, u32[]{:S(2)}, u32[]{:S(2)}) collective-permute-start(bf16[384,1024]{1,0:T(8,128)(2,1)S(1)} %fusion.37), channel_id=1, source_target_pairs={{0,1},{1,2},{2,3},{3,0},{4,5},{5,6},{6,7},{7,4},{8,9},{9,10},{10,1... | collective-permute-start | bytes 2359304 | tf_op jit(solution)/shard_map/ppermute | solution.py:48
  124.8 21.4 %collective-permute-done.1 = bf16[384,1024]{1,0:T(8,128)(2,1)S(1)} collective-permute-done((bf16[384,1024]{1,0:T(8,128)(2,1)S(1)}, bf16[384,1024]{1,0:T(8,128)(2,1)S(1)}, u32[]{:S(2)}, u32[]{:S(2)}) %collective-permute-start.1) | collective-permute-done | bytes 786464 | tf_op jit(solution)/shard_map/ppermute | solution.py:48
  146.2 31.5 %collective-permute-done.2 = bf16[384,1024]{1,0:T(8,128)(2,1)S(1)} collective-permute-done((bf16[384,1024]{1,0:T(8,128)(2,1)S(1)}, bf16[384,1024]{1,0:T(8,128)(2,1)S(1)}, u32[]{:S(2)}, u32[]{:S(2)}) %collective-permute-start.2) | collective-permute-done | bytes 786464 | tf_op jit(solution)/shard_map/ppermute | solution.py:48
  183.0 3.9 convert_bitcast_fusion
  186.9 6.6 %copy.34 = f32[384,4,1024]{0,2,1:T(8,128)} copy(f32[384,4,1024]{2,0,1:T(8,128)} %convert_bitcast_fusion) | data formatting | bytes 12582912 | tf_op jit(solution)/shard_map/convert_element_type | solution.py:109
  195.2 3.7 fusion.3
  199.2 56.6 %all-gather.8.cloned.1.call-done = bf16[4096,2048]{1,0:T(8,128)(2,1)} async-done(((bf16[1024,2048]{1,0:T(8,128)(2,1)}), bf16[4096,2048]{1,0:T(8,128)(2,1)}) %all-gather.8.cloned.1.call-update) | async-done | bytes 16777232 | tf_op jit(solution)/shard_map/all_gather | solution.py:120
  255.8 8.2 %fusion.4 = bf16[384,1536]{1,0:T(8,128)(2,1)S(1)} fusion(bf16[384,4096]{0,1:T(8,128)(2,1)S(1)} %bitcast.199, bf16[4096,2048]{1,0:T(8,128)(2,1)} %all-gather.8.cloned.1.call-done), kind=kOutput, calls=%fused_computation.25 | convolution fusion | flops 4832428032 | bytes 16908288 | tf_op jit(solution)/shard_map/dot_general | solution.py:135
  273.1 8.8 %collective-permute-done.4 = bf16[6,3,512]{0,2,1:T(8,128)(2,1)S(1)} collective-permute-done((bf16[6,3,512]{0,2,1:T(8,128)(2,1)S(1)}, bf16[6,3,512]{0,2,1:T(8,128)(2,1)S(1)}, u32[]{:S(2)}, u32[]{:S(2)}) %collective-permute-start.4) | collective-permute-done | bytes 18464 | tf_op jit(solution)/shard_map/ppermute | solution.py:16
  282.7 5.7 %fusion.8 = f32[384,3,512]{0,2,1:T(8,128)S(1)} fusion(f32[390,3,512]{0,2,1:T(8,128)S(1)} %maximum_convert_fusion, f32[3,512]{1,0:T(4,128)S(1)} %get-tuple-element.274, f32[3,512]{1,0:T(4,128)S(1)} %get-tuple-element.275, f32[3,512]{1,0:T(4,128)S(1)} %get-tuple-element.276, f32[3,512]{1,0:T(4,128)S(1)} %get-tuple-element.277, ...), kind=kLoop, calls=%fused_computation.28 | loop fusion | flops 11796480 | bytes 18920064 | tf_op jit(solution)/shard_map/add | solution.py:80
  290.9 8.5 %collective-permute-done.5 = bf16[127,512]{0,1:T(8,128)(2,1)S(1)} collective-permute-done((bf16[127,512]{0,1:T(8,128)(2,1)S(1)}, bf16[127,512]{0,1:T(8,128)(2,1)S(1)}, u32[]{:S(2)}, u32[]{:S(2)}) %collective-permute-start.5) | collective-permute-done | bytes 130080 | tf_op jit(solution)/shard_map/ppermute | solution.py:16
  300.1 11.7 %fusion.234 = f32[384,512]{0,1:T(8,128)S(1)} fusion(f32[511,512]{0,1:T(8,128)S(1)} %maximum_convert_fusion.1, f32[512]{0:T(512)} %bitcast.336, f32[512]{0:T(512)S(1)} %bitcast.318, f32[512]{0:T(512)S(1)} %bitcast.319, f32[512]{0:T(512)S(1)} %bitcast.320, f32[512]{0:T(512)S(1)} %bitcast.321, f32[512]{0:T(512)S(1)} %bitcast.322, f32[512]{0:T(512)S(1)} %bitcast.323, ...), kind=kLoop, calls=%fused_computation.360 | loop fusion | flops 18677760 | bytes 26030080 | tf_op jit(solution)/shard_map/add | solution.py:80
  311.9 32.6 %fusion.318 = bf16[384,512]{0,1:T(8,128)(2,1)S(1)} fusion(f32[511,512]{0,1:T(8,128)S(1)} %maximum_convert_fusion.1, f32[384,512]{0,1:T(8,128)S(1)} %fusion.234, f32[512]{0:T(512)S(1)} %bitcast.209, f32[512]{0:T(512)S(1)} %bitcast.210, f32[512]{0:T(512)S(1)} %bitcast.268, f32[512]{0:T(512)S(1)} %bitcast.269, f32[512]{0:T(512)S(1)} %bitcast.270, ...), kind=kLoop, calls=%fused_computation.72.clone.clone.1 | loop fusion | flops 57016320 | bytes 77697024 | tf_op jit(solution)/shard_map/dot_general | solution.py:155
  348.0 4.8 %reshape.1079 = bf16[384,4,1024]{2,1,0:T(4,128)(2,1)S(1)} reshape(bf16[384,4096]{1,0:T(8,128)(2,1)} %convolution_convert_fusion) | data formatting | bytes 6291456 | tf_op jit(solution)/shard_map/reshape | solution.py:59
  352.8 7.3 %constant_dynamic-slice_fusion.4 = (bf16[384,1,1024]{2,1,0:T(2,128)(2,1)}, bf16[384,1,1024]{2,1,0:T(2,128)(2,1)S(1)}, bf16[384,1,1024]{2,1,0:T(2,128)(2,1)S(1)}, bf16[384,1,1024]{2,1,0:T(2,128)(2,1)S(1)}) fusion(bf16[384,4,1024]{2,1,0:T(4,128)(2,1)S(1)} %reshape.1079, s32[]{:T(128)S(6)} %select_n.686, s32[]{:T(128)S(6)} %select_n.690, s32[]{:T(128)S(6)} %select_n.688, ...), kind=kLoop, calls=%fused_computation.475 | loop fusion | bytes 6291472 | tf_op jit(solution)/shard_map/jit(dynamic_index_in_dim)/dynamic_slice | solution.py:60
  360.4 8.5 %collective-permute-start.6 = (bf16[384,1024]{1,0:T(8,128)(2,1)S(1)}, bf16[384,1024]{1,0:T(8,128)(2,1)}, u32[]{:S(2)}, u32[]{:S(2)}) collective-permute-start(bf16[384,1024]{1,0:T(8,128)(2,1)S(1)} %bitcast.204), channel_id=1, source_target_pairs={{0,1},{1,2},{2,3},{3,0},{4,5},{5,6},{6,7},{7,4},{8,9},{9,10},{10,1... | collective-permute-start | bytes 2359304 | tf_op jit(solution)/shard_map/ppermute | solution.py:63
  371.7 42.6 %collective-permute-done.6 = bf16[384,1024]{1,0:T(8,128)(2,1)} collective-permute-done((bf16[384,1024]{1,0:T(8,128)(2,1)S(1)}, bf16[384,1024]{1,0:T(8,128)(2,1)}, u32[]{:S(2)}, u32[]{:S(2)}) %collective-permute-start.6) | collective-permute-done | bytes 786464 | tf_op jit(solution)/shard_map/ppermute | solution.py:63
  414.3 21.0 %collective-permute-done.7 = bf16[384,1024]{1,0:T(8,128)(2,1)} collective-permute-done((bf16[384,1024]{1,0:T(8,128)(2,1)}, bf16[384,1024]{1,0:T(8,128)(2,1)}, u32[]{:S(2)}, u32[]{:S(2)}) %collective-permute-start.7) | collective-permute-done | bytes 786464 | tf_op jit(solution)/shard_map/ppermute | solution.py:63
  439.4 9.1 %collective-permute-done.9 = bf16[256,1024]{1,0:T(8,128)(2,1)S(1)} collective-permute-done((bf16[256,1024]{1,0:T(8,128)(2,1)S(1)}, bf16[256,1024]{1,0:T(8,128)(2,1)S(1)}, u32[]{:S(2)}, u32[]{:S(2)}) %collective-permute-start.9) | collective-permute-done | bytes 524320 | tf_op jit(solution)/shard_map/ppermute | solution.py:22
  448.9 9.3 %fusion.30 = bf16[640,1024]{1,0:T(8,128)(2,1)} fusion(s32[]{:T(128)S(6)} %min.20, bf16[1280,1024]{1,0:T(8,128)(2,1)S(1)} %broadcast.1613, s32[]{:T(128)S(6)} %min.21, bf16[256,1024]{1,0:T(8,128)(2,1)S(1)} %collective-permute-done.9, bf16[384,1024]{1,0:T(8,128)(2,1)S(1)} %fusion.23, pred[640]{0:T(1024)(128)(4,1)S(1)} %get-tuple-element.280, ...), kind=kLoop, calls=%fused_computation.59 | loop fusion | flops 10485760 | bytes 5244809 | tf_op jit(solution)/shard_map/jit(_where)/select_n | solution.py:178
  (177 shorter events, 39.5 us)
Async XLA Ops:
  6.5 38.3 %all-gather.4.cloned.1.call-start = ((), (), s32[]{:S(2)}) async-start(), calls=%async_computation | async-start | bytes 1310720 | tf_op jit(solution)/shard_map/all_gather | solution.py:120
  9.1 87.9 %all-gather.6.cloned.1.call-start = ((), (), s32[]{:S(2)}) async-start(), calls=%async_computation.1 | async-start | bytes 5242880 | tf_op jit(solution)/shard_map/all_gather | solution.py:120
  44.9 52.1 %copy-start.3 = (bf16[640,1024]{1,0:T(8,128)(2,1)S(1)}, bf16[640,1024]{1,0:T(8,128)(2,1)}, u32[]{:S(2)}) copy-start(bf16[640,1024]{1,0:T(8,128)(2,1)} %param.7) | copy-start | bytes 3932164
  44.9 210.9 %all-gather.8.cloned.1.call-start = ((), (), s32[]{:S(2)}) async-start(), calls=%async_computation.2 | async-start | bytes 20971520 | tf_op jit(solution)/shard_map/all_gather | solution.py:120
  97.1 12.7 %collective-permute-start = (bf16[256,1024]{1,0:T(8,128)(2,1)S(1)}, bf16[256,1024]{1,0:T(8,128)(2,1)S(1)}, u32[]{:S(2)}, u32[]{:S(2)}) collective-permute-start(bf16[256,1024]{1,0:T(8,128)(2,1)S(1)} %constant_dynamic-slice_fusion.5), channel_id=1, source_target_pairs={{0,4},{4,0},{8,12},{12,8},{16,20},{20,16},{24,28},{28,24},{32,36},... | collective-permute-start | bytes 1572872 | tf_op jit(solution)/shard_map/ppermute | solution.py:22
  114.4 64.0 %copy-start = (bf16[384,1024]{1,0:T(8,128)(2,1)}, bf16[384,1024]{1,0:T(8,128)(2,1)S(1)}, u32[]{:S(2)}) copy-start(bf16[384,1024]{1,0:T(8,128)(2,1)S(1)} %fusion.37) | copy-start | bytes 2359300
  114.4 31.8 %collective-permute-start.1 = (bf16[384,1024]{1,0:T(8,128)(2,1)S(1)}, bf16[384,1024]{1,0:T(8,128)(2,1)S(1)}, u32[]{:S(2)}, u32[]{:S(2)}) collective-permute-start(bf16[384,1024]{1,0:T(8,128)(2,1)S(1)} %fusion.37), channel_id=1, source_target_pairs={{0,1},{1,2},{2,3},{3,0},{4,5},{5,6},{6,7},{7,4},{8,9},{9,10},{10,1... | collective-permute-start | bytes 2359304 | tf_op jit(solution)/shard_map/ppermute | solution.py:48
  121.5 56.2 %collective-permute-start.2 = (bf16[384,1024]{1,0:T(8,128)(2,1)S(1)}, bf16[384,1024]{1,0:T(8,128)(2,1)S(1)}, u32[]{:S(2)}, u32[]{:S(2)}) collective-permute-start(bf16[384,1024]{1,0:T(8,128)(2,1)S(1)} %fusion.37), channel_id=1, source_target_pairs={{0,2},{1,3},{2,0},{3,1},{4,6},{5,7},{6,4},{7,5},{8,10},{9,11},{10,... | collective-permute-start | bytes 2359304 | tf_op jit(solution)/shard_map/ppermute | solution.py:48
  121.5 56.8 %collective-permute-start.3 = (bf16[384,1024]{1,0:T(8,128)(2,1)S(1)}, bf16[384,1024]{1,0:T(8,128)(2,1)S(1)}, u32[]{:S(2)}, u32[]{:S(2)}) collective-permute-start(bf16[384,1024]{1,0:T(8,128)(2,1)S(1)} %fusion.37), channel_id=1, source_target_pairs={{0,3},{1,0},{2,1},{3,2},{4,7},{5,4},{6,5},{7,6},{8,11},{9,8},{10,9... | collective-permute-start | bytes 2359304 | tf_op jit(solution)/shard_map/ppermute | solution.py:48
  265.3 16.5 %collective-permute-start.4 = (bf16[6,3,512]{0,2,1:T(8,128)(2,1)S(1)}, bf16[6,3,512]{0,2,1:T(8,128)(2,1)S(1)}, u32[]{:S(2)}, u32[]{:S(2)}) collective-permute-start(bf16[6,3,512]{0,2,1:T(8,128)(2,1)S(1)} %bitcast.205), channel_id=1, source_target_pairs={{0,4},{4,8},{8,12},{12,16},{16,20},{20,24},{24,28},{28,32},{32,36}... | collective-permute-start | bytes 55304 | tf_op jit(solution)/shard_map/ppermute | solution.py:16
  288.9 10.5 %collective-permute-start.5 = (bf16[127,512]{0,1:T(8,128)(2,1)S(1)}, bf16[127,512]{0,1:T(8,128)(2,1)S(1)}, u32[]{:S(2)}, u32[]{:S(2)}) collective-permute-start(bf16[127,512]{0,1:T(8,128)(2,1)S(1)} %slice_bitcast_fusion.1), channel_id=1, source_target_pairs={{0,4},{4,8},{8,12},{12,16},{16,20},{20,24},{24,28},{28,32},{32,36}... | collective-permute-start | bytes 390152 | tf_op jit(solution)/shard_map/ppermute | solution.py:16
  300.0 11.8 %copy-start.7 = (f32[1,512]{1,0:T(1,128)S(1)}, f32[1,512]{1,0:T(1,128)}, u32[]{:S(2)}) copy-start(f32[1,512]{1,0:T(1,128)} %get-tuple-element.75) | copy-start | bytes 6148
  300.0 11.8 %copy-start.8 = (f32[1,512]{1,0:T(1,128)S(1)}, f32[1,512]{1,0:T(1,128)}, u32[]{:S(2)}) copy-start(f32[1,512]{1,0:T(1,128)} %get-tuple-element.76) | copy-start | bytes 6148
  300.0 11.8 %copy-start.9 = (f32[1,512]{1,0:T(1,128)S(1)}, f32[1,512]{1,0:T(1,128)}, u32[]{:S(2)}) copy-start(f32[1,512]{1,0:T(1,128)} %get-tuple-element.77) | copy-start | bytes 6148
  300.0 11.8 %copy-start.10 = (f32[1,512]{1,0:T(1,128)S(1)}, f32[1,512]{1,0:T(1,128)}, u32[]{:S(2)}) copy-start(f32[1,512]{1,0:T(1,128)} %get-tuple-element.78) | copy-start | bytes 6148
  300.1 11.8 %copy-start.11 = (f32[1,512]{1,0:T(1,128)S(1)}, f32[1,512]{1,0:T(1,128)}, u32[]{:S(2)}) copy-start(f32[1,512]{1,0:T(1,128)} %get-tuple-element.79) | copy-start | bytes 6148
  300.1 11.8 %copy-start.12 = (f32[1,512]{1,0:T(1,128)S(1)}, f32[1,512]{1,0:T(1,128)}, u32[]{:S(2)}) copy-start(f32[1,512]{1,0:T(1,128)} %get-tuple-element.80) | copy-start | bytes 6148
  300.1 11.8 %copy-start.13 = (f32[1,512]{1,0:T(1,128)S(1)}, f32[1,512]{1,0:T(1,128)}, u32[]{:S(2)}) copy-start(f32[1,512]{1,0:T(1,128)} %get-tuple-element.81) | copy-start | bytes 6148
  360.4 53.9 %collective-permute-start.6 = (bf16[384,1024]{1,0:T(8,128)(2,1)S(1)}, bf16[384,1024]{1,0:T(8,128)(2,1)}, u32[]{:S(2)}, u32[]{:S(2)}) collective-permute-start(bf16[384,1024]{1,0:T(8,128)(2,1)S(1)} %bitcast.204), channel_id=1, source_target_pairs={{0,1},{1,2},{2,3},{3,0},{4,5},{5,6},{6,7},{7,4},{8,9},{9,10},{10,1... | collective-permute-start | bytes 2359304 | tf_op jit(solution)/shard_map/ppermute | solution.py:63
  368.9 66.5 %copy-start.1 = (bf16[384,1024]{1,0:T(8,128)(2,1)S(1)}, bf16[384,1024]{1,0:T(8,128)(2,1)}, u32[]{:S(2)}) copy-start(bf16[384,1024]{1,0:T(8,128)(2,1)} %copy-done) | copy-start | bytes 2359300
  368.9 66.5 %copy-start.2 = (bf16[384,1,1024]{2,1,0:T(2,128)(2,1)S(1)}, bf16[384,1,1024]{2,1,0:T(2,128)(2,1)}, u32[]{:S(2)}) copy-start(bf16[384,1,1024]{2,1,0:T(2,128)(2,1)} %get-tuple-element.5) | copy-start | bytes 2359300
  370.1 65.2 %collective-permute-start.7 = (bf16[384,1024]{1,0:T(8,128)(2,1)}, bf16[384,1024]{1,0:T(8,128)(2,1)}, u32[]{:S(2)}, u32[]{:S(2)}) collective-permute-start(bf16[384,1024]{1,0:T(8,128)(2,1)} %bitcast.191), channel_id=1, source_target_pairs={{0,2},{1,3},{2,0},{3,1},{4,6},{5,7},{6,4},{7,5},{8,10},{9,11},{10,... | collective-permute-start | bytes 2359304 | tf_op jit(solution)/shard_map/ppermute | solution.py:63
  371.2 64.2 %collective-permute-start.8 = (bf16[384,1024]{1,0:T(8,128)(2,1)}, bf16[384,1024]{1,0:T(8,128)(2,1)}, u32[]{:S(2)}, u32[]{:S(2)}) collective-permute-start(bf16[384,1024]{1,0:T(8,128)(2,1)} %bitcast.190), channel_id=1, source_target_pairs={{0,3},{1,0},{2,1},{3,2},{4,7},{5,4},{6,5},{7,6},{8,11},{9,8},{10,9... | collective-permute-start | bytes 2359304 | tf_op jit(solution)/shard_map/ppermute | solution.py:63
  438.0 10.5 %collective-permute-start.9 = (bf16[256,1024]{1,0:T(8,128)(2,1)S(1)}, bf16[256,1024]{1,0:T(8,128)(2,1)S(1)}, u32[]{:S(2)}, u32[]{:S(2)}) collective-permute-start(bf16[256,1024]{1,0:T(8,128)(2,1)S(1)} %constant_dynamic-slice_fusion), channel_id=1, source_target_pairs={{0,4},{4,0},{8,12},{12,8},{16,20},{20,16},{24,28},{28,24},{32,36},... | collective-permute-start | bytes 1572872 | tf_op jit(solution)/shard_map/ppermute | solution.py:22
  (46 other events, 389.9 us)
Sparse Core Ops, SparseCore 0:
  9.2 35.6 all-gather.3
  46.7 50.2 all-gather.5
  98.8 156.9 all-gather.7

commit v6 on v5

--- a/solution.py
+++ b/solution.py
@@ -22,22 +22,10 @@
     return lax.ppermute(shard, axis, pairs)
 
 
-def shifted(source, offset, count):
+def from_row(source, start, count):
     width = source.shape[1:]
-    pad = 2 * count
-    zeros = jnp.zeros((pad,) + width, source.dtype)
-    padded = jnp.concatenate([zeros, source, zeros], axis=0)
-    start = jnp.clip(pad + offset, 0, padded.shape[0] - count)
-    return lax.dynamic_slice_in_dim(padded, start, count, 0)
-
-
-def spliced(first, first_off, first_len, second, second_off, count):
-    rows = jnp.arange(count, dtype=jnp.int32).reshape((count,) + (1,) * (first.ndim - 1))
-    return jnp.where(
-        rows < first_len,
-        shifted(first, first_off, count),
-        shifted(second, second_off, count),
-    )
+    padded = jnp.concatenate([source, jnp.zeros((count,) + width, source.dtype)], axis=0)
+    return lax.dynamic_slice_in_dim(padded, jnp.clip(start, 0, source.shape[0]), count, 0)
 
 
 def tp_blocks_gather(block, axis):
@@ -95,8 +83,22 @@
 
     sent = lax.dynamic_slice_in_dim(activations, (1 - parity) * share, window, 0)
     got = swapped(sent, CTX)
-    x_even = spliced(activations, 0, even_rows, got, -even_rows, share)
-    x_odd = spliced(got, 0, even_rows - share, activations, share - even_rows, share)
+    rows = jnp.arange(share, dtype=jnp.int32)[:, None]
+    zeros_front = jnp.zeros((share,) + activations.shape[1:], activations.dtype)
+    x_even = jnp.where(
+        rows < even_rows,
+        activations[:share],
+        from_row(jnp.concatenate([zeros_front, got], axis=0), share - even_rows, share),
+    )
+    x_odd = jnp.where(
+        rows < even_rows - share,
+        from_row(got, 0, share),
+        from_row(
+            jnp.concatenate([zeros_front[:window], activations], axis=0),
+            own_rows - even_rows,
+            share,
+        ),
+    )
     x_own = jnp.where(parity == 0, x_even, x_odd)
 
     positions = my_index * share + jnp.arange(share, dtype=jnp.int32)
@@ -144,33 +146,36 @@
     )
     mixed = (feat[:, 1] * feat[:, 2]).astype(jnp.bfloat16)
     rim_long = passed_along(last_rows(mixed, 127), CTX, 1)
-    filtered = causal_taps(
-        jnp.concatenate([rim_long, mixed], axis=0).astype(jnp.float32),
-        long_taps,
-        positions,
-        gstart,
-        128,
-    )
-    gated = (feat[:, 0] * filtered).astype(jnp.bfloat16)
-    partial_out = lax.dot_general(
-        gated,
-        out_rows,
-        (((1,), (1,)), ((), ())),
-        preferred_element_type=jnp.float32,
-    )
-    branch_out = tp_blocks_sum(partial_out.astype(jnp.bfloat16), TP)
-    result = (x_own.astype(jnp.float32) + branch_out).astype(jnp.bfloat16)
+    long_in = jnp.concatenate([rim_long, mixed], axis=0).astype(jnp.float32)
+    half = share // 2
+    results = []
+    for h in range(2):
+        lo = h * half
+        filtered = causal_taps(
+            long_in[lo : lo + half + 127],
+            long_taps,
+            positions[lo : lo + half],
+            gstart[lo : lo + half],
+            128,
+        )
+        gated = (feat[lo : lo + half, 0] * filtered).astype(jnp.bfloat16)
+        partial_out = lax.dot_general(
+            gated,
+            out_rows,
+            (((1,), (1,)), ((), ())),
+            preferred_element_type=jnp.float32,
+        )
+        branch_out = tp_blocks_sum(partial_out.astype(jnp.bfloat16), TP)
+        results.append(
+            (x_own[lo : lo + half].astype(jnp.float32) + branch_out).astype(jnp.bfloat16)
+        )
+    result = jnp.concatenate(results, axis=0)
 
     back = lax.dynamic_slice_in_dim(result, (1 - parity) * (share - window), window, 0)
     got_back = swapped(back, CTX)
-    out_even = spliced(result, 0, share, got_back, -share, own_rows)
-    out_odd = spliced(
-        got_back,
-        even_rows - (share - window),
-        share - even_rows,
-        result,
-        even_rows - share,
-        own_rows,
+    out_even = jnp.concatenate([result, got_back], axis=0)
+    out_odd = from_row(
+        jnp.concatenate([got_back, result], axis=0), even_rows - (share - window), own_rows
     )
     placed_rows = jnp.where(parity == 0, out_even, out_odd)
     slot_ids = jnp.arange(own_rows, dtype=jnp.int32)

time: 465 us -> 473 us (1.017); the launches traced: 465 us -> 466 us
  waiting for transfers between devices: 296 us -> 242 us
  matrix products: 11.7 us -> 64.7 us
  other arithmetic: 83.5 us -> 69.2 us
  starting transfers between devices: 22.5 us -> 32.9 us
  local copies, waits for them, and re-layouts: 34.8 us -> 40 us
    dot_general x1 -> x2, matrix products: 3.5 us -> 56.4 us  [body(): lax.dot_general(gated, out_rows, (((1,), (1,)), ((), ())), preferred_elem...]
    ppermute x3 -> x6, waiting for transfers between devices: 63.8 us -> 26 us  [tp_blocks_sum(): lax.ppermute(sent, axis, [(i, (i + by) % peers) for i in range(peers)])]
    dot_general x1 -> x0, other arithmetic: 32.6 us -> none  [body(): lax.dot_general(gated, out_rows, (((1,), (1,)), ((), ())), preferred_elem...]
    ge x1 -> x30, other arithmetic: 1.52 us -> 19.8 us  [causal_taps(): in_genome = (positions - j >= gstart).reshape(shape)]
    ppermute x3 -> x6, starting transfers between devices: 8.91 us -> 19.7 us  [tp_blocks_sum(): lax.ppermute(sent, axis, [(i, (i + by) % peers) for i in range(peers)])]
    all_gather x3, waiting for transfers between devices: 144 us -> 136 us  [body(): both_rows = lax.all_gather(both_rows, part, axis=0, tiled=True)]
    ppermute x2, waiting for transfers between devices: 17.1 us -> 11.7 us  [swapped(): return lax.ppermute(shard, axis, pairs)]
    add x2 -> x3, other arithmetic: 17.4 us -> 22.3 us  [causal_taps(): summed = summed + jnp.where(in_genome, window * taps[j], jnp.float32(0.0))]
  transfers between devices with their start and end apart: 13 -> 16, of which waited for: 13 -> 11; matrix products, arithmetic and copies ran while one was open for 8% -> 21% of each run, Pallas kernels for 0% -> 0%
where the time goes in v6:
time: 473 us; the launch traced here: 466 us
  waiting for transfers between devices  242 us (51%)
  other arithmetic  69.2 us (15%)
  matrix products  64.7 us (14%)
  local copies, waits for them, and re-layouts  40 us (8%)
  starting transfers between devices  32.9 us (7%)
  between operations  17.3 us (4%)
    all_gather x3, waiting for transfers between devices, body(): both_rows = lax.all_gather(both_rows, part, axis=0, tiled=True)  136 us
    dot_general x2, matrix products, body(): lax.dot_general(gated, out_rows, (((1,), (1,)), ((), ())), preferred_elem...  56.4 us
    ppermute x3, waiting for transfers between devices, tp_blocks_gather(): lax.ppermute(block, axis, [(i, (i + by) % peers) for i in range(peers)])  54.1 us
    ppermute x6, waiting for transfers between devices, tp_blocks_sum(): lax.ppermute(sent, axis, [(i, (i + by) % peers) for i in range(peers)])  26 us
    add x3, other arithmetic, causal_taps(): summed = summed + jnp.where(in_genome, window * taps[j], jnp.float32(0.0))  22.3 us
    ge x30, other arithmetic, causal_taps(): in_genome = (positions - j >= gstart).reshape(shape)  19.8 us
    ppermute x6, starting transfers between devices, tp_blocks_sum(): lax.ppermute(sent, axis, [(i, (i + by) % peers) for i in range(peers)])  19.7 us
    ppermute x2, waiting for transfers between devices, passed_along(): return lax.ppermute(shard, axis, pairs)  14.9 us
  transfers between devices with their start and end apart: 16, of which 11 were waited for; matrix products, arithmetic and copies ran while one was open for 21% of the time, Pallas kernels for 0%

profile of v6, /device:TPU:9, one launch (start us, length us, event | category | flops | bytes accessed | tf_op | source)
XLA Modules:
  0.0 466.4 jit_solution(8159346396411009770)
XLA Ops:
  9.1 35.8 %all-gather.4.cloned.1.call-done = bf16[256,2048]{1,0:T(8,128)(2,1)} async-done(((bf16[64,2048]{1,0:T(8,128)(2,1)}), bf16[256,2048]{1,0:T(8,128)(2,1)}) %all-gather.4.cloned.1.call-update) | async-done | bytes 1048592 | tf_op jit(solution)/shard_map/all_gather | solution.py:122
  45.0 52.0 %all-gather.6.cloned.1.call-done = bf16[1024,2048]{1,0:T(8,128)(2,1)} async-done(((bf16[256,2048]{1,0:T(8,128)(2,1)}), bf16[1024,2048]{1,0:T(8,128)(2,1)}) %all-gather.6.cloned.1.call-update) | async-done | bytes 4194320 | tf_op jit(solution)/shard_map/all_gather | solution.py:122
  121.3 3.9 fusion.27
  125.3 6.5 %collective-permute-start.1 = (bf16[384,1024]{1,0:T(8,128)(2,1)S(1)}, bf16[384,1024]{1,0:T(8,128)(2,1)S(1)}, u32[]{:S(2)}, u32[]{:S(2)}) collective-permute-start(bf16[384,1024]{1,0:T(8,128)(2,1)S(1)} %fusion.27), channel_id=1, source_target_pairs={{0,1},{1,2},{2,3},{3,0},{4,5},{5,6},{6,7},{7,4},{8,9},{9,10},{10,1... | collective-permute-start | bytes 2359304 | tf_op jit(solution)/shard_map/ppermute | solution.py:36
  134.5 21.9 %collective-permute-done.1 = bf16[384,1024]{1,0:T(8,128)(2,1)S(1)} collective-permute-done((bf16[384,1024]{1,0:T(8,128)(2,1)S(1)}, bf16[384,1024]{1,0:T(8,128)(2,1)S(1)}, u32[]{:S(2)}, u32[]{:S(2)}) %collective-permute-start.1) | collective-permute-done | bytes 786464 | tf_op jit(solution)/shard_map/ppermute | solution.py:36
  156.5 31.5 %collective-permute-done.2 = bf16[384,1024]{1,0:T(8,128)(2,1)S(1)} collective-permute-done((bf16[384,1024]{1,0:T(8,128)(2,1)S(1)}, bf16[384,1024]{1,0:T(8,128)(2,1)S(1)}, u32[]{:S(2)}, u32[]{:S(2)}) %collective-permute-start.2) | collective-permute-done | bytes 786464 | tf_op jit(solution)/shard_map/ppermute | solution.py:36
  196.3 6.6 %copy.40 = f32[384,4,1024]{0,2,1:T(8,128)} copy(f32[384,4,1024]{2,0,1:T(8,128)} %convert_bitcast_fusion) | data formatting | bytes 12582912 | tf_op jit(solution)/shard_map/convert_element_type | solution.py:111
  203.9 3.7 fusion.3
  208.0 47.8 %all-gather.8.cloned.1.call-done = bf16[4096,2048]{1,0:T(8,128)(2,1)} async-done(((bf16[1024,2048]{1,0:T(8,128)(2,1)}), bf16[4096,2048]{1,0:T(8,128)(2,1)}) %all-gather.8.cloned.1.call-update) | async-done | bytes 16777232 | tf_op jit(solution)/shard_map/all_gather | solution.py:122
  255.8 8.3 %fusion.4 = bf16[384,1536]{1,0:T(8,128)(2,1)S(1)} fusion(bf16[384,4096]{0,1:T(8,128)(2,1)S(1)} %bitcast.215, bf16[4096,2048]{1,0:T(8,128)(2,1)} %all-gather.8.cloned.1.call-done), kind=kOutput, calls=%fused_computation.12 | convolution fusion | flops 4832428032 | bytes 16908288 | tf_op jit(solution)/shard_map/dot_general | solution.py:137
  275.5 6.4 %collective-permute-done.4 = bf16[6,3,512]{0,2,1:T(8,128)(2,1)S(1)} collective-permute-done((bf16[6,3,512]{0,2,1:T(8,128)(2,1)S(1)}, bf16[6,3,512]{0,2,1:T(8,128)(2,1)S(1)}, u32[]{:S(2)}, u32[]{:S(2)}) %collective-permute-start.4) | collective-permute-done | bytes 18464 | tf_op jit(solution)/shard_map/ppermute | solution.py:16
  282.7 5.7 %fusion.8 = f32[384,3,512]{0,2,1:T(8,128)S(1)} fusion(f32[390,3,512]{0,2,1:T(8,128)S(1)} %maximum_convert_fusion, f32[3,512]{1,0:T(4,128)S(1)} %get-tuple-element.415, f32[3,512]{1,0:T(4,128)S(1)} %get-tuple-element.416, f32[3,512]{1,0:T(4,128)S(1)} %get-tuple-element.417, f32[3,512]{1,0:T(4,128)S(1)} %get-tuple-element.418, ...), kind=kLoop, calls=%fused_computation.21 | loop fusion | flops 11796480 | bytes 18920064 | tf_op jit(solution)/shard_map/add | solution.py:68
  291.2 8.5 %collective-permute-done.5 = bf16[127,512]{0,1:T(8,128)(2,1)S(1)} collective-permute-done((bf16[127,512]{0,1:T(8,128)(2,1)S(1)}, bf16[127,512]{0,1:T(8,128)(2,1)S(1)}, u32[]{:S(2)}, u32[]{:S(2)}) %collective-permute-start.5) | collective-permute-done | bytes 130080 | tf_op jit(solution)/shard_map/ppermute | solution.py:16
  300.4 9.1 %fusion.494 = f32[192,512]{0,1:T(8,128)} fusion(f32[511,512]{0,1:T(8,128)S(1)} %maximum_convert_fusion.1, f32[512]{0:T(512)S(1)} %bitcast.288, f32[512]{0:T(512)S(1)} %bitcast.252, f32[512]{0:T(512)S(1)} %bitcast.254, f32[512]{0:T(512)S(1)} %bitcast.256, f32[512]{0:T(512)S(1)} %bitcast.258, f32[512]{0:T(512)S(1)} %bitcast.260, f32[512]{0:T(512)S(1)} %bitcast.262, ...), kind=kLoop, calls=%fused_computation.749 | loop fusion | flops 9338880 | bytes 13047808 | tf_op jit(solution)/shard_map/add | solution.py:68
  309.5 28.0 %convolution_convert_fusion.1 = bf16[192,4096]{1,0:T(8,128)(2,1)} fusion(bf16[4096,512]{1,0:T(8,128)(2,1)} %bitcast.213, f32[511,512]{0,1:T(8,128)S(1)} %maximum_convert_fusion.1, f32[192,512]{0,1:T(8,128)} %fusion.494, f32[512]{0:T(512)} %bitcast.290, f32[512]{0:T(512)} %bitcast.292, f32[512]{0:T(512)} %bitcast.408, f32[512]{0:T(512)} %bitcast.410, ...), kind=kOutput, calls=%fused_computation.8 | convolution fusion | flops 834600960 | bytes 57231360 | tf_op jit(solution)/shard_map/dot_general | solution.py:162
  345.1 8.2 %collective-permute-start.6 = (bf16[192,1024]{1,0:T(8,128)(2,1)}, bf16[192,1024]{1,0:T(8,128)(2,1)}, u32[]{:S(2)}, u32[]{:S(2)}) collective-permute-start(bf16[192,1024]{1,0:T(8,128)(2,1)} %bitcast.207), channel_id=1, source_target_pairs={{0,1},{1,2},{2,3},{3,0},{4,5},{5,6},{6,7},{7,4},{8,9},{9,10},{10,1... | collective-permute-start | bytes 1179656 | tf_op jit(solution)/shard_map/ppermute | solution.py:51
  355.8 7.5 %fusion.237 = f32[192,512]{0,1:T(8,128)S(1)} fusion(f32[511,512]{0,1:T(8,128)S(1)} %maximum_convert_fusion.1, f32[512]{0:T(512)S(1)} %bitcast.289, f32[512]{0:T(512)S(1)} %bitcast.253, f32[512]{0:T(512)S(1)} %bitcast.255, f32[512]{0:T(512)S(1)} %bitcast.257, f32[512]{0:T(512)S(1)} %bitcast.259, f32[512]{0:T(512)S(1)} %bitcast.261, f32[512]{0:T(512)S(1)} %bitcast.263, ...), kind=kLoop, calls=%fused_computation.363 | loop fusion | flops 9338880 | bytes 13047808 | tf_op jit(solution)/shard_map/add | solution.py:68
  363.4 28.4 %convolution_convert_fusion = bf16[192,4096]{1,0:T(8,128)(2,1)} fusion(bf16[4096,512]{1,0:T(8,128)(2,1)} %bitcast.214, f32[511,512]{0,1:T(8,128)S(1)} %maximum_convert_fusion.1, f32[192,512]{0,1:T(8,128)S(1)} %fusion.237, f32[512]{0:T(512)S(1)} %bitcast.291, f32[512]{0:T(512)S(1)} %bitcast.293, f32[512]{0:T(512)} %bitcast.409, f32[512]{0:T(512)} %bitcast.411, ...), kind=kOutput, calls=%fused_computation.7 | convolution fusion | flops 834600960 | bytes 57393152 | tf_op jit(solution)/shard_map/dot_general | solution.py:162
  398.1 5.1 %collective-permute-start.10 = (bf16[192,1024]{1,0:T(8,128)(2,1)S(1)}, bf16[192,1024]{1,0:T(8,128)(2,1)}, u32[]{:S(2)}, u32[]{:S(2)}) collective-permute-start(bf16[192,1024]{1,0:T(8,128)(2,1)S(1)} %bitcast.221), channel_id=1, source_target_pairs={{0,2},{1,3},{2,0},{3,1},{4,6},{5,7},{6,4},{7,5},{8,10},{9,11},{10,... | collective-permute-start | bytes 1179656 | tf_op jit(solution)/shard_map/ppermute | solution.py:51
  404.9 5.3 %collective-permute-start.9 = (bf16[192,1024]{1,0:T(8,128)(2,1)}, bf16[192,1024]{1,0:T(8,128)(2,1)}, u32[]{:S(2)}, u32[]{:S(2)}) collective-permute-start(bf16[192,1024]{1,0:T(8,128)(2,1)} %bitcast.204), channel_id=1, source_target_pairs={{0,1},{1,2},{2,3},{3,0},{4,5},{5,6},{6,7},{7,4},{8,9},{9,10},{10,1... | collective-permute-start | bytes 1179656 | tf_op jit(solution)/shard_map/ppermute | solution.py:51
  410.2 17.5 %collective-permute-done.10 = bf16[192,1024]{1,0:T(8,128)(2,1)} collective-permute-done((bf16[192,1024]{1,0:T(8,128)(2,1)S(1)}, bf16[192,1024]{1,0:T(8,128)(2,1)}, u32[]{:S(2)}, u32[]{:S(2)}) %collective-permute-start.10) | collective-permute-done | bytes 393248 | tf_op jit(solution)/shard_map/ppermute | solution.py:51
  427.7 8.4 %collective-permute-done.11 = bf16[192,1024]{1,0:T(8,128)(2,1)} collective-permute-done((bf16[192,1024]{1,0:T(8,128)(2,1)S(1)}, bf16[192,1024]{1,0:T(8,128)(2,1)}, u32[]{:S(2)}, u32[]{:S(2)}) %collective-permute-start.11) | collective-permute-done | bytes 393248 | tf_op jit(solution)/shard_map/ppermute | solution.py:51
  440.5 11.7 %collective-permute-done.12 = bf16[256,1024]{1,0:T(8,128)(2,1)S(1)} collective-permute-done((bf16[256,1024]{1,0:T(8,128)(2,1)S(1)}, bf16[256,1024]{1,0:T(8,128)(2,1)S(1)}, u32[]{:S(2)}, u32[]{:S(2)}) %collective-permute-start.12) | collective-permute-done | bytes 524320 | tf_op jit(solution)/shard_map/ppermute | solution.py:22
  452.4 7.1 %fusion.24 = bf16[640,1024]{1,0:T(8,128)(2,1)} fusion(bf16[640,1024]{1,0:T(8,128)(2,1)S(1)} %broadcast.1235, s32[]{:T(128)S(6)} %min.14, bf16[256,1024]{1,0:T(8,128)(2,1)S(1)} %collective-permute-done.12, bf16[192,1024]{1,0:T(8,128)(2,1)S(1)} %get-tuple-element.14, bf16[192,1024]{1,0:T(8,128)(2,1)S(1)} %get-tuple-element.13, ...), kind=kLoop, calls=%fused_computation.47 | loop fusion | flops 10485760 | bytes 3932805 | tf_op jit(solution)/shard_map/jit(_where)/select_n | solution.py:183
  (299 shorter events, 74.2 us)
Async XLA Ops:
  6.5 38.3 %all-gather.4.cloned.1.call-start = ((), (), s32[]{:S(2)}) async-start(), calls=%async_computation | async-start | bytes 1310720 | tf_op jit(solution)/shard_map/all_gather | solution.py:122
  9.1 87.9 %all-gather.6.cloned.1.call-start = ((), (), s32[]{:S(2)}) async-start(), calls=%async_computation.1 | async-start | bytes 5242880 | tf_op jit(solution)/shard_map/all_gather | solution.py:122
  44.9 52.1 %copy-start.3 = (bf16[640,1024]{1,0:T(8,128)(2,1)S(1)}, bf16[640,1024]{1,0:T(8,128)(2,1)}, u32[]{:S(2)}) copy-start(bf16[640,1024]{1,0:T(8,128)(2,1)} %param.7) | copy-start | bytes 3932164
  44.9 210.9 %all-gather.8.cloned.1.call-start = ((), (), s32[]{:S(2)}) async-start(), calls=%async_computation.2 | async-start | bytes 20971520 | tf_op jit(solution)/shard_map/all_gather | solution.py:122
  97.0 21.6 %copy-start.6 = (f32[7,3,512]{2,0,1:T(8,128)S(1)}, f32[7,3,512]{2,0,1:T(8,128)}, u32[]{:S(2)}) copy-start(f32[7,3,512]{2,0,1:T(8,128)} %param.11) | copy-start | bytes 129028
  97.0 21.6 %copy-start.5 = (f32[128,512]{1,0:T(8,128)S(1)}, f32[128,512]{1,0:T(8,128)}, u32[]{:S(2)}) copy-start(f32[128,512]{1,0:T(8,128)} %param.12) | copy-start | bytes 786436
  97.1 24.2 %collective-permute-start = (bf16[256,1024]{1,0:T(8,128)(2,1)S(1)}, bf16[256,1024]{1,0:T(8,128)(2,1)S(1)}, u32[]{:S(2)}, u32[]{:S(2)}) collective-permute-start(bf16[256,1024]{1,0:T(8,128)(2,1)S(1)} %constant_dynamic-slice_fusion.8), channel_id=1, source_target_pairs={{0,4},{4,0},{8,12},{12,8},{16,20},{20,16},{24,28},{28,24},{32,36},... | collective-permute-start | bytes 1572872 | tf_op jit(solution)/shard_map/ppermute | solution.py:22
  125.3 63.3 %copy-start.1 = (bf16[384,1024]{1,0:T(8,128)(2,1)}, bf16[384,1024]{1,0:T(8,128)(2,1)S(1)}, u32[]{:S(2)}) copy-start(bf16[384,1024]{1,0:T(8,128)(2,1)S(1)} %fusion.27) | copy-start | bytes 2359300
  125.3 31.2 %collective-permute-start.1 = (bf16[384,1024]{1,0:T(8,128)(2,1)S(1)}, bf16[384,1024]{1,0:T(8,128)(2,1)S(1)}, u32[]{:S(2)}, u32[]{:S(2)}) collective-permute-start(bf16[384,1024]{1,0:T(8,128)(2,1)S(1)} %fusion.27), channel_id=1, source_target_pairs={{0,1},{1,2},{2,3},{3,0},{4,5},{5,6},{6,7},{7,4},{8,9},{9,10},{10,1... | collective-permute-start | bytes 2359304 | tf_op jit(solution)/shard_map/ppermute | solution.py:36
  131.8 56.1 %collective-permute-start.2 = (bf16[384,1024]{1,0:T(8,128)(2,1)S(1)}, bf16[384,1024]{1,0:T(8,128)(2,1)S(1)}, u32[]{:S(2)}, u32[]{:S(2)}) collective-permute-start(bf16[384,1024]{1,0:T(8,128)(2,1)S(1)} %fusion.27), channel_id=1, source_target_pairs={{0,2},{1,3},{2,0},{3,1},{4,6},{5,7},{6,4},{7,5},{8,10},{9,11},{10,... | collective-permute-start | bytes 2359304 | tf_op jit(solution)/shard_map/ppermute | solution.py:36
  131.8 56.8 %collective-permute-start.3 = (bf16[384,1024]{1,0:T(8,128)(2,1)S(1)}, bf16[384,1024]{1,0:T(8,128)(2,1)S(1)}, u32[]{:S(2)}, u32[]{:S(2)}) collective-permute-start(bf16[384,1024]{1,0:T(8,128)(2,1)S(1)} %fusion.27), channel_id=1, source_target_pairs={{0,3},{1,0},{2,1},{3,2},{4,7},{5,4},{6,5},{7,6},{8,11},{9,8},{10,9... | collective-permute-start | bytes 2359304 | tf_op jit(solution)/shard_map/ppermute | solution.py:36
  265.3 16.5 %collective-permute-start.4 = (bf16[6,3,512]{0,2,1:T(8,128)(2,1)S(1)}, bf16[6,3,512]{0,2,1:T(8,128)(2,1)S(1)}, u32[]{:S(2)}, u32[]{:S(2)}) collective-permute-start(bf16[6,3,512]{0,2,1:T(8,128)(2,1)S(1)} %bitcast.220), channel_id=1, source_target_pairs={{0,4},{4,8},{8,12},{12,16},{16,20},{20,24},{24,28},{28,32},{32,36}... | collective-permute-start | bytes 55304 | tf_op jit(solution)/shard_map/ppermute | solution.py:16
  288.5 21.0 %copy-start = (f32[384,3,512]{0,2,1:T(8,128)}, f32[384,3,512]{0,2,1:T(8,128)S(1)}, u32[]{:S(2)}) copy-start(f32[384,3,512]{0,2,1:T(8,128)S(1)} %fusion.8) | copy-start | bytes 7077892
  289.1 10.7 %collective-permute-start.5 = (bf16[127,512]{0,1:T(8,128)(2,1)S(1)}, bf16[127,512]{0,1:T(8,128)(2,1)S(1)}, u32[]{:S(2)}, u32[]{:S(2)}) collective-permute-start(bf16[127,512]{0,1:T(8,128)(2,1)S(1)} %slice_bitcast_fusion.2), channel_id=1, source_target_pairs={{0,4},{4,8},{8,12},{12,16},{16,20},{20,24},{24,28},{28,32},{32,36}... | collective-permute-start | bytes 390152 | tf_op jit(solution)/shard_map/ppermute | solution.py:16
  343.9 11.5 %copy-start.17 = (pred[192]{0:T(512)(128)(4,1)S(1)}, pred[192]{0:T(512)(128)(4,1)}, u32[]{:S(2)}) copy-start(pred[192]{0:T(512)(128)(4,1)} %get-tuple-element.151) | copy-start | bytes 580
  343.9 11.5 %copy-start.18 = (pred[192]{0:T(512)(128)(4,1)S(1)}, pred[192]{0:T(512)(128)(4,1)}, u32[]{:S(2)}) copy-start(pred[192]{0:T(512)(128)(4,1)} %get-tuple-element.152) | copy-start | bytes 580
  345.1 59.8 %collective-permute-start.6 = (bf16[192,1024]{1,0:T(8,128)(2,1)}, bf16[192,1024]{1,0:T(8,128)(2,1)}, u32[]{:S(2)}, u32[]{:S(2)}) collective-permute-start(bf16[192,1024]{1,0:T(8,128)(2,1)} %bitcast.207), channel_id=1, source_target_pairs={{0,1},{1,2},{2,3},{3,0},{4,5},{5,6},{6,7},{7,4},{8,9},{9,10},{10,1... | collective-permute-start | bytes 1179656 | tf_op jit(solution)/shard_map/ppermute | solution.py:51
  354.2 56.0 %collective-permute-start.7 = (bf16[192,1024]{1,0:T(8,128)(2,1)}, bf16[192,1024]{1,0:T(8,128)(2,1)}, u32[]{:S(2)}, u32[]{:S(2)}) collective-permute-start(bf16[192,1024]{1,0:T(8,128)(2,1)} %bitcast.206), channel_id=1, source_target_pairs={{0,2},{1,3},{2,0},{3,1},{4,6},{5,7},{6,4},{7,5},{8,10},{9,11},{10,... | collective-permute-start | bytes 1179656 | tf_op jit(solution)/shard_map/ppermute | solution.py:51
  355.0 55.2 %collective-permute-start.8 = (bf16[192,1024]{1,0:T(8,128)(2,1)}, bf16[192,1024]{1,0:T(8,128)(2,1)}, u32[]{:S(2)}, u32[]{:S(2)}) collective-permute-start(bf16[192,1024]{1,0:T(8,128)(2,1)} %bitcast.205), channel_id=1, source_target_pairs={{0,3},{1,0},{2,1},{3,2},{4,7},{5,4},{6,5},{7,6},{8,11},{9,8},{10,9... | collective-permute-start | bytes 1179656 | tf_op jit(solution)/shard_map/ppermute | solution.py:51
  398.0 38.2 %copy-start.2 = (bf16[384,1024]{1,0:T(8,128)(2,1)S(1)}, bf16[384,1024]{1,0:T(8,128)(2,1)}, u32[]{:S(2)}) copy-start(bf16[384,1024]{1,0:T(8,128)(2,1)} %copy-done.1) | copy-start | bytes 2359300
  398.1 29.6 %collective-permute-start.10 = (bf16[192,1024]{1,0:T(8,128)(2,1)S(1)}, bf16[192,1024]{1,0:T(8,128)(2,1)}, u32[]{:S(2)}, u32[]{:S(2)}) collective-permute-start(bf16[192,1024]{1,0:T(8,128)(2,1)S(1)} %bitcast.221), channel_id=1, source_target_pairs={{0,2},{1,3},{2,0},{3,1},{4,6},{5,7},{6,4},{7,5},{8,10},{9,11},{10,... | collective-permute-start | bytes 1179656 | tf_op jit(solution)/shard_map/ppermute | solution.py:51
  403.3 32.8 %collective-permute-start.11 = (bf16[192,1024]{1,0:T(8,128)(2,1)S(1)}, bf16[192,1024]{1,0:T(8,128)(2,1)}, u32[]{:S(2)}, u32[]{:S(2)}) collective-permute-start(bf16[192,1024]{1,0:T(8,128)(2,1)S(1)} %bitcast.222), channel_id=1, source_target_pairs={{0,3},{1,0},{2,1},{3,2},{4,7},{5,4},{6,5},{7,6},{8,11},{9,8},{10,9... | collective-permute-start | bytes 1179656 | tf_op jit(solution)/shard_map/ppermute | solution.py:51
  404.9 31.2 %collective-permute-start.9 = (bf16[192,1024]{1,0:T(8,128)(2,1)}, bf16[192,1024]{1,0:T(8,128)(2,1)}, u32[]{:S(2)}, u32[]{:S(2)}) collective-permute-start(bf16[192,1024]{1,0:T(8,128)(2,1)} %bitcast.204), channel_id=1, source_target_pairs={{0,1},{1,2},{2,3},{3,0},{4,5},{5,6},{6,7},{7,4},{8,9},{9,10},{10,1... | collective-permute-start | bytes 1179656 | tf_op jit(solution)/shard_map/ppermute | solution.py:51
  439.0 13.2 %collective-permute-start.12 = (bf16[256,1024]{1,0:T(8,128)(2,1)S(1)}, bf16[256,1024]{1,0:T(8,128)(2,1)S(1)}, u32[]{:S(2)}, u32[]{:S(2)}) collective-permute-start(bf16[256,1024]{1,0:T(8,128)(2,1)S(1)} %fusion.41), channel_id=1, source_target_pairs={{0,4},{4,0},{8,12},{12,8},{16,20},{20,16},{24,28},{28,24},{32,36},... | collective-permute-start | bytes 1572872 | tf_op jit(solution)/shard_map/ppermute | solution.py:22
  (89 other events, 875.8 us)
Sparse Core Ops, SparseCore 0:
  9.2 35.6 all-gather.3
  46.7 50.2 all-gather.5
  98.8 156.9 all-gather.7

commit v7 on v6

--- a/solution.py
+++ b/solution.py
@@ -38,6 +38,19 @@
     order = (me - jnp.arange(peers, dtype=jnp.int32)) % peers
     ordered = jnp.take(stacked, order, axis=0)
     return jnp.moveaxis(ordered, 0, 1).reshape(block.shape[0], peers * block.shape[1])
+
+
+def tp_blocks_swap(blocks, axis):
+    peers = lax.axis_size(axis)
+    me = lax.axis_index(axis)
+    got = [lax.dynamic_index_in_dim(blocks, me, 0, keepdims=False)]
+    for by in range(1, peers):
+        sent = lax.dynamic_index_in_dim(blocks, (me + by) % peers, 0, keepdims=False)
+        got.append(lax.ppermute(sent, axis, [(i, (i + by) % peers) for i in range(peers)]))
+    stacked = jnp.stack(got)
+    order = (me - jnp.arange(peers, dtype=jnp.int32)) % peers
+    ordered = jnp.take(stacked, order, axis=0)
+    return jnp.moveaxis(ordered, 0, 1).reshape(blocks.shape[1], peers * blocks.shape[2])
 
 
 def tp_blocks_sum(full, axis):
@@ -146,30 +159,24 @@
     )
     mixed = (feat[:, 1] * feat[:, 2]).astype(jnp.bfloat16)
     rim_long = passed_along(last_rows(mixed, 127), CTX, 1)
-    long_in = jnp.concatenate([rim_long, mixed], axis=0).astype(jnp.float32)
-    half = share // 2
-    results = []
-    for h in range(2):
-        lo = h * half
-        filtered = causal_taps(
-            long_in[lo : lo + half + 127],
-            long_taps,
-            positions[lo : lo + half],
-            gstart[lo : lo + half],
-            128,
-        )
-        gated = (feat[lo : lo + half, 0] * filtered).astype(jnp.bfloat16)
-        partial_out = lax.dot_general(
-            gated,
-            out_rows,
-            (((1,), (1,)), ((), ())),
-            preferred_element_type=jnp.float32,
-        )
-        branch_out = tp_blocks_sum(partial_out.astype(jnp.bfloat16), TP)
-        results.append(
-            (x_own[lo : lo + half].astype(jnp.float32) + branch_out).astype(jnp.bfloat16)
-        )
-    result = jnp.concatenate(results, axis=0)
+    filtered = causal_taps(
+        jnp.concatenate([rim_long, mixed], axis=0).astype(jnp.float32),
+        long_taps,
+        positions,
+        gstart,
+        128,
+    )
+    gated = (feat[:, 0] * filtered).astype(jnp.bfloat16)
+    feats = x_own.shape[1]
+    my_cols = tp_blocks_swap(out_rows.reshape(-1, feats, chans), TP)
+    gated_all = tp_blocks_gather(gated, TP)
+    branch_out = lax.dot_general(
+        gated_all,
+        my_cols,
+        (((1,), (1,)), ((), ())),
+        preferred_element_type=jnp.float32,
+    )
+    result = (x_own.astype(jnp.float32) + branch_out).astype(jnp.bfloat16)
 
     back = lax.dynamic_slice_in_dim(result, (1 - parity) * (share - window), window, 0)
     got_back = swapped(back, CTX)

time: 473 us -> 504 us (1.066); the launches traced: 466 us -> 503 us
  waiting for transfers between devices: 242 us -> 336 us
  matrix products: 64.7 us -> 12.5 us
  local copies, waits for them, and re-layouts: 40 us -> 27.6 us
  other arithmetic: 69.2 us -> 79.6 us
    ppermute x2, waiting for transfers between devices: 14.9 us -> 89.2 us  [passed_along(): return lax.ppermute(shard, axis, pairs)]
    dot_general x2 -> x1, matrix products: 56.4 us -> 4.32 us  [body(): lax.dot_general(gated_all, my_cols, (((1,), (1,)), ((), ())), preferred_e...]
    convert_element_type x2, other arithmetic: 2.79 us -> 32.9 us  [the longest x1 32.6 us: body(): gated = (feat[:, 0] * filtered).astype(jnp.bfloat16)]
    ppermute x3 -> x6, waiting for transfers between devices: 54.1 us -> 83 us  [tp_blocks_gather(): lax.ppermute(block, axis, [(i, (i + by) % peers) for i in range(peers)])]
    ppermute x6 -> x3, waiting for transfers between devices: 26 us -> 0.01 us  [tp_blocks_swap(): lax.ppermute(sent, axis, [(i, (i + by) % peers) for i in range(peers)])]
    ge x30 -> x1, other arithmetic: 19.8 us -> 1.5 us  [causal_taps(): in_genome = (positions - j >= gstart).reshape(shape)]
    ppermute x6 -> x3, starting transfers between devices: 19.7 us -> 7.03 us  [tp_blocks_swap(): lax.ppermute(sent, axis, [(i, (i + by) % peers) for i in range(peers)])]
    ppermute x3 -> x6, starting transfers between devices: 7.23 us -> 18.4 us  [tp_blocks_gather(): lax.ppermute(block, axis, [(i, (i + by) % peers) for i in range(peers)])]
  transfers between devices with their start and end apart: 16 -> 16, of which waited for: 11 -> 13; matrix products, arithmetic and copies ran while one was open for 21% -> 18% of each run, Pallas kernels for 0% -> 0%
where the time goes in v7:
time: 504 us; the launch traced here: 503 us
  waiting for transfers between devices  336 us (67%)
  other arithmetic  79.6 us (16%)
  starting transfers between devices  31.7 us (6%)
  local copies, waits for them, and re-layouts  27.6 us (5%)
  between operations  16 us (3%)
  matrix products  12.5 us (2%)
    all_gather x3, waiting for transfers between devices, body(): both_rows = lax.all_gather(both_rows, part, axis=0, tiled=True)  145 us
    ppermute x2, waiting for transfers between devices, passed_along(): return lax.ppermute(shard, axis, pairs)  89.2 us
    ppermute x6, waiting for transfers between devices, tp_blocks_gather(): lax.ppermute(block, axis, [(i, (i + by) % peers) for i in range(peers)])  83 us
    convert_element_type x1, other arithmetic, body(): gated = (feat[:, 0] * filtered).astype(jnp.bfloat16)  32.6 us
    ppermute x6, starting transfers between devices, tp_blocks_gather(): lax.ppermute(block, axis, [(i, (i + by) % peers) for i in range(peers)])  18.4 us
    ppermute x2, waiting for transfers between devices, swapped(): return lax.ppermute(shard, axis, pairs)  18.3 us
    add x2, other arithmetic, causal_taps(): summed = summed + jnp.where(in_genome, window * taps[j], jnp.float32(0.0))  17.4 us
  transfers between devices with their start and end apart: 16, of which 13 were waited for; matrix products, arithmetic and copies ran while one was open for 18% of the time, Pallas kernels for 0%

profile of v7, /device:TPU:9, one launch (start us, length us, event | category | flops | bytes accessed | tf_op | source)
XLA Modules:
  0.0 503.1 jit_solution(13915628207697848480)
XLA Ops:
  9.1 35.8 %all-gather.4.cloned.1.call-done = bf16[256,2048]{1,0:T(8,128)(2,1)} async-done(((bf16[64,2048]{1,0:T(8,128)(2,1)}), bf16[256,2048]{1,0:T(8,128)(2,1)}) %all-gather.4.cloned.1.call-update) | async-done | bytes 1048592 | tf_op jit(solution)/shard_map/all_gather | solution.py:135
  45.0 52.0 %all-gather.6.cloned.1.call-done = bf16[1024,2048]{1,0:T(8,128)(2,1)} async-done(((bf16[256,2048]{1,0:T(8,128)(2,1)}), bf16[1024,2048]{1,0:T(8,128)(2,1)}) %all-gather.6.cloned.1.call-update) | async-done | bytes 4194320 | tf_op jit(solution)/shard_map/all_gather | solution.py:135
  102.0 7.9 %collective-permute-done = bf16[256,1024]{1,0:T(8,128)(2,1)S(1)} collective-permute-done((bf16[256,1024]{1,0:T(8,128)(2,1)S(1)}, bf16[256,1024]{1,0:T(8,128)(2,1)S(1)}, u32[]{:S(2)}, u32[]{:S(2)}) %collective-permute-start) | collective-permute-done | bytes 524320 | tf_op jit(solution)/shard_map/ppermute | solution.py:22
  109.9 3.9 fusion.39
  113.8 7.1 %collective-permute-start.1 = (bf16[384,1024]{1,0:T(8,128)(2,1)S(1)}, bf16[384,1024]{1,0:T(8,128)(2,1)S(1)}, u32[]{:S(2)}, u32[]{:S(2)}) collective-permute-start(bf16[384,1024]{1,0:T(8,128)(2,1)S(1)} %fusion.39), channel_id=1, source_target_pairs={{0,1},{1,2},{2,3},{3,0},{4,5},{5,6},{6,7},{7,4},{8,9},{9,10},{10,1... | collective-permute-start | bytes 2359304 | tf_op jit(solution)/shard_map/ppermute | solution.py:36
  124.2 21.5 %collective-permute-done.1 = bf16[384,1024]{1,0:T(8,128)(2,1)S(1)} collective-permute-done((bf16[384,1024]{1,0:T(8,128)(2,1)S(1)}, bf16[384,1024]{1,0:T(8,128)(2,1)S(1)}, u32[]{:S(2)}, u32[]{:S(2)}) %collective-permute-start.1) | collective-permute-done | bytes 786464 | tf_op jit(solution)/shard_map/ppermute | solution.py:36
  145.6 31.5 %collective-permute-done.2 = bf16[384,1024]{1,0:T(8,128)(2,1)S(1)} collective-permute-done((bf16[384,1024]{1,0:T(8,128)(2,1)S(1)}, bf16[384,1024]{1,0:T(8,128)(2,1)S(1)}, u32[]{:S(2)}, u32[]{:S(2)}) %collective-permute-start.2) | collective-permute-done | bytes 786464 | tf_op jit(solution)/shard_map/ppermute | solution.py:36
  182.5 3.7 convert_bitcast_fusion
  186.2 6.7 %copy.19 = f32[384,4,1024]{0,2,1:T(8,128)} copy(f32[384,4,1024]{2,0,1:T(8,128)} %convert_bitcast_fusion) | data formatting | bytes 12582912 | tf_op jit(solution)/shard_map/convert_element_type | solution.py:124
  198.5 57.3 %all-gather.8.cloned.1.call-done = bf16[4096,2048]{1,0:T(8,128)(2,1)} async-done(((bf16[1024,2048]{1,0:T(8,128)(2,1)}), bf16[4096,2048]{1,0:T(8,128)(2,1)}) %all-gather.8.cloned.1.call-update) | async-done | bytes 16777232 | tf_op jit(solution)/shard_map/all_gather | solution.py:135
  255.8 8.2 %fusion.8 = bf16[384,1536]{1,0:T(8,128)(2,1)S(1)} fusion(bf16[384,4096]{0,1:T(8,128)(2,1)S(1)} %bitcast.205, bf16[4096,2048]{1,0:T(8,128)(2,1)} %all-gather.8.cloned.1.call-done), kind=kOutput, calls=%fused_computation.17 | convolution fusion | flops 4832428032 | bytes 16908288 | tf_op jit(solution)/shard_map/dot_general | solution.py:150
  272.8 6.5 %collective-permute-start.9 = (bf16[1024,512]{1,0:T(8,128)(2,1)}, bf16[1024,512]{1,0:T(8,128)(2,1)}, u32[]{:S(2)}, u32[]{:S(2)}) collective-permute-start(bf16[1024,512]{1,0:T(8,128)(2,1)} %get-tuple-element.8), channel_id=1, source_target_pairs={{0,1},{1,2},{2,3},{3,0},{4,5},{5,6},{6,7},{7,4},{8,9},{9,10},{10,1... | collective-permute-start | bytes 3145736 | tf_op jit(solution)/shard_map/ppermute | solution.py:49
  282.9 5.7 %fusion.12 = f32[384,3,512]{0,2,1:T(8,128)S(1)} fusion(f32[390,3,512]{0,2,1:T(8,128)S(1)} %maximum_convert_fusion, f32[3,512]{1,0:T(4,128)S(1)} %get-tuple-element.274, f32[3,512]{1,0:T(4,128)S(1)} %get-tuple-element.275, f32[3,512]{1,0:T(4,128)S(1)} %get-tuple-element.276, f32[3,512]{1,0:T(4,128)S(1)} %get-tuple-element.277, ...), kind=kLoop, calls=%fused_computation.25 | loop fusion | flops 11796480 | bytes 18920064 | tf_op jit(solution)/shard_map/add | solution.py:81
  291.2 87.0 %collective-permute-done.5 = bf16[127,512]{0,1:T(8,128)(2,1)S(1)} collective-permute-done((bf16[127,512]{0,1:T(8,128)(2,1)S(1)}, bf16[127,512]{0,1:T(8,128)(2,1)S(1)}, u32[]{:S(2)}, u32[]{:S(2)}) %collective-permute-start.5) | collective-permute-done | bytes 130080 | tf_op jit(solution)/shard_map/ppermute | solution.py:16
  378.9 11.7 %fusion.239 = f32[384,512]{0,1:T(8,128)S(1)} fusion(f32[511,512]{0,1:T(8,128)S(1)} %maximum_convert_fusion.1, f32[512]{0:T(512)} %bitcast.345, f32[512]{0:T(512)S(1)} %bitcast.327, f32[512]{0:T(512)S(1)} %bitcast.328, f32[512]{0:T(512)S(1)} %bitcast.329, f32[512]{0:T(512)S(1)} %bitcast.330, f32[512]{0:T(512)S(1)} %bitcast.331, f32[512]{0:T(512)S(1)} %bitcast.332, ...), kind=kLoop, calls=%fused_computation.361 | loop fusion | flops 18677760 | bytes 26030080 | tf_op jit(solution)/shard_map/add | solution.py:81
  390.7 32.6 %fusion.47 = bf16[384,512]{0,1:T(8,128)(2,1)S(1)} fusion(f32[511,512]{0,1:T(8,128)S(1)} %maximum_convert_fusion.1, f32[384,512]{0,1:T(8,128)S(1)} %fusion.239, f32[512]{0:T(512)S(1)} %bitcast.218, f32[512]{0:T(512)S(1)} %bitcast.219, f32[512]{0:T(512)S(1)} %bitcast.277, f32[512]{0:T(512)S(1)} %bitcast.278, f32[512]{0:T(512)S(1)} %bitcast.279, ...), kind=kLoop, calls=%fused_computation.73 | loop fusion | flops 57016320 | bytes 77697024 | tf_op jit(solution)/shard_map/convert_element_type | solution.py:169
  423.3 5.1 %collective-permute-start.6 = (bf16[384,512]{0,1:T(8,128)(2,1)S(1)}, bf16[384,512]{0,1:T(8,128)(2,1)S(1)}, u32[]{:S(2)}, u32[]{:S(2)}) collective-permute-start(bf16[384,512]{0,1:T(8,128)(2,1)S(1)} %fusion.47), channel_id=1, source_target_pairs={{0,1},{1,2},{2,3},{3,0},{4,5},{5,6},{6,7},{7,4},{8,9},{9,10},{10,1... | collective-permute-start | bytes 1179656 | tf_op jit(solution)/shard_map/ppermute | solution.py:36
  430.0 21.6 %collective-permute-done.6 = bf16[384,512]{0,1:T(8,128)(2,1)S(1)} collective-permute-done((bf16[384,512]{0,1:T(8,128)(2,1)S(1)}, bf16[384,512]{0,1:T(8,128)(2,1)S(1)}, u32[]{:S(2)}, u32[]{:S(2)}) %collective-permute-start.6) | collective-permute-done | bytes 393248 | tf_op jit(solution)/shard_map/ppermute | solution.py:36
  451.6 4.1 collective-permute-start.8
  459.2 4.2 collective-permute-done.8
  471.3 5.3 %gather_fusion.2 = bf16[4,1024,512]{2,1,0:T(8,128)(2,1)} fusion(bf16[4,1024,512]{2,1,0:T(8,128)(2,1)} %pad_maximum_fusion, s32[1024]{0:T(1024)} %pad_clamp_fusion), kind=kCustom, calls=%fused_computation.2 | custom fusion | bytes 8388624 | tf_op jit(solution)/shard_map/jit(_take)/gather | solution.py:52
  476.6 4.3 fusion.25
  482.2 10.5 %collective-permute-done.12 = bf16[256,1024]{1,0:T(8,128)(2,1)S(1)} collective-permute-done((bf16[256,1024]{1,0:T(8,128)(2,1)S(1)}, bf16[256,1024]{1,0:T(8,128)(2,1)S(1)}, u32[]{:S(2)}, u32[]{:S(2)}) %collective-permute-start.12) | collective-permute-done | bytes 524320 | tf_op jit(solution)/shard_map/ppermute | solution.py:22
  492.8 3.8 fusion.32
  (189 shorter events, 49.3 us)
Async XLA Ops:
  6.5 38.3 %all-gather.4.cloned.1.call-start = ((), (), s32[]{:S(2)}) async-start(), calls=%async_computation | async-start | bytes 1310720 | tf_op jit(solution)/shard_map/all_gather | solution.py:135
  9.1 87.9 %all-gather.6.cloned.1.call-start = ((), (), s32[]{:S(2)}) async-start(), calls=%async_computation.1 | async-start | bytes 5242880 | tf_op jit(solution)/shard_map/all_gather | solution.py:135
  44.9 210.9 %all-gather.8.cloned.1.call-start = ((), (), s32[]{:S(2)}) async-start(), calls=%async_computation.2 | async-start | bytes 20971520 | tf_op jit(solution)/shard_map/all_gather | solution.py:135
  97.1 12.7 %collective-permute-start = (bf16[256,1024]{1,0:T(8,128)(2,1)S(1)}, bf16[256,1024]{1,0:T(8,128)(2,1)S(1)}, u32[]{:S(2)}, u32[]{:S(2)}) collective-permute-start(bf16[256,1024]{1,0:T(8,128)(2,1)S(1)} %constant_dynamic-slice_fusion.2), channel_id=1, source_target_pairs={{0,4},{4,0},{8,12},{12,8},{16,20},{20,16},{24,28},{28,24},{32,36},... | collective-permute-start | bytes 1572872 | tf_op jit(solution)/shard_map/ppermute | solution.py:22
  113.8 31.8 %collective-permute-start.1 = (bf16[384,1024]{1,0:T(8,128)(2,1)S(1)}, bf16[384,1024]{1,0:T(8,128)(2,1)S(1)}, u32[]{:S(2)}, u32[]{:S(2)}) collective-permute-start(bf16[384,1024]{1,0:T(8,128)(2,1)S(1)} %fusion.39), channel_id=1, source_target_pairs={{0,1},{1,2},{2,3},{3,0},{4,5},{5,6},{6,7},{7,4},{8,9},{9,10},{10,1... | collective-permute-start | bytes 2359304 | tf_op jit(solution)/shard_map/ppermute | solution.py:36
  120.9 56.2 %collective-permute-start.2 = (bf16[384,1024]{1,0:T(8,128)(2,1)S(1)}, bf16[384,1024]{1,0:T(8,128)(2,1)S(1)}, u32[]{:S(2)}, u32[]{:S(2)}) collective-permute-start(bf16[384,1024]{1,0:T(8,128)(2,1)S(1)} %fusion.39), channel_id=1, source_target_pairs={{0,2},{1,3},{2,0},{3,1},{4,6},{5,7},{6,4},{7,5},{8,10},{9,11},{10,... | collective-permute-start | bytes 2359304 | tf_op jit(solution)/shard_map/ppermute | solution.py:36
  121.0 56.8 %collective-permute-start.3 = (bf16[384,1024]{1,0:T(8,128)(2,1)S(1)}, bf16[384,1024]{1,0:T(8,128)(2,1)S(1)}, u32[]{:S(2)}, u32[]{:S(2)}) collective-permute-start(bf16[384,1024]{1,0:T(8,128)(2,1)S(1)} %fusion.39), channel_id=1, source_target_pairs={{0,3},{1,0},{2,1},{3,2},{4,7},{5,4},{6,5},{7,6},{8,11},{9,8},{10,9... | collective-permute-start | bytes 2359304 | tf_op jit(solution)/shard_map/ppermute | solution.py:36
  265.3 16.8 %collective-permute-start.4 = (bf16[6,3,512]{0,2,1:T(8,128)(2,1)S(1)}, bf16[6,3,512]{0,2,1:T(8,128)(2,1)S(1)}, u32[]{:S(2)}, u32[]{:S(2)}) collective-permute-start(bf16[6,3,512]{0,2,1:T(8,128)(2,1)S(1)} %bitcast.214), channel_id=1, source_target_pairs={{0,4},{4,8},{8,12},{12,16},{16,20},{20,24},{24,28},{28,32},{32,36}... | collective-permute-start | bytes 55304 | tf_op jit(solution)/shard_map/ppermute | solution.py:16
  272.8 194.7 %collective-permute-start.9 = (bf16[1024,512]{1,0:T(8,128)(2,1)}, bf16[1024,512]{1,0:T(8,128)(2,1)}, u32[]{:S(2)}, u32[]{:S(2)}) collective-permute-start(bf16[1024,512]{1,0:T(8,128)(2,1)} %get-tuple-element.8), channel_id=1, source_target_pairs={{0,1},{1,2},{2,3},{3,0},{4,5},{5,6},{6,7},{7,4},{8,9},{9,10},{10,1... | collective-permute-start | bytes 3145736 | tf_op jit(solution)/shard_map/ppermute | solution.py:49
  279.4 188.2 %collective-permute-start.10 = (bf16[1024,512]{1,0:T(8,128)(2,1)}, bf16[1024,512]{1,0:T(8,128)(2,1)}, u32[]{:S(2)}, u32[]{:S(2)}) collective-permute-start(bf16[1024,512]{1,0:T(8,128)(2,1)} %get-tuple-element.7), channel_id=1, source_target_pairs={{0,2},{1,3},{2,0},{3,1},{4,6},{5,7},{6,4},{7,5},{8,10},{9,11},{10,... | collective-permute-start | bytes 3145736 | tf_op jit(solution)/shard_map/ppermute | solution.py:49
  279.4 188.2 %collective-permute-start.11 = (bf16[1024,512]{1,0:T(8,128)(2,1)}, bf16[1024,512]{1,0:T(8,128)(2,1)}, u32[]{:S(2)}, u32[]{:S(2)}) collective-permute-start(bf16[1024,512]{1,0:T(8,128)(2,1)} %get-tuple-element.6), channel_id=1, source_target_pairs={{0,3},{1,0},{2,1},{3,2},{4,7},{5,4},{6,5},{7,6},{8,11},{9,8},{10,9... | collective-permute-start | bytes 3145736 | tf_op jit(solution)/shard_map/ppermute | solution.py:49
  288.8 89.7 %copy-start.19 = (f32[1,512]{1,0:T(1,128)S(1)}, f32[1,512]{1,0:T(1,128)}, u32[]{:S(2)}) copy-start(f32[1,512]{1,0:T(1,128)} %get-tuple-element.124) | copy-start | bytes 6148
  288.8 89.7 %copy-start.20 = (f32[1,512]{1,0:T(1,128)S(1)}, f32[1,512]{1,0:T(1,128)}, u32[]{:S(2)}) copy-start(f32[1,512]{1,0:T(1,128)} %get-tuple-element.125) | copy-start | bytes 6148
  288.8 89.7 %copy-start.21 = (f32[1,512]{1,0:T(1,128)S(1)}, f32[1,512]{1,0:T(1,128)}, u32[]{:S(2)}) copy-start(f32[1,512]{1,0:T(1,128)} %get-tuple-element.126) | copy-start | bytes 6148
  288.8 89.7 %copy-start.22 = (f32[1,512]{1,0:T(1,128)S(1)}, f32[1,512]{1,0:T(1,128)}, u32[]{:S(2)}) copy-start(f32[1,512]{1,0:T(1,128)} %get-tuple-element.127) | copy-start | bytes 6148
  288.8 89.7 %copy-start.23 = (f32[1,512]{1,0:T(1,128)S(1)}, f32[1,512]{1,0:T(1,128)}, u32[]{:S(2)}) copy-start(f32[1,512]{1,0:T(1,128)} %get-tuple-element.128) | copy-start | bytes 6148
  288.8 89.7 %copy-start.24 = (f32[1,512]{1,0:T(1,128)S(1)}, f32[1,512]{1,0:T(1,128)}, u32[]{:S(2)}) copy-start(f32[1,512]{1,0:T(1,128)} %get-tuple-element.129) | copy-start | bytes 6148
  288.8 89.7 %copy-start.25 = (f32[1,512]{1,0:T(1,128)S(1)}, f32[1,512]{1,0:T(1,128)}, u32[]{:S(2)}) copy-start(f32[1,512]{1,0:T(1,128)} %get-tuple-element.130) | copy-start | bytes 6148
  288.8 89.7 %copy-start.26 = (f32[1,512]{1,0:T(1,128)S(1)}, f32[1,512]{1,0:T(1,128)}, u32[]{:S(2)}) copy-start(f32[1,512]{1,0:T(1,128)} %get-tuple-element.131) | copy-start | bytes 6148
  289.2 89.0 %collective-permute-start.5 = (bf16[127,512]{0,1:T(8,128)(2,1)S(1)}, bf16[127,512]{0,1:T(8,128)(2,1)S(1)}, u32[]{:S(2)}, u32[]{:S(2)}) collective-permute-start(bf16[127,512]{0,1:T(8,128)(2,1)S(1)} %slice_bitcast_fusion.1), channel_id=1, source_target_pairs={{0,4},{4,8},{8,12},{12,16},{16,20},{20,24},{24,28},{28,32},{32,36}... | collective-permute-start | bytes 390152 | tf_op jit(solution)/shard_map/ppermute | solution.py:16
  423.3 28.3 %collective-permute-start.6 = (bf16[384,512]{0,1:T(8,128)(2,1)S(1)}, bf16[384,512]{0,1:T(8,128)(2,1)S(1)}, u32[]{:S(2)}, u32[]{:S(2)}) collective-permute-start(bf16[384,512]{0,1:T(8,128)(2,1)S(1)} %fusion.47), channel_id=1, source_target_pairs={{0,1},{1,2},{2,3},{3,0},{4,5},{5,6},{6,7},{7,4},{8,9},{9,10},{10,1... | collective-permute-start | bytes 1179656 | tf_op jit(solution)/shard_map/ppermute | solution.py:36
  428.3 30.9 %collective-permute-start.7 = (bf16[384,512]{0,1:T(8,128)(2,1)S(1)}, bf16[384,512]{0,1:T(8,128)(2,1)S(1)}, u32[]{:S(2)}, u32[]{:S(2)}) collective-permute-start(bf16[384,512]{0,1:T(8,128)(2,1)S(1)} %fusion.47), channel_id=1, source_target_pairs={{0,2},{1,3},{2,0},{3,1},{4,6},{5,7},{6,4},{7,5},{8,10},{9,11},{10,... | collective-permute-start | bytes 1179656 | tf_op jit(solution)/shard_map/ppermute | solution.py:36
  451.6 11.9 %collective-permute-start.8 = (bf16[384,512]{0,1:T(8,128)(2,1)S(1)}, bf16[384,512]{0,1:T(8,128)(2,1)S(1)}, u32[]{:S(2)}, u32[]{:S(2)}) collective-permute-start(bf16[384,512]{0,1:T(8,128)(2,1)S(1)} %fusion.47), channel_id=1, source_target_pairs={{0,3},{1,0},{2,1},{3,2},{4,7},{5,4},{6,5},{7,6},{8,11},{9,8},{10,9... | collective-permute-start | bytes 1179656 | tf_op jit(solution)/shard_map/ppermute | solution.py:36
  481.0 11.7 %collective-permute-start.12 = (bf16[256,1024]{1,0:T(8,128)(2,1)S(1)}, bf16[256,1024]{1,0:T(8,128)(2,1)S(1)}, u32[]{:S(2)}, u32[]{:S(2)}) collective-permute-start(bf16[256,1024]{1,0:T(8,128)(2,1)S(1)} %constant_dynamic-slice_fusion), channel_id=1, source_target_pairs={{0,4},{4,0},{8,12},{12,8},{16,20},{20,16},{24,28},{28,24},{32,36},... | collective-permute-start | bytes 1572872 | tf_op jit(solution)/shard_map/ppermute | solution.py:22
  (52 other events, 2247.3 us)
Sparse Core Ops, SparseCore 0:
  9.2 35.6 all-gather.3
  46.7 50.2 all-gather.5
  98.8 156.9 all-gather.7

commit v8 on v7

--- a/solution.py
+++ b/solution.py
@@ -26,6 +26,17 @@
     width = source.shape[1:]
     padded = jnp.concatenate([source, jnp.zeros((count,) + width, source.dtype)], axis=0)
     return lax.dynamic_slice_in_dim(padded, jnp.clip(start, 0, source.shape[0]), count, 0)
+
+
+def ring_gather(block, axis):
+    peers = lax.axis_size(axis)
+    me = lax.axis_index(axis)
+    got = [block]
+    for by in range(1, peers):
+        got.append(lax.ppermute(block, axis, [(i, (i + by) % peers) for i in range(peers)]))
+    stacked = jnp.stack(got)
+    order = (me - jnp.arange(peers, dtype=jnp.int32)) % peers
+    return jnp.take(stacked, order, axis=0).reshape((peers * block.shape[0],) + block.shape[1:])
 
 
 def tp_blocks_gather(block, axis):
@@ -38,19 +49,6 @@
     order = (me - jnp.arange(peers, dtype=jnp.int32)) % peers
     ordered = jnp.take(stacked, order, axis=0)
     return jnp.moveaxis(ordered, 0, 1).reshape(block.shape[0], peers * block.shape[1])
-
-
-def tp_blocks_swap(blocks, axis):
-    peers = lax.axis_size(axis)
-    me = lax.axis_index(axis)
-    got = [lax.dynamic_index_in_dim(blocks, me, 0, keepdims=False)]
-    for by in range(1, peers):
-        sent = lax.dynamic_index_in_dim(blocks, (me + by) % peers, 0, keepdims=False)
-        got.append(lax.ppermute(sent, axis, [(i, (i + by) % peers) for i in range(peers)]))
-    stacked = jnp.stack(got)
-    order = (me - jnp.arange(peers, dtype=jnp.int32)) % peers
-    ordered = jnp.take(stacked, order, axis=0)
-    return jnp.moveaxis(ordered, 0, 1).reshape(blocks.shape[1], peers * blocks.shape[2])
 
 
 def tp_blocks_sum(full, axis):
@@ -129,22 +127,22 @@
     branches = in_weight.shape[1]
     chans = in_weight.shape[2]
     local_in = in_weight.reshape(in_weight.shape[0], branches * chans)
-    both = jnp.concatenate([local_in, out_weight.T], axis=1)
-    both_rows = both
+    flat = local_in
     for part in GATHER_ORDER:
-        both_rows = lax.all_gather(both_rows, part, axis=0, tiled=True)
+        flat = lax.all_gather(flat, part, axis=0, tiled=True)
     ny, nz, nx = (lax.axis_size(a) for a in CTX)
     block = in_weight.shape[0]
-    flat = both_rows[:, : branches * chans]
     normed = (
         normed.reshape(row_count, ny, nz, nx, block)
         .transpose(0, 1, 3, 2, 4)
         .reshape(row_count, ny * nz * nx * block)
     )
+    out_rows = out_weight.T
+    for part in ("y", "zl", "x"):
+        out_rows = ring_gather(out_rows, part)
     out_rows = (
-        both_rows[:, branches * chans :]
-        .reshape(ny, nx, nz, block, -1)
-        .transpose(0, 2, 1, 3, 4)
+        out_rows.reshape(nx, nz, ny, block, -1)
+        .transpose(2, 1, 0, 3, 4)
         .reshape(ny * nz * nx * block, -1)
     )
     summed = jnp.dot(normed, flat, preferred_element_type=jnp.float32)
@@ -167,15 +165,13 @@
         128,
     )
     gated = (feat[:, 0] * filtered).astype(jnp.bfloat16)
-    feats = x_own.shape[1]
-    my_cols = tp_blocks_swap(out_rows.reshape(-1, feats, chans), TP)
-    gated_all = tp_blocks_gather(gated, TP)
-    branch_out = lax.dot_general(
-        gated_all,
-        my_cols,
+    partial_out = lax.dot_general(
+        gated,
+        out_rows,
         (((1,), (1,)), ((), ())),
         preferred_element_type=jnp.float32,
     )
+    branch_out = tp_blocks_sum(partial_out.astype(jnp.bfloat16), TP)
     result = (x_own.astype(jnp.float32) + branch_out).astype(jnp.bfloat16)
 
     back = lax.dynamic_slice_in_dim(result, (1 - parity) * (share - window), window, 0)

time: 504 us -> 452 us (0.90)
  the two profiles are of different devices: /device:TPU:9 before, /device:TPU:32 now
where the time goes in v8:
time: 452 us; the launch traced here: 443 us
  waiting for transfers between devices  221 us (49%)
  other arithmetic  88.6 us (20%)
  starting transfers between devices  44 us (10%)
  local copies, waits for them, and re-layouts  40.8 us (9%)
  blocking collectives  19.4 us (4%)
  between operations  17 us (4%)
  matrix products  11.7 us (3%)
    ppermute x9, waiting for transfers between devices, ring_gather(): lax.ppermute(block, axis, [(i, (i + by) % peers) for i in range(peers)])  92.9 us
    ppermute x3, waiting for transfers between devices, tp_blocks_sum(): lax.ppermute(sent, axis, [(i, (i + by) % peers) for i in range(peers)])  59.9 us
    all_gather x2, waiting for transfers between devices, body(): flat = lax.all_gather(flat, part, axis=0, tiled=True)  44 us
    dot_general x1, other arithmetic, body(): lax.dot_general(gated, out_rows, (((1,), (1,)), ((), ())), preferred_elem...  32.8 us
    all_gather x1, blocking collectives, body(): flat = lax.all_gather(flat, part, axis=0, tiled=True)  19.4 us
    ppermute x3, starting transfers between devices, tp_blocks_sum(): lax.ppermute(sent, axis, [(i, (i + by) % peers) for i in range(peers)])  18.8 us
    add x2, other arithmetic, causal_taps(): summed = summed + jnp.where(in_genome, window * taps[j], jnp.float32(0.0))  17.4 us
    ppermute x9, starting transfers between devices, ring_gather(): lax.ppermute(block, axis, [(i, (i + by) % peers) for i in range(peers)])  14.9 us
  transfers between devices with their start and end apart: 21, of which 13 were waited for; matrix products, arithmetic and copies ran while one was open for 13% of the time, Pallas kernels for 0%

profile of v8, /device:TPU:32, one launch (start us, length us, event | category | flops | bytes accessed | tf_op | source)
XLA Modules:
  0.0 442.7 jit_solution(209941022246960287)
XLA Ops:
  7.5 19.4 %all_gather.9 = bf16[256,1536]{1,0:T(8,128)(2,1)} all-gather(bf16[64,1536]{1,0:T(8,128)(2,1)S(1)} %bitcast.231), channel_id=1, replica_groups=mesh['y'=4,'zl'=4,'x'=4,'zh'=2,'core'=2] {'zl'}, dimensions={0}, use_global_device_ids=true | all-gather | bytes 983040 | tf_op jit(solution)/shard_map/all_gather | solution.py:132
  27.0 44.0 %all-gather.3.cloned.1.call-done = bf16[1024,1536]{1,0:T(8,128)(2,1)} async-done(((bf16[256,1536]{1,0:T(8,128)(2,1)}), bf16[1024,1536]{1,0:T(8,128)(2,1)}) %all-gather.3.cloned.1.call-update) | async-done | bytes 3145744 | tf_op jit(solution)/shard_map/all_gather | solution.py:132
  93.5 4.6 %fusion.25 = bf16[384,1024]{1,0:T(8,128)(2,1)S(1)} fusion(s32[]{:T(128)S(6)} %min.13, bf16[384,1024]{1,0:T(8,128)(2,1)S(1)} %broadcast.1783, bf16[256,1024]{1,0:T(8,128)(2,1)S(1)} %collective-permute-done, s32[]{:T(128)S(6)} %min.12, bf16[640,1024]{1,0:T(8,128)(2,1)S(1)} %copy-done.3, pred[384]{0:T(512)(128)(4,1)} %get-tuple-element.276, ...), kind=kLoop, calls=%fused_computation.59 | loop fusion | flops 5898240 | bytes 4195849 | tf_op jit(solution)/shard_map/jit(_where)/select_n | solution.py:113
  98.2 4.1 collective-permute-start.2
  102.3 65.0 %collective-permute-done.9 = bf16[256,512]{1,0:T(8,128)(2,1)S(1)} collective-permute-done((bf16[256,512]{1,0:T(8,128)(2,1)S(1)}, bf16[256,512]{1,0:T(8,128)(2,1)S(1)}, u32[]{:S(2)}, u32[]{:S(2)}) %collective-permute-start.9) | collective-permute-done | bytes 262176 | tf_op jit(solution)/shard_map/ppermute | solution.py:36
  189.2 6.5 %copy.33 = f32[384,4,1024]{0,2,1:T(8,128)} copy(f32[384,4,1024]{2,0,1:T(8,128)} %convert_bitcast_fusion) | data formatting | bytes 12582912 | tf_op jit(solution)/shard_map/convert_element_type | solution.py:122
  197.3 3.6 fusion.1
  202.1 21.6 %collective-permute-done.13 = bf16[1024,512]{1,0:T(8,128)(2,1)} collective-permute-done((bf16[1024,512]{1,0:T(8,128)(2,1)}, bf16[1024,512]{1,0:T(8,128)(2,1)}, u32[]{:S(2)}, u32[]{:S(2)}) %collective-permute-start.13) | collective-permute-done | bytes 1048608 | tf_op jit(solution)/shard_map/ppermute | solution.py:36
  224.3 3.6 pad_maximum_fusion
  227.9 5.1 %gather_fusion.3 = bf16[4,1024,512]{2,1,0:T(8,128)(2,1)} fusion(bf16[4,1024,512]{2,1,0:T(8,128)(2,1)} %pad_maximum_fusion, s32[1024]{0:T(1024)} %pad_clamp_fusion), kind=kCustom, calls=%fused_computation.3 | custom fusion | bytes 8388624 | tf_op jit(solution)/shard_map/jit(_take)/gather | solution.py:39
  233.1 8.2 %convolution_convert_fusion.1 = bf16[384,1536]{1,0:T(8,128)(2,1)S(1)} fusion(bf16[384,4096]{0,1:T(8,128)(2,1)S(1)} %bitcast.228, bf16[4096,1536]{1,0:T(8,128)(2,1)} %all-gather.5.cloned.1.call-done), kind=kOutput, calls=%fused_computation.14 | convolution fusion | flops 4832428032 | bytes 16908288 | tf_op jit(solution)/shard_map/dot_general | solution.py:148
  251.5 5.0 %collective-permute-done.4 = bf16[6,3,512]{0,2,1:T(8,128)(2,1)S(1)} collective-permute-done((bf16[6,3,512]{0,2,1:T(8,128)(2,1)S(1)}, bf16[6,3,512]{0,2,1:T(8,128)(2,1)S(1)}, u32[]{:S(2)}, u32[]{:S(2)}) %collective-permute-start.4) | collective-permute-done | bytes 18464 | tf_op jit(solution)/shard_map/ppermute | solution.py:16
  257.4 5.7 %fusion.3 = f32[384,3,512]{0,2,1:T(8,128)S(1)} fusion(f32[390,3,512]{0,2,1:T(8,128)S(1)} %maximum_convert_fusion, f32[3,512]{1,0:T(4,128)S(1)} %get-tuple-element.278, f32[3,512]{1,0:T(4,128)S(1)} %get-tuple-element.279, f32[3,512]{1,0:T(4,128)S(1)} %get-tuple-element.280, f32[3,512]{1,0:T(4,128)S(1)} %get-tuple-element.281, ...), kind=kLoop, calls=%fused_computation.22 | loop fusion | flops 11796480 | bytes 18920064 | tf_op jit(solution)/shard_map/add | solution.py:79
  265.9 6.7 %collective-permute-done.5 = bf16[127,512]{0,1:T(8,128)(2,1)S(1)} collective-permute-done((bf16[127,512]{0,1:T(8,128)(2,1)S(1)}, bf16[127,512]{0,1:T(8,128)(2,1)S(1)}, u32[]{:S(2)}, u32[]{:S(2)}) %collective-permute-start.5) | collective-permute-done | bytes 130080 | tf_op jit(solution)/shard_map/ppermute | solution.py:16
  273.3 11.7 %fusion.225 = f32[384,512]{0,1:T(8,128)S(1)} fusion(f32[511,512]{0,1:T(8,128)S(1)} %maximum_convert_fusion.1, f32[512]{0:T(512)} %bitcast.372, f32[512]{0:T(512)S(1)} %bitcast.354, f32[512]{0:T(512)S(1)} %bitcast.355, f32[512]{0:T(512)S(1)} %bitcast.356, f32[512]{0:T(512)S(1)} %bitcast.357, f32[512]{0:T(512)S(1)} %bitcast.358, f32[512]{0:T(512)S(1)} %bitcast.359, ...), kind=kLoop, calls=%fused_computation.356 | loop fusion | flops 18677760 | bytes 26030080 | tf_op jit(solution)/shard_map/add | solution.py:79
  285.1 32.8 %fusion.319 = bf16[384,512]{0,1:T(8,128)(2,1)S(1)} fusion(f32[511,512]{0,1:T(8,128)S(1)} %maximum_convert_fusion.1, f32[384,512]{0,1:T(8,128)S(1)} %fusion.225, f32[512]{0:T(512)S(1)} %bitcast.245, f32[512]{0:T(512)S(1)} %bitcast.246, f32[512]{0:T(512)S(1)} %bitcast.304, f32[512]{0:T(512)S(1)} %bitcast.305, f32[512]{0:T(512)S(1)} %bitcast.306, ...), kind=kLoop, calls=%fused_computation.68.clone.clone.1 | loop fusion | flops 57016320 | bytes 77697024 | tf_op jit(solution)/shard_map/dot_general | solution.py:168
  321.5 4.8 %reshape.1294 = bf16[384,4,1024]{2,1,0:T(4,128)(2,1)S(1)} reshape(bf16[384,4096]{1,0:T(8,128)(2,1)} %convolution_convert_fusion) | data formatting | bytes 6291456 | tf_op jit(solution)/shard_map/reshape | solution.py:58
  326.3 7.3 %constant_dynamic-slice_fusion.4 = (bf16[384,1,1024]{2,1,0:T(2,128)(2,1)}, bf16[384,1,1024]{2,1,0:T(2,128)(2,1)S(1)}, bf16[384,1,1024]{2,1,0:T(2,128)(2,1)S(1)}, bf16[384,1,1024]{2,1,0:T(2,128)(2,1)S(1)}) fusion(bf16[384,4,1024]{2,1,0:T(4,128)(2,1)S(1)} %reshape.1294, s32[]{:T(128)S(6)} %select_n.816, s32[]{:T(128)S(6)} %select_n.820, s32[]{:T(128)S(6)} %select_n.818, ...), kind=kLoop, calls=%fused_computation.479 | loop fusion | bytes 6291472 | tf_op jit(solution)/shard_map/jit(dynamic_index_in_dim)/dynamic_slice | solution.py:59
  335.5 13.1 %collective-permute-start.16 = (bf16[384,1024]{1,0:T(8,128)(2,1)}, bf16[384,1024]{1,0:T(8,128)(2,1)}, u32[]{:S(2)}, u32[]{:S(2)}) collective-permute-start(bf16[384,1024]{1,0:T(8,128)(2,1)} %bitcast.217), channel_id=1, source_target_pairs={{0,2},{1,3},{2,0},{3,1},{4,6},{5,7},{6,4},{7,5},{8,10},{9,11},{10,... | collective-permute-start | bytes 2359304 | tf_op jit(solution)/shard_map/ppermute | solution.py:62
  349.7 5.3 %collective-permute-start.17 = (bf16[384,1024]{1,0:T(8,128)(2,1)}, bf16[384,1024]{1,0:T(8,128)(2,1)}, u32[]{:S(2)}, u32[]{:S(2)}) collective-permute-start(bf16[384,1024]{1,0:T(8,128)(2,1)} %bitcast.216), channel_id=1, source_target_pairs={{0,3},{1,0},{2,1},{3,2},{4,7},{5,4},{6,5},{7,6},{8,11},{9,8},{10,9... | collective-permute-start | bytes 2359304 | tf_op jit(solution)/shard_map/ppermute | solution.py:62
  355.1 39.8 %collective-permute-done.15 = bf16[384,1024]{1,0:T(8,128)(2,1)} collective-permute-done((bf16[384,1024]{1,0:T(8,128)(2,1)S(1)}, bf16[384,1024]{1,0:T(8,128)(2,1)}, u32[]{:S(2)}, u32[]{:S(2)}) %collective-permute-start.15) | collective-permute-done | bytes 786464 | tf_op jit(solution)/shard_map/ppermute | solution.py:62
  397.0 18.0 %collective-permute-done.17 = bf16[384,1024]{1,0:T(8,128)(2,1)} collective-permute-done((bf16[384,1024]{1,0:T(8,128)(2,1)}, bf16[384,1024]{1,0:T(8,128)(2,1)}, u32[]{:S(2)}, u32[]{:S(2)}) %collective-permute-start.17) | collective-permute-done | bytes 786464 | tf_op jit(solution)/shard_map/ppermute | solution.py:62
  419.0 12.6 %collective-permute-done.18 = bf16[256,1024]{1,0:T(8,128)(2,1)S(1)} collective-permute-done((bf16[256,1024]{1,0:T(8,128)(2,1)S(1)}, bf16[256,1024]{1,0:T(8,128)(2,1)S(1)}, u32[]{:S(2)}, u32[]{:S(2)}) %collective-permute-start.18) | collective-permute-done | bytes 524320 | tf_op jit(solution)/shard_map/ppermute | solution.py:22
  431.7 3.8 fusion.22
  (229 shorter events, 73.1 us)
Async XLA Ops:
  6.5 64.5 %all-gather.3.cloned.1.call-start = ((), (), s32[]{:S(2)}) async-start(), calls=%async_computation | async-start | bytes 3932160 | tf_op jit(solution)/shard_map/all_gather | solution.py:132
  27.0 206.1 %all-gather.5.cloned.1.call-start = ((), (), s32[]{:S(2)}) async-start(), calls=%async_computation.1 | async-start | bytes 15728640 | tf_op jit(solution)/shard_map/all_gather | solution.py:132
  71.1 16.8 %collective-permute-start.6 = (bf16[64,512]{1,0:T(8,128)(2,1)S(1)}, bf16[64,512]{1,0:T(8,128)(2,1)S(1)}, u32[]{:S(2)}, u32[]{:S(2)}) collective-permute-start(bf16[64,512]{1,0:T(8,128)(2,1)S(1)} %bitcast.237), channel_id=1, source_target_pairs={{0,64},{64,128},{128,192},{192,0},{1,65},{65,129},{129,193},{193,1... | collective-permute-start | bytes 196616 | tf_op jit(solution)/shard_map/ppermute | solution.py:36
  72.7 15.2 %collective-permute-start.7 = (bf16[64,512]{1,0:T(8,128)(2,1)S(1)}, bf16[64,512]{1,0:T(8,128)(2,1)S(1)}, u32[]{:S(2)}, u32[]{:S(2)}) collective-permute-start(bf16[64,512]{1,0:T(8,128)(2,1)S(1)} %bitcast.238), channel_id=1, source_target_pairs={{0,128},{64,192},{128,0},{192,64},{1,129},{65,193},{129,1},{193,65... | collective-permute-start | bytes 196616 | tf_op jit(solution)/shard_map/ppermute | solution.py:36
  75.4 12.5 %collective-permute-start.8 = (bf16[64,512]{1,0:T(8,128)(2,1)S(1)}, bf16[64,512]{1,0:T(8,128)(2,1)S(1)}, u32[]{:S(2)}, u32[]{:S(2)}) collective-permute-start(bf16[64,512]{1,0:T(8,128)(2,1)S(1)} %bitcast.239), channel_id=1, source_target_pairs={{0,192},{64,0},{128,64},{192,128},{1,193},{65,1},{129,65},{193,129... | collective-permute-start | bytes 196616 | tf_op jit(solution)/shard_map/ppermute | solution.py:36
  76.9 16.5 %collective-permute-start = (bf16[256,1024]{1,0:T(8,128)(2,1)S(1)}, bf16[256,1024]{1,0:T(8,128)(2,1)S(1)}, u32[]{:S(2)}, u32[]{:S(2)}) collective-permute-start(bf16[256,1024]{1,0:T(8,128)(2,1)S(1)} %constant_dynamic-slice_fusion.5), channel_id=1, source_target_pairs={{0,4},{4,0},{8,12},{12,8},{16,20},{20,16},{24,28},{28,24},{32,36},... | collective-permute-start | bytes 1572872 | tf_op jit(solution)/shard_map/ppermute | solution.py:22
  88.8 78.6 %collective-permute-start.9 = (bf16[256,512]{1,0:T(8,128)(2,1)S(1)}, bf16[256,512]{1,0:T(8,128)(2,1)S(1)}, u32[]{:S(2)}, u32[]{:S(2)}) collective-permute-start(bf16[256,512]{1,0:T(8,128)(2,1)S(1)} %bitcast_select_fusion.2), channel_id=1, source_target_pairs={{0,16},{16,32},{32,48},{48,0},{1,17},{17,33},{33,49},{49,1},{2,18}... | collective-permute-start | bytes 786440 | tf_op jit(solution)/shard_map/ppermute | solution.py:36
  90.4 80.1 %collective-permute-start.10 = (bf16[256,512]{1,0:T(8,128)(2,1)S(1)}, bf16[256,512]{1,0:T(8,128)(2,1)S(1)}, u32[]{:S(2)}, u32[]{:S(2)}) collective-permute-start(bf16[256,512]{1,0:T(8,128)(2,1)S(1)} %bitcast_select_fusion.2), channel_id=1, source_target_pairs={{0,32},{16,48},{32,0},{48,16},{1,33},{17,49},{33,1},{49,17},{2,34}... | collective-permute-start | bytes 786440 | tf_op jit(solution)/shard_map/ppermute | solution.py:36
  91.7 80.6 %collective-permute-start.11 = (bf16[256,512]{1,0:T(8,128)(2,1)S(1)}, bf16[256,512]{1,0:T(8,128)(2,1)S(1)}, u32[]{:S(2)}, u32[]{:S(2)}) collective-permute-start(bf16[256,512]{1,0:T(8,128)(2,1)S(1)} %bitcast_select_fusion.2), channel_id=1, source_target_pairs={{0,48},{16,0},{32,16},{48,32},{1,49},{17,1},{33,17},{49,33},{2,50}... | collective-permute-start | bytes 786440 | tf_op jit(solution)/shard_map/ppermute | solution.py:36
  98.1 82.0 %copy-start = (bf16[384,1024]{1,0:T(8,128)(2,1)}, bf16[384,1024]{1,0:T(8,128)(2,1)S(1)}, u32[]{:S(2)}) copy-start(bf16[384,1024]{1,0:T(8,128)(2,1)S(1)} %fusion.25) | copy-start | bytes 2359300
  98.1 80.9 %collective-permute-start.1 = (bf16[384,1024]{1,0:T(8,128)(2,1)S(1)}, bf16[384,1024]{1,0:T(8,128)(2,1)}, u32[]{:S(2)}, u32[]{:S(2)}) collective-permute-start(bf16[384,1024]{1,0:T(8,128)(2,1)S(1)} %fusion.25), channel_id=1, source_target_pairs={{0,1},{1,2},{2,3},{3,0},{4,5},{5,6},{6,7},{7,4},{8,9},{9,10},{10,1... | collective-permute-start | bytes 2359304 | tf_op jit(solution)/shard_map/ppermute | solution.py:47
  98.2 81.9 %collective-permute-start.2 = (bf16[384,1024]{1,0:T(8,128)(2,1)S(1)}, bf16[384,1024]{1,0:T(8,128)(2,1)}, u32[]{:S(2)}, u32[]{:S(2)}) collective-permute-start(bf16[384,1024]{1,0:T(8,128)(2,1)S(1)} %fusion.25), channel_id=1, source_target_pairs={{0,2},{1,3},{2,0},{3,1},{4,6},{5,7},{6,4},{7,5},{8,10},{9,11},{10,... | collective-permute-start | bytes 2359304 | tf_op jit(solution)/shard_map/ppermute | solution.py:47
  167.3 12.8 %collective-permute-start.3 = (bf16[384,1024]{1,0:T(8,128)(2,1)S(1)}, bf16[384,1024]{1,0:T(8,128)(2,1)}, u32[]{:S(2)}, u32[]{:S(2)}) collective-permute-start(bf16[384,1024]{1,0:T(8,128)(2,1)S(1)} %fusion.25), channel_id=1, source_target_pairs={{0,3},{1,0},{2,1},{3,2},{4,7},{5,4},{6,5},{7,6},{8,11},{9,8},{10,9... | collective-permute-start | bytes 2359304 | tf_op jit(solution)/shard_map/ppermute | solution.py:47
  174.4 27.7 %collective-permute-start.12 = (bf16[1024,512]{1,0:T(8,128)(2,1)}, bf16[1024,512]{1,0:T(8,128)(2,1)}, u32[]{:S(2)}, u32[]{:S(2)}) collective-permute-start(bf16[1024,512]{1,0:T(8,128)(2,1)} %bitcast_select_fusion), channel_id=1, source_target_pairs={{0,4},{4,8},{8,12},{12,0},{1,5},{5,9},{9,13},{13,1},{2,6},{6,10},{... | collective-permute-start | bytes 3145736 | tf_op jit(solution)/shard_map/ppermute | solution.py:36
  175.9 47.9 %collective-permute-start.13 = (bf16[1024,512]{1,0:T(8,128)(2,1)}, bf16[1024,512]{1,0:T(8,128)(2,1)}, u32[]{:S(2)}, u32[]{:S(2)}) collective-permute-start(bf16[1024,512]{1,0:T(8,128)(2,1)} %bitcast_select_fusion), channel_id=1, source_target_pairs={{0,8},{4,12},{8,0},{12,4},{1,9},{5,13},{9,1},{13,5},{2,10},{6,14},... | collective-permute-start | bytes 3145736 | tf_op jit(solution)/shard_map/ppermute | solution.py:36
  179.0 45.4 %collective-permute-start.14 = (bf16[1024,512]{1,0:T(8,128)(2,1)}, bf16[1024,512]{1,0:T(8,128)(2,1)}, u32[]{:S(2)}, u32[]{:S(2)}) collective-permute-start(bf16[1024,512]{1,0:T(8,128)(2,1)} %bitcast_select_fusion), channel_id=1, source_target_pairs={{0,12},{4,0},{8,4},{12,8},{1,13},{5,1},{9,5},{13,9},{2,14},{6,2},{... | collective-permute-start | bytes 3145736 | tf_op jit(solution)/shard_map/ppermute | solution.py:36
  242.6 14.0 %collective-permute-start.4 = (bf16[6,3,512]{0,2,1:T(8,128)(2,1)S(1)}, bf16[6,3,512]{0,2,1:T(8,128)(2,1)S(1)}, u32[]{:S(2)}, u32[]{:S(2)}) collective-permute-start(bf16[6,3,512]{0,2,1:T(8,128)(2,1)S(1)} %bitcast.232), channel_id=1, source_target_pairs={{0,4},{4,8},{8,12},{12,16},{16,20},{20,24},{24,28},{28,32},{32,36}... | collective-permute-start | bytes 55304 | tf_op jit(solution)/shard_map/ppermute | solution.py:16
  263.7 9.0 %collective-permute-start.5 = (bf16[127,512]{0,1:T(8,128)(2,1)S(1)}, bf16[127,512]{0,1:T(8,128)(2,1)S(1)}, u32[]{:S(2)}, u32[]{:S(2)}) collective-permute-start(bf16[127,512]{0,1:T(8,128)(2,1)S(1)} %slice_bitcast_fusion.1), channel_id=1, source_target_pairs={{0,4},{4,8},{8,12},{12,16},{16,20},{20,24},{24,28},{28,32},{32,36}... | collective-permute-start | bytes 390152 | tf_op jit(solution)/shard_map/ppermute | solution.py:16
  333.9 61.0 %collective-permute-start.15 = (bf16[384,1024]{1,0:T(8,128)(2,1)S(1)}, bf16[384,1024]{1,0:T(8,128)(2,1)}, u32[]{:S(2)}, u32[]{:S(2)}) collective-permute-start(bf16[384,1024]{1,0:T(8,128)(2,1)S(1)} %bitcast.230), channel_id=1, source_target_pairs={{0,1},{1,2},{2,3},{3,0},{4,5},{5,6},{6,7},{7,4},{8,9},{9,10},{10,1... | collective-permute-start | bytes 2359304 | tf_op jit(solution)/shard_map/ppermute | solution.py:62
  334.2 80.8 %copy-start.1 = (bf16[384,1024]{1,0:T(8,128)(2,1)S(1)}, bf16[384,1024]{1,0:T(8,128)(2,1)}, u32[]{:S(2)}) copy-start(bf16[384,1024]{1,0:T(8,128)(2,1)} %copy-done) | copy-start | bytes 2359300
  334.3 80.7 %copy-start.2 = (bf16[384,1,1024]{2,1,0:T(2,128)(2,1)S(1)}, bf16[384,1,1024]{2,1,0:T(2,128)(2,1)}, u32[]{:S(2)}) copy-start(bf16[384,1,1024]{2,1,0:T(2,128)(2,1)} %get-tuple-element.5) | copy-start | bytes 2359300
  335.5 61.5 %collective-permute-start.16 = (bf16[384,1024]{1,0:T(8,128)(2,1)}, bf16[384,1024]{1,0:T(8,128)(2,1)}, u32[]{:S(2)}, u32[]{:S(2)}) collective-permute-start(bf16[384,1024]{1,0:T(8,128)(2,1)} %bitcast.217), channel_id=1, source_target_pairs={{0,2},{1,3},{2,0},{3,1},{4,6},{5,7},{6,4},{7,5},{8,10},{9,11},{10,... | collective-permute-start | bytes 2359304 | tf_op jit(solution)/shard_map/ppermute | solution.py:62
  349.7 65.3 %collective-permute-start.17 = (bf16[384,1024]{1,0:T(8,128)(2,1)}, bf16[384,1024]{1,0:T(8,128)(2,1)}, u32[]{:S(2)}, u32[]{:S(2)}) collective-permute-start(bf16[384,1024]{1,0:T(8,128)(2,1)} %bitcast.216), channel_id=1, source_target_pairs={{0,3},{1,0},{2,1},{3,2},{4,7},{5,4},{6,5},{7,6},{8,11},{9,8},{10,9... | collective-permute-start | bytes 2359304 | tf_op jit(solution)/shard_map/ppermute | solution.py:62
  417.6 13.9 %collective-permute-start.18 = (bf16[256,1024]{1,0:T(8,128)(2,1)S(1)}, bf16[256,1024]{1,0:T(8,128)(2,1)S(1)}, u32[]{:S(2)}, u32[]{:S(2)}) collective-permute-start(bf16[256,1024]{1,0:T(8,128)(2,1)S(1)} %constant_dynamic-slice_fusion), channel_id=1, source_target_pairs={{0,4},{4,0},{8,12},{12,8},{16,20},{20,16},{24,28},{28,24},{32,36},... | collective-permute-start | bytes 1572872 | tf_op jit(solution)/shard_map/ppermute | solution.py:22
  (61 other events, 920.1 us)
Sparse Core Ops, SparseCore 0:
  27.1 43.9 all-gather.2
  72.9 121.3 all-gather.4
